TPU v7x, 256 devices: a whole 4x4x8 slice. The times are simulated.
256 devices in a mesh: tok: 32 (over x, z), head: 8 (over y, core).
Axes of the slice: x: 4, y: 4, z: 8, core: 2. Of those that a mesh axis runs over, the one named last changes fastest.
Arguments:
- tokens: bfloat16 [32768, 1664], P(('tok', 'head')), may hold values from -75 to 75
- attn_gain: float32 [1664], replicated, may hold values from 0.1 to 1.9
- qkv_weight: bfloat16 [3, 1664, 1664], P(None, 'head'), may hold values from -5 to 5
- out_weight: bfloat16 [1664, 1664], P('head'), may hold values from -0.4375 to 0.4375
- merge_gain: float32 [1664], replicated, may hold values from 0.1 to 1.9
- merge_weight: bfloat16 [6656, 4096], P('head', 'tok'), may hold values from -0.078125 to 0.078125
- grid_sizes: int32 [2, 128], P(None, 'tok'), may hold values from 2 to 16, as said below
- segment_ids: int32 [32768], P('tok'), may hold values from 0 to 127, as said below
- patch_pos: int32 [2, 32768], P(None, 'tok'), may hold values from 0 to 15, as said below
- live_mask: int32 [32768], P('tok'), may hold values from 0 to 1, as said below
- owners: int32 [8192, 1], P(('tok', 'head')), may hold values from 0 to 31; in each aligned block of 32 rows (0 to 31, 32 to 63, ...) at most 2 rows name the same one
Outputs:
- delivered: bfloat16 [16384, 4096], P(('tok', 'head'))
Inputs may be any that keep to these rules, and one draw needn't show every extreme that they name: `grid_sizes`: both sides of every image are even, and some image is 16 by 16. `segment_ids`: never fall along the tokens. The aligned block b of 1024 tokens holds images b * 4 to (b + 1) * 4 - 1 packed in order from the block's start, image s taking grid_sizes[0, s] * grid_sizes[1, s] tokens; the block's remaining tokens carry the number of its last image. `patch_pos`: an image's tokens come in 2x2 windows, windows in row-major order, each window as (2 * r, 2 * c), (2 * r, 2 * c + 1), (2 * r + 1, 2 * c), (2 * r + 1, 2 * c + 1); padding tokens sit at (0, 0). `live_mask`: 1 exactly on the tokens that belong to an image. `owners`: in each aligned block of 32 rows (the merged rows of one device) no owner is named more than 2 times.
All inputs are finite; a program needn't handle non-finite values.
Results may differ from a plain program's by a relative error of at most 0.024.
Values may be sent and summed in bfloat16 or wider, within the bound.
No kernel may reach another device: no remote copies, remote signals or barrier semaphores. Data moves between devices by JAX's collectives and lax.ppermute only.
A program may use at most 64 MiB of HBM per device.

v0:
```python
import jax
import jax.numpy as jnp
from jax import lax
from jax.sharding import PartitionSpec as P

D = 1664
HD = 104
SIDE = 16


EPSILON = 1e-06
NEGATIVE = -1e30


def layer_norm(values, gain_vec):
    average = jnp.mean(values, axis=-1, keepdims=True)
    centred = values - average
    variance = jnp.mean(centred * centred, axis=-1, keepdims=True)
    return centred * lax.rsqrt(variance + EPSILON) * gain_vec


def rotate(vectors, row_coord, col_coord):
    quarter = vectors.shape[-1] // 4
    frequency = 10000.0 ** (-jnp.arange(quarter, dtype=jnp.float32) / quarter)
    pieces = []
    for which_axis, coordinate in ((0, row_coord), (1, col_coord)):
        leading = vectors[..., 2 * which_axis * quarter : (2 * which_axis + 1) * quarter]
        trailing = vectors[..., (2 * which_axis + 1) * quarter : (2 * which_axis + 2) * quarter]
        angles = coordinate[:, None, None] * frequency
        cosine = jnp.cos(angles)
        sine_val = jnp.sin(angles)
        pieces.append(leading * cosine - trailing * sine_val)
        pieces.append(leading * sine_val + trailing * cosine)
    return jnp.concatenate(pieces, axis=-1)


def body(
    tokens,
    attn_gain,
    qkv_weight,
    out_weight,
    merge_gain,
    merge_weight,
    grid_sizes,
    segment_ids,
    patch_pos,
    live_mask,
    owners,
):
    group_len = segment_ids.shape[0]
    local_rows = tokens.shape[0]
    head_width = qkv_weight.shape[1]
    heads_here = head_width // HD
    tok_count = lax.axis_size("tok")
    image_count = grid_sizes.shape[1]
    local_image = segment_ids - lax.axis_index("tok") * image_count
    image_match = local_image[:, None] == jnp.arange(image_count, dtype=jnp.int32)[None, :]
    grid_float = grid_sizes.astype(jnp.float32)
    row_size = jnp.sum(jnp.where(image_match, grid_float[0][None, :], 0.0), axis=1)
    col_size = jnp.sum(jnp.where(image_match, grid_float[1][None, :], 0.0), axis=1)
    row_coord = patch_pos[0].astype(jnp.float32) * SIDE / row_size
    col_coord = patch_pos[1].astype(jnp.float32) * SIDE / col_size
    stacked_weight = qkv_weight.reshape(3 * head_width, D)
    normed = layer_norm(tokens.astype(jnp.float32), attn_gain).astype(jnp.bfloat16)
    projected_rows = lax.dot_general(
        lax.all_gather(normed, "head", axis=0, tiled=True),
        stacked_weight,
        (((1,), (1,)), ((), ())),
        preferred_element_type=jnp.float32,
    )
    projected_rows = projected_rows.reshape(group_len, 3, heads_here, HD)
    query_all = (rotate(projected_rows[:, 0], row_coord, col_coord) * HD ** (-0.5)).astype(
        jnp.bfloat16
    )
    key_all = rotate(projected_rows[:, 1], row_coord, col_coord).astype(jnp.bfloat16)
    value_all = projected_rows[:, 2].astype(jnp.bfloat16)
    block_len = min(512, group_len)
    block_count = group_len // block_len
    key_live = live_mask == 1

    def allowed_pairs(query_start, span):
        query_seg = lax.dynamic_slice_in_dim(segment_ids, query_start, block_len)
        query_place = query_start + jnp.arange(block_len, dtype=jnp.int32)
        key_place = jnp.arange(span, dtype=jnp.int32)
        same_image = query_seg[:, None] == segment_ids[None, :]
        return same_image & (key_live[None, :] | (query_place[:, None] == key_place[None, :]))

    def query_block(query_start):
        queries = lax.dynamic_slice_in_dim(query_all, query_start, block_len, 0)
        allowed = allowed_pairs(query_start, group_len)
        scores = jnp.einsum("qhd,khd->hqk", queries, key_all, preferred_element_type=jnp.float32)
        masked = jnp.where(allowed[None], scores, NEGATIVE)
        row_top = jnp.max(masked, axis=2, keepdims=True)
        exponent = jnp.where(allowed[None], jnp.exp(masked - row_top), 0.0)
        denominator = jnp.sum(exponent, axis=2)
        numerator = jnp.einsum(
            "hqk,khd->qhd",
            exponent.astype(jnp.bfloat16),
            value_all,
            preferred_element_type=jnp.float32,
        )
        return (numerator / denominator.T[:, :, None]).astype(jnp.bfloat16)

    block_starts = jnp.arange(block_count, dtype=jnp.int32) * block_len
    heads_out = lax.map(query_block, block_starts).reshape(group_len, head_width)
    attn_rows = lax.psum_scatter(
        jnp.dot(heads_out, out_weight, preferred_element_type=jnp.float32).astype(jnp.bfloat16),
        "head",
        scatter_dimension=0,
        tiled=True,
    ).astype(jnp.float32)
    stream = (tokens.astype(jnp.float32) + attn_rows).reshape(local_rows // 4, 4, D)
    average = jnp.sum(stream, axis=2, keepdims=True) / D
    variance = jnp.sum(stream * stream, axis=2, keepdims=True) / D - average * average
    window_rows = ((stream - average) * lax.rsqrt(variance + EPSILON) * merge_gain).astype(
        jnp.bfloat16
    )
    merged_slice = lax.all_to_all(
        window_rows.reshape(local_rows // 4, 4 * D), "head", split_axis=1, concat_axis=0, tiled=True
    )
    merged_count = local_rows // 4
    column_terms = jnp.dot(
        merged_slice,
        lax.all_gather(merge_weight, "tok", axis=1, tiled=True),
        preferred_element_type=jnp.float32,
    )
    projected = lax.psum_scatter(
        column_terms.astype(jnp.bfloat16), "head", scatter_dimension=0, tiled=True
    )
    slot_count = max(2, 2 * merged_count // tok_count)
    owner_col = owners[:, 0]
    owner_hot = (owner_col[:, None] == jnp.arange(tok_count, dtype=jnp.int32)[None, :]).astype(
        jnp.int32
    )
    earlier = jnp.cumsum(owner_hot, axis=0, dtype=jnp.int32) - owner_hot
    slot_index = jnp.sum(earlier * owner_hot, axis=1, dtype=jnp.int32)
    target = owner_col * slot_count + slot_index
    select = (
        jnp.arange(tok_count * slot_count, dtype=jnp.int32)[:, None] == target[None, :]
    ).astype(jnp.bfloat16)
    send_rows = jnp.dot(select, projected, preferred_element_type=jnp.float32).astype(jnp.bfloat16)
    send_rows = send_rows.reshape(tok_count, slot_count, -1)
    received = lax.all_to_all(send_rows, "tok", split_axis=0, concat_axis=0, tiled=True)
    return received.reshape(tok_count * slot_count, -1)


def solution(mesh):
    placed = (
        P(("tok", "head"), None),
        P(),
        P(None, "head", None),
        P("head", None),
        P(),
        P("head", "tok"),
        P(None, "tok"),
        P("tok"),
        P(None, "tok"),
        P("tok"),
        P(("tok", "head"), None),
    )
    return jax.shard_map(
        body, mesh=mesh, in_specs=placed, out_specs=P(("tok", "head"), None), check_vma=False
    )
```

profile of v0, /device:TPU:57, one launch (start us, length us, event | category | flops | bytes accessed | tf_op | source)
XLA Modules:
  0.0 257.5 jit_solution(5983882378429077472)
XLA Ops:
  7.4 1.3 convert_reduce_fusion
  8.7 1.3 fusion.46
  10.0 2.1 fusion.48
  15.1 1.0 multiply_cosine_fusion.1
  16.1 28.8 %all-gather.3.cloned.1.call-done = bf16[1024,1664]{1,0:T(8,128)(2,1)} async-done(((bf16[128,1664]{1,0:T(8,128)(2,1)}), bf16[1024,1664]{1,0:T(8,128)(2,1)}) %all-gather.3.cloned.1.call-update) | async-done | bytes 3407888 | tf_op jit(solution)/shard_map/all_gather | solution.py:66
  44.9 4.5 %fusion.39 = f32[1024,3,2,104]{0,3,2,1:T(8,128)S(1)} fusion(bf16[3,2,104,1664]{3,2,1,0:T(8,128)(2,1)S(1)} %bitcast.70, bf16[1024,1664]{1,0:T(8,128)(2,1)} %all-gather.3.cloned.1.call-done), kind=kOutput, calls=%fused_computation.27 | convolution fusion | flops 2126512128 | bytes 8040448 | tf_op jit(solution)/shard_map/dot_general | solution.py:65
  51.7 0.9 fusion.49
  52.6 23.1 %while.10 = (s32[]{:T(128)}, bf16[2,512,2,104]{1,3,2,0:T(8,128)(2,1)}, s32[2]{0:T(128)S(1)}, s32[1024]{0:T(1024)S(1)}, pred[1024]{0:T(1024)(128)(4,1)S(1)}, /*in...) while((s32[]{:T(128)}, ...), condition=%wide.region_9.10_spmd, body=%wide.region_6.0_spmd.sunk | while | flops 443762176 | bytes 7069351 | solution.py:105
  56.4 4.6 %fusion.81 = (f32[2,512]{1,0:T(2,128)S(1)}, bf16[2,512,1024]{2,1,0:T(8,128)(2,1)}) fusion(pred[512,1024]{1,0:T(8,128)(4,1)S(1)} %fusion.80, bf16[1024,2,104]{0,2,1:T(8,128)(2,1)} %get-tuple-element.180, bf16[1024,2,104]{0,2,1:T(8,128)(2,1)} %get-tuple-element.179, s32[]{:T(128)S(6)} %select_n.34), kind=kOutput, calls=%fused_computation.84.clone.1 | convolution fusion | flops 223347712 | bytes 3788804 | tf_op jit(solution)/shard_map/while/body/eval_jaxpr/sub | solution.py:94
  61.0 3.1 %fusion.82 = bf16[2,512,2,104]{1,3,2,0:T(8,128)(2,1)} fusion(bf16[2,512,2,104]{1,3,2,0:T(8,128)(2,1)} %get-tuple-element.164, s32[]{:T(128)} %get-tuple-element.163, bf16[1024,2,104]{0,2,1:T(8,128)(2,1)} %get-tuple-element.181, bf16[2,512,1024]{2,1,0:T(8,128)(2,1)} %get-tuple-element.150, f32[512,2]{0,1:T(2,128)S(1)} %bitcast.80), kind=kOutput, calls=%fused_computation.15.clone.1 | convolution fusion | flops 218316800 | bytes 2740736 | tf_op jit(solution)/shard_map/while/body/eval_jaxpr/hqk,khd->qhd/dot_general | solution.py:96
  68.0 4.6 %fusion.81 = (f32[2,512]{1,0:T(2,128)S(1)}, bf16[2,512,1024]{2,1,0:T(8,128)(2,1)}) fusion(pred[512,1024]{1,0:T(8,128)(4,1)S(1)} %fusion.80, bf16[1024,2,104]{0,2,1:T(8,128)(2,1)} %get-tuple-element.180, bf16[1024,2,104]{0,2,1:T(8,128)(2,1)} %get-tuple-element.179, s32[]{:T(128)S(6)} %select_n.34), kind=kOutput, calls=%fused_computation.84.clone.1 | convolution fusion | flops 223347712 | bytes 3788804 | tf_op jit(solution)/shard_map/while/body/eval_jaxpr/sub | solution.py:94
  72.6 3.1 %fusion.82 = bf16[2,512,2,104]{1,3,2,0:T(8,128)(2,1)} fusion(bf16[2,512,2,104]{1,3,2,0:T(8,128)(2,1)} %get-tuple-element.164, s32[]{:T(128)} %get-tuple-element.163, bf16[1024,2,104]{0,2,1:T(8,128)(2,1)} %get-tuple-element.181, bf16[2,512,1024]{2,1,0:T(8,128)(2,1)} %get-tuple-element.150, f32[512,2]{0,1:T(2,128)S(1)} %bitcast.80), kind=kOutput, calls=%fused_computation.15.clone.1 | convolution fusion | flops 218316800 | bytes 2740736 | tf_op jit(solution)/shard_map/while/body/eval_jaxpr/hqk,khd->qhd/dot_general | solution.py:96
  75.7 1.4 copy.16
  77.2 3.0 %convolution_convert_fusion.2 = bf16[1024,1664]{1,0:T(8,128)(2,1)} fusion(bf16[1024,208]{0,1:T(8,128)(2,1)S(1)} %bitcast.71, bf16[208,1664]{1,0:T(8,128)(2,1)S(1)} %copy-done.2), kind=kOutput, calls=%fused_computation.26 | convolution fusion | flops 710541312 | bytes 4526080 | tf_op jit(solution)/shard_map/dot_general | solution.py:107
  81.0 38.2 %reduce-scatter.3.cloned.1.call-done = bf16[128,1664]{1,0:T(8,128)(2,1)} async-done(((bf16[1024,1664]{1,0:T(8,128)(2,1)}), bf16[128,1664]{1,0:T(8,128)(2,1)}) %reduce-scatter.3.cloned.1.call-update) | async-done | bytes 426000 | tf_op jit(solution)/shard_map/reduce_scatter | solution.py:106
  119.2 2.1 fusion.53
  121.7 1.4 reshape.306
  123.4 11.3 %all_to_all.21 = bf16[32,8,832]{2,0,1:T(8,128)(2,1)S(1)} all-to-all(bf16[32,8,832]{2,0,1:T(8,128)(2,1)S(1)} %fusion.45), channel_id=1, replica_groups=mesh['tok'=32,'head'=8] {'head'}, dimensions={1} | all-to-all | bytes 851968 | tf_op jit(solution)/shard_map/all_to_all | solution.py:118
  134.7 39.1 %all-gather.5.cloned.1.call-done = bf16[832,4096]{1,0:T(8,128)(2,1)} async-done(((bf16[832,128]{1,0:T(8,128)(2,1)}), bf16[832,4096]{1,0:T(8,128)(2,1)}) %all-gather.5.cloned.1.call-update) | async-done | bytes 6815760 | tf_op jit(solution)/shard_map/all_gather | solution.py:124
  173.8 6.8 %convolution_convert_fusion = bf16[256,4096]{1,0:T(8,128)(2,1)} fusion(bf16[256,832]{1,0:T(8,128)(2,1)S(1)} %bitcast.73, bf16[832,4096]{1,0:T(8,128)(2,1)} %all-gather.5.cloned.1.call-done), kind=kOutput, calls=%fused_computation.24 | convolution fusion | flops 1745879040 | bytes 9338880 | tf_op jit(solution)/shard_map/dot_general | solution.py:122
  180.9 39.6 %reduce-scatter.5.cloned.1.call-done = bf16[32,4096]{1,0:T(8,128)(2,1)} async-done(((bf16[256,4096]{1,0:T(8,128)(2,1)}), bf16[32,4096]{1,0:T(8,128)(2,1)}) %reduce-scatter.5.cloned.1.call-update) | async-done | bytes 262160 | tf_op jit(solution)/shard_map/reduce_scatter | solution.py:127
  220.5 1.2 convolution_convert_fusion.1
  222.1 27.3 %all_to_all.22 = bf16[32,2,4096]{2,1,0:T(2,128)(2,1)S(1)} all-to-all(bf16[32,2,4096]{2,1,0:T(2,128)(2,1)S(1)} %reshape.307), channel_id=1, replica_groups=mesh['tok'=32,'head'=8] {'tok'}, dimensions={0} | all-to-all | bytes 1048576 | tf_op jit(solution)/shard_map/all_to_all | solution.py:143
  249.4 1.0 reshape.308
  (64 shorter events, 11.5 us)
Async XLA Ops:
  7.4 37.5 %copy-start = (bf16[3,208,1664]{2,1,0:T(8,128)(2,1)S(1)}, bf16[3,208,1664]{2,1,0:T(8,128)(2,1)}, u32[]{:S(2)}) copy-start(bf16[3,208,1664]{2,1,0:T(8,128)(2,1)} %param.15) | copy-start | bytes 6230020
  7.4 37.5 %all-gather.3.cloned.1.call-start = ((), (), s32[]{:S(2)}) async-start(), calls=%async_computation.4 | async-start | bytes 3833856 | tf_op jit(solution)/shard_map/all_gather | solution.py:66
  12.1 107.1 %reduce-scatter.3.cloned.1.call-start = ((), (), s32[]{:S(2)}) async-start(), calls=%async_computation.5 | async-start | bytes 3833856 | tf_op jit(solution)/shard_map/reduce_scatter | solution.py:106
  50.4 2.2 copy-start.3
  52.6 24.6 %copy-start.2 = (bf16[208,1664]{1,0:T(8,128)(2,1)S(1)}, bf16[208,1664]{1,0:T(8,128)(2,1)}, u32[]{:S(2)}) copy-start(bf16[208,1664]{1,0:T(8,128)(2,1)} %param.16) | copy-start | bytes 2076676
  80.2 0.7 copy-start.4
  80.2 39.0 %copy-start.1 = (bf16[128,1664]{1,0:T(8,128)(2,1)S(1)}, bf16[128,1664]{1,0:T(8,128)(2,1)}, u32[]{:S(2)}) copy-start(bf16[128,1664]{1,0:T(8,128)(2,1)} %param.13) | copy-start | bytes 1277956
  80.2 93.6 %all-gather.5.cloned.1.call-start = ((), (), s32[]{:S(2)}) async-start(), calls=%async_computation.6 | async-start | bytes 7028736 | tf_op jit(solution)/shard_map/all_gather | solution.py:124
  80.8 139.7 %reduce-scatter.5.cloned.1.call-start = ((), (), s32[]{:S(2)}) async-start(), calls=%async_computation.7 | async-start | bytes 2359296 | tf_op jit(solution)/shard_map/reduce_scatter | solution.py:127
  173.8 6.8 %copy-start.5 = (s32[32,1]{0,1:T(1,128)S(1)}, s32[32,1]{0,1:T(1,128)}, u32[]{:S(2)}) copy-start(s32[32,1]{0,1:T(1,128)} %param.23) | copy-start | bytes 388
Sparse Core Ops, SparseCore 0:
  12.2 32.6 all-gather.2
  80.3 38.8 reduce-scatter.2
  180.7 39.7 reduce-scatter.4
Sparse Core Ops, SparseCore 1:
  83.2 90.5 all-gather.4
where the time goes:
time: 258 us; the launch traced here: 257 us
  waiting for transfers between devices  146 us (57%)
  blocking collectives  38.6 us (15%)
  matrix products  30.8 us (12%)
  other arithmetic  16.1 us (6%)
  between operations  14.7 us (6%)
  local copies, waits for them, and re-layouts  7.14 us (3%)
  loops' own time  3.76 us (1%)
    reduce_scatter x1, waiting for transfers between devices, body(): lax.psum_scatter(column_terms.astype(jnp.bfloat16), 'head', scatter_dimen...  39.6 us
    all_gather x1, waiting for transfers between devices, body(): lax.all_gather(merge_weight, 'tok', axis=1, tiled=True)  39.1 us
    reduce_scatter x1, waiting for transfers between devices, body(): lax.psum_scatter(jnp.dot(heads_out, out_weight, preferred_element_type=jn...  38.2 us
    all_gather x1, waiting for transfers between devices, body(): lax.all_gather(normed, 'head', axis=0, tiled=True)  28.8 us
    all_to_all x1, blocking collectives, body(): lax.all_to_all(send_rows, 'tok', split_axis=0, concat_axis=0, tiled=True)  27.3 us
    all_to_all x1, blocking collectives, body(): lax.all_to_all(window_rows.reshape(local_rows // 4, 4 * D), 'head', split...  11.3 us
    sub x2, matrix products, query_block(): exponent = jnp.where(allowed[None], jnp.exp(masked - row_top), 0.0)  9.22 us
    dot_general x1, matrix products, body(): jnp.dot(merged_slice, lax.all_gather(merge_weight, 'tok', axis=1, tiled=T...  6.76 us
  transfers between devices with their start and end apart: 4, of which 4 were waited for; matrix products, arithmetic and copies ran while one was open for 3% of the time, Pallas kernels for 0%

commit v1 on v0

--- a/solution.py
+++ b/solution.py
@@ -6,6 +6,7 @@
 D = 1664
 HD = 104
 SIDE = 16
+CHUNKS = 2
 
 
 EPSILON = 1e-06
@@ -119,14 +120,6 @@
         window_rows.reshape(local_rows // 4, 4 * D), "head", split_axis=1, concat_axis=0, tiled=True
     )
     merged_count = local_rows // 4
-    column_terms = jnp.dot(
-        merged_slice,
-        lax.all_gather(merge_weight, "tok", axis=1, tiled=True),
-        preferred_element_type=jnp.float32,
-    )
-    projected = lax.psum_scatter(
-        column_terms.astype(jnp.bfloat16), "head", scatter_dimension=0, tiled=True
-    )
     slot_count = max(2, 2 * merged_count // tok_count)
     owner_col = owners[:, 0]
     owner_hot = (owner_col[:, None] == jnp.arange(tok_count, dtype=jnp.int32)[None, :]).astype(
@@ -138,9 +131,24 @@
     select = (
         jnp.arange(tok_count * slot_count, dtype=jnp.int32)[:, None] == target[None, :]
     ).astype(jnp.bfloat16)
-    send_rows = jnp.dot(select, projected, preferred_element_type=jnp.float32).astype(jnp.bfloat16)
-    send_rows = send_rows.reshape(tok_count, slot_count, -1)
-    received = lax.all_to_all(send_rows, "tok", split_axis=0, concat_axis=0, tiled=True)
+    local_cols = merge_weight.shape[1]
+    chunk_cols = local_cols // CHUNKS
+    pieces = []
+    for chunk in range(CHUNKS):
+        weight_part = lax.all_gather(
+            merge_weight[:, chunk * chunk_cols : (chunk + 1) * chunk_cols], "tok", axis=1, tiled=True
+        )
+        column_terms = jnp.dot(merged_slice, weight_part, preferred_element_type=jnp.float32)
+        projected = lax.psum_scatter(
+            column_terms.astype(jnp.bfloat16), "head", scatter_dimension=0, tiled=True
+        )
+        send_rows = jnp.dot(select, projected, preferred_element_type=jnp.float32).astype(
+            jnp.bfloat16
+        )
+        send_rows = send_rows.reshape(tok_count, slot_count, -1)
+        received = lax.all_to_all(send_rows, "tok", split_axis=0, concat_axis=0, tiled=True)
+        pieces.append(received.reshape(tok_count * slot_count, tok_count, 1, chunk_cols))
+    received = jnp.concatenate(pieces, axis=2)
     return received.reshape(tok_count * slot_count, -1)
 
 

time: 258 us -> 325 us (1.26)
  waiting for transfers between devices: 146 us -> 209 us
  blocking collectives: 38.6 us -> 0 us
  starting transfers between devices: 0.13 us -> 21.1 us
  local copies, waits for them, and re-layouts: 7.14 us -> 18 us
  other arithmetic: 16.1 us -> 21.6 us
    all_gather x1 -> x2, waiting for transfers between devices: 39.1 us -> 106 us  [body(): lax.all_gather(merge_weight[:, chunk * chunk_cols:(chunk + 1) * chunk_col...]
    all_to_all x2 -> x0, blocking collectives: 38.6 us -> none  [the longest x1 27.3 us: body(): lax.all_to_all(send_rows, 'tok', split_axis=0, concat_axis=0, tiled=True)]
    all_to_all x0 -> x3, starting transfers between devices: none -> 21 us  [the longest x2 15.1 us: body(): lax.all_to_all(send_rows, 'tok', split_axis=0, concat_axis=0, tiled=True)]
    reduce_scatter x1 -> x2, waiting for transfers between devices: 39.6 us -> 26.6 us  [body(): lax.psum_scatter(column_terms.astype(jnp.bfloat16), 'head', scatter_dimen...]
    all_to_all x0 -> x3, waiting for transfers between devices: none -> 12 us  [the longest x2 12 us: body(): lax.all_to_all(send_rows, 'tok', split_axis=0, concat_axis=0, tiled=True)]
    concatenate x0 -> x1, other arithmetic: none -> 4.7 us  [body(): received = jnp.concatenate(pieces, axis=2)]
    reshape x0 -> x2, local copies, waits for them, and re-layouts: none -> 4.01 us  [body(): received.reshape(tok_count * slot_count, tok_count, 1, chunk_cols)]
    dot_general x1 -> x2, matrix products: 6.76 us -> 8.62 us  [body(): jnp.dot(merged_slice, weight_part, preferred_element_type=jnp.float32)]
  transfers between devices with their start and end apart: 4 -> 9, of which waited for: 4 -> 6; matrix products, arithmetic and copies ran while one was open for 3% -> 8% of each run, Pallas kernels for 0% -> 0%
where the time goes in v1:
time: 325 us; the launch traced here: 323 us
  waiting for transfers between devices  209 us (64%)
  matrix products  33.7 us (10%)
  other arithmetic  21.6 us (7%)
  starting transfers between devices  21.1 us (6%)
  local copies, waits for them, and re-layouts  18 us (6%)
  between operations  14.8 us (5%)
  loops' own time  3.84 us (1%)
    all_gather x2, waiting for transfers between devices, body(): lax.all_gather(merge_weight[:, chunk * chunk_cols:(chunk + 1) * chunk_col...  106 us
    reduce_scatter x1, waiting for transfers between devices, body(): lax.psum_scatter(jnp.dot(heads_out, out_weight, preferred_element_type=jn...  35.6 us
    all_gather x1, waiting for transfers between devices, body(): lax.all_gather(normed, 'head', axis=0, tiled=True)  28.8 us
    reduce_scatter x2, waiting for transfers between devices, body(): lax.psum_scatter(column_terms.astype(jnp.bfloat16), 'head', scatter_dimen...  26.6 us
    all_to_all x2, starting transfers between devices, body(): lax.all_to_all(send_rows, 'tok', split_axis=0, concat_axis=0, tiled=True)  15.1 us
    all_to_all x2, waiting for transfers between devices, body(): lax.all_to_all(send_rows, 'tok', split_axis=0, concat_axis=0, tiled=True)  12 us
    sub x2, matrix products, query_block(): exponent = jnp.where(allowed[None], jnp.exp(masked - row_top), 0.0)  9.18 us
    dot_general x2, matrix products, body(): jnp.dot(merged_slice, weight_part, preferred_element_type=jnp.float32)  8.62 us
  transfers between devices with their start and end apart: 9, of which 6 were waited for; matrix products, arithmetic and copies ran while one was open for 8% of the time, Pallas kernels for 0%

profile of v1, /device:TPU:57, one launch (start us, length us, event | category | flops | bytes accessed | tf_op | source)
XLA Modules:
  0.0 322.6 jit_solution(3806696823510344831)
XLA Ops:
  10.0 2.1 fusion.48
  16.1 28.8 %all-gather.4.cloned.1.call-done = bf16[1024,1664]{1,0:T(8,128)(2,1)} async-done(((bf16[128,1664]{1,0:T(8,128)(2,1)}), bf16[1024,1664]{1,0:T(8,128)(2,1)}) %all-gather.4.cloned.1.call-update) | async-done | bytes 3407888 | tf_op jit(solution)/shard_map/all_gather | solution.py:67
  44.9 4.5 %fusion.39 = f32[1024,3,2,104]{0,3,2,1:T(8,128)S(1)} fusion(bf16[3,2,104,1664]{3,2,1,0:T(8,128)(2,1)S(1)} %bitcast.73, bf16[1024,1664]{1,0:T(8,128)(2,1)} %all-gather.4.cloned.1.call-done), kind=kOutput, calls=%fused_computation.25 | convolution fusion | flops 2126512128 | bytes 8040448 | tf_op jit(solution)/shard_map/dot_general | solution.py:66
  52.6 23.3 %while.10 = (s32[]{:T(128)}, bf16[2,512,2,104]{1,3,2,0:T(8,128)(2,1)}, s32[2]{0:T(128)S(1)}, s32[1024]{0:T(1024)S(1)}, pred[1024]{0:T(1024)(128)(4,1)S(1)}, /*in...) while((s32[]{:T(128)}, ...), condition=%wide.region_9.10_spmd, body=%wide.region_6.0_spmd.sunk | while | flops 443762176 | bytes 7068851 | solution.py:106
  56.6 4.6 %fusion.86 = (f32[2,512]{1,0:T(2,128)S(1)}, bf16[2,512,1024]{2,1,0:T(8,128)(2,1)}) fusion(pred[512,1024]{1,0:T(8,128)(4,1)S(1)} %fusion.85, bf16[1024,2,104]{0,2,1:T(8,128)(2,1)} %get-tuple-element.182, bf16[1024,2,104]{0,2,1:T(8,128)(2,1)} %get-tuple-element.181, s32[]{:T(128)S(6)} %select_n.34), kind=kOutput, calls=%fused_computation.88.clone.1 | convolution fusion | flops 223347712 | bytes 3788804 | tf_op jit(solution)/shard_map/while/body/eval_jaxpr/sub | solution.py:95
  61.1 3.1 fusion.87
  68.2 4.6 %fusion.86 = (f32[2,512]{1,0:T(2,128)S(1)}, bf16[2,512,1024]{2,1,0:T(8,128)(2,1)}) fusion(pred[512,1024]{1,0:T(8,128)(4,1)S(1)} %fusion.85, bf16[1024,2,104]{0,2,1:T(8,128)(2,1)} %get-tuple-element.182, bf16[1024,2,104]{0,2,1:T(8,128)(2,1)} %get-tuple-element.181, s32[]{:T(128)S(6)} %select_n.34), kind=kOutput, calls=%fused_computation.88.clone.1 | convolution fusion | flops 223347712 | bytes 3788804 | tf_op jit(solution)/shard_map/while/body/eval_jaxpr/sub | solution.py:95
  72.8 3.1 fusion.87
  75.9 1.4 copy.28
  77.4 3.0 convolution_convert_fusion
  83.3 35.6 %reduce-scatter.4.cloned.1.call-done = bf16[128,1664]{1,0:T(8,128)(2,1)} async-done(((bf16[1024,1664]{1,0:T(8,128)(2,1)}), bf16[128,1664]{1,0:T(8,128)(2,1)}) %reduce-scatter.4.cloned.1.call-update) | async-done | bytes 426000 | tf_op jit(solution)/shard_map/reduce_scatter | solution.py:107
  118.9 2.1 fusion.54
  123.9 5.9 %all-to-all-start = ((bf16[32,8,832]{2,0,1:T(8,128)(2,1)}), bf16[32,8,832]{2,0,1:T(8,128)(2,1)S(1)}, u32[]{:S(2)}, u32[]{:S(2)}) async-start(bf16[32,8,832]{2,0,1:T(8,128)(2,1)} %fusion.45), calls=%async_computation.1 | async-start | bytes 917504 | tf_op jit(solution)/shard_map/all_to_all | solution.py:119
  129.8 30.9 %all-gather.8.cloned.1.call-done = bf16[832,2048]{0,1:T(8,128)(2,1)} async-done(((bf16[832,64]{0,1:T(8,128)(2,1)}), bf16[832,2048]{0,1:T(8,128)(2,1)}) %all-gather.8.cloned.1.call-update) | async-done | bytes 3407888 | tf_op jit(solution)/shard_map/all_gather | solution.py:138
  160.7 4.3 %convolution_convert_fusion.1 = bf16[256,2048]{1,0:T(8,128)(2,1)} fusion(bf16[256,832]{1,0:T(8,128)(2,1)S(1)} %bitcast.76, bf16[832,2048]{0,1:T(8,128)(2,1)} %all-gather.8.cloned.1.call-done), kind=kOutput, calls=%fused_computation.27 | convolution fusion | flops 872939520 | bytes 4882432 | tf_op jit(solution)/shard_map/dot_general | solution.py:141
  165.1 75.5 %all-gather.6.cloned.1.call-done = bf16[832,2048]{0,1:T(8,128)(2,1)} async-done(((bf16[832,64]{0,1:T(8,128)(2,1)}), bf16[832,2048]{0,1:T(8,128)(2,1)}) %all-gather.6.cloned.1.call-update) | async-done | bytes 3407888 | tf_op jit(solution)/shard_map/all_gather | solution.py:138
  240.6 4.3 %convolution_convert_fusion.2 = bf16[256,2048]{1,0:T(8,128)(2,1)} fusion(bf16[256,832]{1,0:T(8,128)(2,1)S(1)} %bitcast.77, bf16[832,2048]{0,1:T(8,128)(2,1)} %all-gather.6.cloned.1.call-done), kind=kOutput, calls=%fused_computation.28 | convolution fusion | flops 872939520 | bytes 4882432 | tf_op jit(solution)/shard_map/dot_general | solution.py:141
  247.3 5.5 %all-to-all-start.2 = ((bf16[32,2,2048]{2,1,0:T(2,128)(2,1)}), bf16[32,2,2048]{2,1,0:T(2,128)(2,1)S(1)}, u32[]{:S(2)}, u32[]{:S(2)}) async-start(bf16[32,2,2048]{2,1,0:T(2,128)(2,1)} %reshape.318), calls=%async_computation.5 | async-start | bytes 524288 | tf_op jit(solution)/shard_map/all_to_all | solution.py:149
  252.7 26.5 %reduce-scatter.6.cloned.1.call-done = bf16[32,2048]{1,0:T(8,128)(2,1)} async-done(((bf16[256,2048]{1,0:T(8,128)(2,1)}), bf16[32,2048]{1,0:T(8,128)(2,1)}) %reduce-scatter.6.cloned.1.call-update) | async-done | bytes 131088 | tf_op jit(solution)/shard_map/reduce_scatter | solution.py:142
  281.3 9.6 %all-to-all-start.1 = ((bf16[32,2,2048]{2,1,0:T(2,128)(2,1)}), bf16[32,2,2048]{2,1,0:T(2,128)(2,1)}, u32[]{:S(2)}, u32[]{:S(2)}) async-start(bf16[32,2,2048]{2,1,0:T(2,128)(2,1)} %reshape.316), calls=%async_computation.3 | async-start | bytes 524288 | tf_op jit(solution)/shard_map/all_to_all | solution.py:149
  291.5 12.0 %all-to-all-done.1 = bf16[32,2,2048]{2,1,0:T(2,128)(2,1)} async-done(((bf16[32,2,2048]{2,1,0:T(2,128)(2,1)}), bf16[32,2,2048]{2,1,0:T(2,128)(2,1)}, u32[]{:S(2)}, u32[]{:S(2)}) %all-to-all-start.1) | async-done | bytes 262176 | tf_op jit(solution)/shard_map/all_to_all | solution.py:149
  303.5 3.4 %reshape.322 = bf16[64,32,1,64]{3,2,1,0:T(2,128)(2,1)} reshape(bf16[32,2,2048]{2,1,0:T(2,128)(2,1)} %all-to-all-done.1) | data formatting | bytes 524288 | tf_op jit(solution)/shard_map/reshape | solution.py:150
  306.9 4.7 %pad_maximum_fusion = bf16[64,32,2,64]{3,2,1,0:T(2,128)(2,1)} fusion(bf16[64,32,1,64]{3,2,1,0:T(2,128)(2,1)S(1)} %reshape.323, bf16[64,32,1,64]{3,2,1,0:T(2,128)(2,1)} %reshape.322), kind=kLoop, calls=%fused_computation.34 | loop fusion | flops 1048576 | bytes 1048576 | tf_op jit(solution)/shard_map/concatenate | solution.py:151
  311.6 3.9 %reshape.320 = bf16[64,4096]{1,0:T(8,128)(2,1)} reshape(bf16[64,32,2,64]{3,2,1,0:T(2,128)(2,1)} %pad_maximum_fusion) | data formatting | bytes 1048576 | tf_op jit(solution)/shard_map/reshape | solution.py:152
  (85 shorter events, 24.6 us)
Async XLA Ops:
  7.4 37.5 %copy-start = (bf16[3,208,1664]{2,1,0:T(8,128)(2,1)S(1)}, bf16[3,208,1664]{2,1,0:T(8,128)(2,1)}, u32[]{:S(2)}) copy-start(bf16[3,208,1664]{2,1,0:T(8,128)(2,1)} %param.15) | copy-start | bytes 6230020
  7.4 37.5 %all-gather.4.cloned.1.call-start = ((), (), s32[]{:S(2)}) async-start(), calls=%async_computation.6 | async-start | bytes 3833856 | tf_op jit(solution)/shard_map/all_gather | solution.py:67
  12.1 106.8 %reduce-scatter.4.cloned.1.call-start = ((), (), s32[]{:S(2)}) async-start(), calls=%async_computation.7 | async-start | bytes 3833856 | tf_op jit(solution)/shard_map/reduce_scatter | solution.py:107
  50.4 2.2 copy-start.4
  52.6 24.8 %copy-start.3 = (bf16[208,1664]{1,0:T(8,128)(2,1)S(1)}, bf16[208,1664]{1,0:T(8,128)(2,1)}, u32[]{:S(2)}) copy-start(bf16[208,1664]{1,0:T(8,128)(2,1)} %param.16) | copy-start | bytes 2076676
  80.4 0.9 copy-start.2
  80.4 2.7 copy-start.5
  80.4 38.5 %copy-start.1 = (bf16[128,1664]{1,0:T(8,128)(2,1)S(1)}, bf16[128,1664]{1,0:T(8,128)(2,1)}, u32[]{:S(2)}) copy-start(bf16[128,1664]{1,0:T(8,128)(2,1)} %param.13) | copy-start | bytes 1277956
  80.4 80.3 %all-gather.8.cloned.1.call-start = ((), (), s32[]{:S(2)}) async-start(), calls=%async_computation.10 | async-start | bytes 3784704 | tf_op jit(solution)/shard_map/all_gather | solution.py:138
  82.3 158.3 %all-gather.6.cloned.1.call-start = ((), (), s32[]{:S(2)}) async-start(), calls=%async_computation.8 | async-start | bytes 3784704 | tf_op jit(solution)/shard_map/all_gather | solution.py:138
  123.9 36.8 %all-to-all-start = ((bf16[32,8,832]{2,0,1:T(8,128)(2,1)}), bf16[32,8,832]{2,0,1:T(8,128)(2,1)S(1)}, u32[]{:S(2)}, u32[]{:S(2)}) async-start(bf16[32,8,832]{2,0,1:T(8,128)(2,1)} %fusion.45), calls=%async_computation.1 | async-start | bytes 917504 | tf_op jit(solution)/shard_map/all_to_all | solution.py:119
  129.8 115.5 %reduce-scatter.8.cloned.1.call-start = ((), (), s32[]{:S(2)}) async-start(), calls=%async_computation.11 | async-start | bytes 1179648 | tf_op jit(solution)/shard_map/reduce_scatter | solution.py:142
  165.1 79.8 %copy-start.6 = (s32[32,1]{0,1:T(1,128)S(1)}, s32[32,1]{0,1:T(1,128)}, u32[]{:S(2)}) copy-start(s32[32,1]{0,1:T(1,128)} %param.23) | copy-start | bytes 388
  165.1 114.2 %reduce-scatter.6.cloned.1.call-start = ((), (), s32[]{:S(2)}) async-start(), calls=%async_computation.9 | async-start | bytes 1179648 | tf_op jit(solution)/shard_map/reduce_scatter | solution.py:142
  247.3 34.0 %all-to-all-start.2 = ((bf16[32,2,2048]{2,1,0:T(2,128)(2,1)}), bf16[32,2,2048]{2,1,0:T(2,128)(2,1)S(1)}, u32[]{:S(2)}, u32[]{:S(2)}) async-start(bf16[32,2,2048]{2,1,0:T(2,128)(2,1)} %reshape.318), calls=%async_computation.5 | async-start | bytes 524288 | tf_op jit(solution)/shard_map/all_to_all | solution.py:149
  281.3 22.2 %all-to-all-start.1 = ((bf16[32,2,2048]{2,1,0:T(2,128)(2,1)}), bf16[32,2,2048]{2,1,0:T(2,128)(2,1)}, u32[]{:S(2)}, u32[]{:S(2)}) async-start(bf16[32,2,2048]{2,1,0:T(2,128)(2,1)} %reshape.316), calls=%async_computation.3 | async-start | bytes 524288 | tf_op jit(solution)/shard_map/all_to_all | solution.py:149
Sparse Core Ops, SparseCore 0:
  12.2 32.6 all-gather.3
  80.6 38.2 reduce-scatter.3
  165.2 34.1 reduce-scatter.7
  245.0 34.2 reduce-scatter.5
Sparse Core Ops, SparseCore 1:
  83.5 77.2 all-gather.7
  163.2 77.4 all-gather.5

commit v2 on v0

--- a/solution.py
+++ b/solution.py
@@ -6,6 +6,9 @@
 D = 1664
 HD = 104
 SIDE = 16
+TOK = ("tx", "tz")
+HEAD = ("hy", "hc")
+Z_SIZE = 8
 
 
 EPSILON = 1e-06
@@ -51,9 +54,9 @@
     local_rows = tokens.shape[0]
     head_width = qkv_weight.shape[1]
     heads_here = head_width // HD
-    tok_count = lax.axis_size("tok")
+    tok_count = lax.axis_size("tx") * lax.axis_size("tz")
     image_count = grid_sizes.shape[1]
-    local_image = segment_ids - lax.axis_index("tok") * image_count
+    local_image = segment_ids - (lax.axis_index("tx") * lax.axis_size("tz") + lax.axis_index("tz")) * image_count
     image_match = local_image[:, None] == jnp.arange(image_count, dtype=jnp.int32)[None, :]
     grid_float = grid_sizes.astype(jnp.float32)
     row_size = jnp.sum(jnp.where(image_match, grid_float[0][None, :], 0.0), axis=1)
@@ -63,7 +66,7 @@
     stacked_weight = qkv_weight.reshape(3 * head_width, D)
     normed = layer_norm(tokens.astype(jnp.float32), attn_gain).astype(jnp.bfloat16)
     projected_rows = lax.dot_general(
-        lax.all_gather(normed, "head", axis=0, tiled=True),
+        lax.all_gather(normed, HEAD, axis=0, tiled=True),
         stacked_weight,
         (((1,), (1,)), ((), ())),
         preferred_element_type=jnp.float32,
@@ -105,7 +108,7 @@
     heads_out = lax.map(query_block, block_starts).reshape(group_len, head_width)
     attn_rows = lax.psum_scatter(
         jnp.dot(heads_out, out_weight, preferred_element_type=jnp.float32).astype(jnp.bfloat16),
-        "head",
+        HEAD,
         scatter_dimension=0,
         tiled=True,
     ).astype(jnp.float32)
@@ -116,16 +119,18 @@
         jnp.bfloat16
     )
     merged_slice = lax.all_to_all(
-        window_rows.reshape(local_rows // 4, 4 * D), "head", split_axis=1, concat_axis=0, tiled=True
+        window_rows.reshape(local_rows // 4, 4 * D), HEAD, split_axis=1, concat_axis=0, tiled=True
     )
     merged_count = local_rows // 4
     column_terms = jnp.dot(
         merged_slice,
-        lax.all_gather(merge_weight, "tok", axis=1, tiled=True),
+        lax.all_gather(
+            lax.all_gather(merge_weight, "tz", axis=1, tiled=True), "tx", axis=1, tiled=True
+        ),
         preferred_element_type=jnp.float32,
     )
     projected = lax.psum_scatter(
-        column_terms.astype(jnp.bfloat16), "head", scatter_dimension=0, tiled=True
+        column_terms.astype(jnp.bfloat16), HEAD, scatter_dimension=0, tiled=True
     )
     slot_count = max(2, 2 * merged_count // tok_count)
     owner_col = owners[:, 0]
@@ -140,24 +145,28 @@
     ).astype(jnp.bfloat16)
     send_rows = jnp.dot(select, projected, preferred_element_type=jnp.float32).astype(jnp.bfloat16)
     send_rows = send_rows.reshape(tok_count, slot_count, -1)
-    received = lax.all_to_all(send_rows, "tok", split_axis=0, concat_axis=0, tiled=True)
+    received = lax.all_to_all(send_rows, TOK, split_axis=0, concat_axis=0, tiled=True)
     return received.reshape(tok_count * slot_count, -1)
 
 
 def solution(mesh):
+    tok_size, head_size = (mesh.shape[name] for name in mesh.axis_names)
+    split_mesh = jax.sharding.Mesh(
+        mesh.devices.reshape(tok_size // Z_SIZE, Z_SIZE, head_size // 2, 2), TOK + HEAD
+    )
     placed = (
-        P(("tok", "head"), None),
+        P(TOK + HEAD, None),
         P(),
-        P(None, "head", None),
-        P("head", None),
+        P(None, HEAD, None),
+        P(HEAD, None),
         P(),
-        P("head", "tok"),
-        P(None, "tok"),
-        P("tok"),
-        P(None, "tok"),
-        P("tok"),
-        P(("tok", "head"), None),
+        P(HEAD, TOK),
+        P(None, TOK),
+        P(TOK),
+        P(None, TOK),
+        P(TOK),
+        P(TOK + HEAD, None),
     )
     return jax.shard_map(
-        body, mesh=mesh, in_specs=placed, out_specs=P(("tok", "head"), None), check_vma=False
+        body, mesh=split_mesh, in_specs=placed, out_specs=P(TOK + HEAD, None), check_vma=False
     )

time: 258 us -> 284 us (1.10)
  waiting for transfers between devices: 146 us -> 173 us
    all_gather x2 -> x3, waiting for transfers between devices: 67.9 us -> 92.9 us  [the longest x1 58.5 us: body(): lax.all_gather(lax.all_gather(merge_weight, 'tz', axis=1, tiled=True), 't...]
    reduce_scatter x1, waiting for transfers between devices: 38.2 us -> 43.7 us  [body(): lax.psum_scatter(jnp.dot(heads_out, out_weight, preferred_element_type=jn...]
    reduce_scatter x1, waiting for transfers between devices: 39.6 us -> 35.4 us  [body(): lax.psum_scatter(column_terms.astype(jnp.bfloat16), HEAD, scatter_dimensi...]
  transfers between devices with their start and end apart: 4 -> 5, of which waited for: 4 -> 5; matrix products, arithmetic and copies ran while one was open for 3% -> 14% of each run, Pallas kernels for 0% -> 0%
where the time goes in v2:
time: 284 us; the launch traced here: 283 us
  waiting for transfers between devices  173 us (61%)
  blocking collectives  39.2 us (14%)
  matrix products  30.9 us (11%)
  other arithmetic  16.1 us (6%)
  between operations  13.4 us (5%)
  local copies, waits for them, and re-layouts  7.1 us (2%)
  loops' own time  3.76 us (1%)
    all_gather x1, waiting for transfers between devices, body(): lax.all_gather(lax.all_gather(merge_weight, 'tz', axis=1, tiled=True), 't...  58.5 us
    reduce_scatter x1, waiting for transfers between devices, body(): lax.psum_scatter(jnp.dot(heads_out, out_weight, preferred_element_type=jn...  43.7 us
    reduce_scatter x1, waiting for transfers between devices, body(): lax.psum_scatter(column_terms.astype(jnp.bfloat16), HEAD, scatter_dimensi...  35.4 us
    all_gather x1, waiting for transfers between devices, body(): lax.all_gather(normed, HEAD, axis=0, tiled=True)  28 us
    all_to_all x1, blocking collectives, body(): lax.all_to_all(send_rows, TOK, split_axis=0, concat_axis=0, tiled=True)  27.3 us
    all_to_all x1, blocking collectives, body(): lax.all_to_all(window_rows.reshape(local_rows // 4, 4 * D), HEAD, split_a...  11.9 us
    sub x2, matrix products, query_block(): exponent = jnp.where(allowed[None], jnp.exp(masked - row_top), 0.0)  9.24 us
    dot_general x1, matrix products, body(): jnp.dot(merged_slice, lax.all_gather(lax.all_gather(merge_weight, 'tz', a...  6.76 us
  transfers between devices with their start and end apart: 5, of which 5 were waited for; matrix products, arithmetic and copies ran while one was open for 14% of the time, Pallas kernels for 0%

profile of v2, /device:TPU:57, one launch (start us, length us, event | category | flops | bytes accessed | tf_op | source)
XLA Modules:
  0.0 283.4 jit_solution(1939351082981799064)
XLA Ops:
  6.5 1.3 convert_reduce_fusion
  7.8 1.3 fusion.46
  9.1 2.1 fusion.48
  15.1 1.0 multiply_cosine_fusion.1
  16.0 28.0 %all-gather.4.cloned.1.call-done = bf16[1024,1664]{1,0:T(8,128)(2,1)} async-done(((bf16[128,1664]{1,0:T(8,128)(2,1)}), bf16[1024,1664]{1,0:T(8,128)(2,1)}) %all-gather.4.cloned.1.call-update) | async-done | bytes 3407888 | tf_op jit(solution)/shard_map/all_gather | solution.py:69
  44.1 4.5 %fusion.39 = f32[1024,3,2,104]{0,3,2,1:T(8,128)S(1)} fusion(bf16[3,2,104,1664]{3,2,1,0:T(8,128)(2,1)S(1)} %bitcast.70, bf16[1024,1664]{1,0:T(8,128)(2,1)} %all-gather.4.cloned.1.call-done), kind=kOutput, calls=%fused_computation.27 | convolution fusion | flops 2126512128 | bytes 8040448 | tf_op jit(solution)/shard_map/dot_general | solution.py:68
  51.8 23.2 %while.10 = (s32[]{:T(128)}, bf16[2,512,2,104]{1,3,2,0:T(8,128)(2,1)}, s32[2]{0:T(128)S(1)}, s32[1024]{0:T(1024)S(1)}, pred[1024]{0:T(1024)(128)(4,1)S(1)}, /*in...) while((s32[]{:T(128)}, ...), condition=%wide.region_9.10_spmd, body=%wide.region_6.0_spmd.sunk | while | flops 443762176 | bytes 7069351 | solution.py:108
  55.6 4.6 %fusion.81 = (f32[2,512]{1,0:T(2,128)S(1)}, bf16[2,512,1024]{2,1,0:T(8,128)(2,1)}) fusion(pred[512,1024]{1,0:T(8,128)(4,1)S(1)} %fusion.80, bf16[1024,2,104]{0,2,1:T(8,128)(2,1)} %get-tuple-element.180, bf16[1024,2,104]{0,2,1:T(8,128)(2,1)} %get-tuple-element.179, s32[]{:T(128)S(6)} %select_n.34), kind=kOutput, calls=%fused_computation.84.clone.1 | convolution fusion | flops 223347712 | bytes 3788804 | tf_op jit(solution)/shard_map/while/body/eval_jaxpr/sub | solution.py:97
  60.2 3.1 %fusion.82 = bf16[2,512,2,104]{1,3,2,0:T(8,128)(2,1)} fusion(bf16[2,512,2,104]{1,3,2,0:T(8,128)(2,1)} %get-tuple-element.164, s32[]{:T(128)} %get-tuple-element.163, bf16[1024,2,104]{0,2,1:T(8,128)(2,1)} %get-tuple-element.181, bf16[2,512,1024]{2,1,0:T(8,128)(2,1)} %get-tuple-element.150, f32[512,2]{0,1:T(2,128)S(1)} %bitcast.80), kind=kOutput, calls=%fused_computation.15.clone.1 | convolution fusion | flops 218316800 | bytes 2740736 | tf_op jit(solution)/shard_map/while/body/eval_jaxpr/hqk,khd->qhd/dot_general | solution.py:99
  67.2 4.6 %fusion.81 = (f32[2,512]{1,0:T(2,128)S(1)}, bf16[2,512,1024]{2,1,0:T(8,128)(2,1)}) fusion(pred[512,1024]{1,0:T(8,128)(4,1)S(1)} %fusion.80, bf16[1024,2,104]{0,2,1:T(8,128)(2,1)} %get-tuple-element.180, bf16[1024,2,104]{0,2,1:T(8,128)(2,1)} %get-tuple-element.179, s32[]{:T(128)S(6)} %select_n.34), kind=kOutput, calls=%fused_computation.84.clone.1 | convolution fusion | flops 223347712 | bytes 3788804 | tf_op jit(solution)/shard_map/while/body/eval_jaxpr/sub | solution.py:97
  71.8 3.1 %fusion.82 = bf16[2,512,2,104]{1,3,2,0:T(8,128)(2,1)} fusion(bf16[2,512,2,104]{1,3,2,0:T(8,128)(2,1)} %get-tuple-element.164, s32[]{:T(128)} %get-tuple-element.163, bf16[1024,2,104]{0,2,1:T(8,128)(2,1)} %get-tuple-element.181, bf16[2,512,1024]{2,1,0:T(8,128)(2,1)} %get-tuple-element.150, f32[512,2]{0,1:T(2,128)S(1)} %bitcast.80), kind=kOutput, calls=%fused_computation.15.clone.1 | convolution fusion | flops 218316800 | bytes 2740736 | tf_op jit(solution)/shard_map/while/body/eval_jaxpr/hqk,khd->qhd/dot_general | solution.py:99
  74.9 1.5 copy.16
  76.5 3.0 %convolution_convert_fusion.2 = bf16[1024,1664]{1,0:T(8,128)(2,1)} fusion(bf16[1024,208]{0,1:T(8,128)(2,1)S(1)} %bitcast.71, bf16[208,1664]{1,0:T(8,128)(2,1)S(1)} %copy-done.2), kind=kOutput, calls=%fused_computation.26 | convolution fusion | flops 710541312 | bytes 4526080 | tf_op jit(solution)/shard_map/dot_general | solution.py:110
  79.5 6.4 %all-gather.6.cloned.1.call-done = bf16[832,1024]{1,0:T(8,128)(2,1)} async-done(((bf16[832,128]{1,0:T(8,128)(2,1)}), bf16[832,1024]{1,0:T(8,128)(2,1)}) %all-gather.6.cloned.1.call-update) | async-done | bytes 1703952 | tf_op jit(solution)/shard_map/all_gather | solution.py:128
  86.1 43.7 %reduce-scatter.3.cloned.1.call-done = bf16[128,1664]{1,0:T(8,128)(2,1)} async-done(((bf16[1024,1664]{1,0:T(8,128)(2,1)}), bf16[128,1664]{1,0:T(8,128)(2,1)}) %reduce-scatter.3.cloned.1.call-update) | async-done | bytes 426000 | tf_op jit(solution)/shard_map/reduce_scatter | solution.py:109
  129.8 2.1 fusion.53
  132.3 1.4 reshape.306
  134.0 11.9 %all_to_all.21 = bf16[32,8,832]{2,0,1:T(8,128)(2,1)S(1)} all-to-all(bf16[32,8,832]{2,0,1:T(8,128)(2,1)S(1)} %fusion.45), channel_id=1, replica_groups=mesh['tx'=4,'tz'=8,'hy'=4,'hc'=2] {'hy','hc'}, dimensions={1} | all-to-all | bytes 851968 | tf_op jit(solution)/shard_map/all_to_all | solution.py:121
  145.9 58.5 %all-gather.8.cloned.1.call-done = bf16[832,4096]{1,0:T(8,128)(2,1)} async-done(((bf16[832,1024]{1,0:T(8,128)(2,1)}), bf16[832,4096]{1,0:T(8,128)(2,1)}) %all-gather.8.cloned.1.call-update) | async-done | bytes 6815760 | tf_op jit(solution)/shard_map/all_gather | solution.py:127
  204.4 6.8 %convolution_convert_fusion = bf16[256,4096]{1,0:T(8,128)(2,1)} fusion(bf16[256,832]{1,0:T(8,128)(2,1)S(1)} %bitcast.73, bf16[832,4096]{1,0:T(8,128)(2,1)} %all-gather.8.cloned.1.call-done), kind=kOutput, calls=%fused_computation.24 | convolution fusion | flops 1745879040 | bytes 9338880 | tf_op jit(solution)/shard_map/dot_general | solution.py:125
  211.5 35.4 %reduce-scatter.5.cloned.1.call-done = bf16[32,4096]{1,0:T(8,128)(2,1)} async-done(((bf16[256,4096]{1,0:T(8,128)(2,1)}), bf16[32,4096]{1,0:T(8,128)(2,1)}) %reduce-scatter.5.cloned.1.call-update) | async-done | bytes 262160 | tf_op jit(solution)/shard_map/reduce_scatter | solution.py:132
  247.0 1.2 convolution_convert_fusion.1
  248.5 27.3 %all_to_all.22 = bf16[32,2,4096]{2,1,0:T(2,128)(2,1)S(1)} all-to-all(bf16[32,2,4096]{2,1,0:T(2,128)(2,1)S(1)} %reshape.307), channel_id=1, replica_groups=mesh['tx'=4,'tz'=8,'hy'=4,'hc'=2] {'tx','tz'}, dimensions={0} | all-to-all | bytes 1048576 | tf_op jit(solution)/shard_map/all_to_all | solution.py:148
  275.8 1.0 reshape.308
  (67 shorter events, 12.6 us)
Async XLA Ops:
  6.5 37.5 %copy-start = (bf16[3,208,1664]{2,1,0:T(8,128)(2,1)S(1)}, bf16[3,208,1664]{2,1,0:T(8,128)(2,1)}, u32[]{:S(2)}) copy-start(bf16[3,208,1664]{2,1,0:T(8,128)(2,1)} %param.15) | copy-start | bytes 6230020
  6.5 37.5 %all-gather.4.cloned.1.call-start = ((), (), s32[]{:S(2)}) async-start(), calls=%async_computation.4 | async-start | bytes 3833856 | tf_op jit(solution)/shard_map/all_gather | solution.py:69
  11.2 74.7 %all-gather.6.cloned.1.call-start = ((), (), s32[]{:S(2)}) async-start(), calls=%async_computation.6 | async-start | bytes 1916928 | tf_op jit(solution)/shard_map/all_gather | solution.py:128
  12.0 117.8 %reduce-scatter.3.cloned.1.call-start = ((), (), s32[]{:S(2)}) async-start(), calls=%async_computation.5 | async-start | bytes 3833856 | tf_op jit(solution)/shard_map/reduce_scatter | solution.py:109
  49.0 2.8 copy-start.3
  51.8 24.7 %copy-start.2 = (bf16[208,1664]{1,0:T(8,128)(2,1)S(1)}, bf16[208,1664]{1,0:T(8,128)(2,1)}, u32[]{:S(2)}) copy-start(bf16[208,1664]{1,0:T(8,128)(2,1)} %param.16) | copy-start | bytes 2076676
  79.4 6.6 %copy-start.4 = (f32[1664]{0:T(1024)S(1)}, f32[1664]{0:T(1024)}, u32[]{:S(2)}) copy-start(f32[1664]{0:T(1024)} %param.17) | copy-start | bytes 19972
  79.4 50.4 %copy-start.1 = (bf16[128,1664]{1,0:T(8,128)(2,1)S(1)}, bf16[128,1664]{1,0:T(8,128)(2,1)}, u32[]{:S(2)}) copy-start(bf16[128,1664]{1,0:T(8,128)(2,1)} %param.13) | copy-start | bytes 1277956
  79.5 125.0 %all-gather.8.cloned.1.call-start = ((), (), s32[]{:S(2)}) async-start(), calls=%async_computation.7 | async-start | bytes 8519680 | tf_op jit(solution)/shard_map/all_gather | solution.py:127
  86.0 161.0 %reduce-scatter.5.cloned.1.call-start = ((), (), s32[]{:S(2)}) async-start(), calls=%async_computation.8 | async-start | bytes 2359296 | tf_op jit(solution)/shard_map/reduce_scatter | solution.py:132
  204.4 6.8 %copy-start.5 = (s32[32,1]{0,1:T(1,128)S(1)}, s32[32,1]{0,1:T(1,128)}, u32[]{:S(2)}) copy-start(s32[32,1]{0,1:T(1,128)} %param.23) | copy-start | bytes 388
Sparse Core Ops, SparseCore 0:
  11.3 32.6 all-gather.3
  45.8 40.0 all-gather.5
  88.5 41.2 reduce-scatter.2
  131.5 72.9 all-gather.7
  211.3 35.5 reduce-scatter.4

commit v3 on v0

--- a/solution.py
+++ b/solution.py
@@ -62,6 +62,7 @@
     col_coord = patch_pos[1].astype(jnp.float32) * SIDE / col_size
     stacked_weight = qkv_weight.reshape(3 * head_width, D)
     normed = layer_norm(tokens.astype(jnp.float32), attn_gain).astype(jnp.bfloat16)
+    full_merge_weight = lax.all_gather(merge_weight, "tok", axis=1, tiled=True)
     projected_rows = lax.dot_general(
         lax.all_gather(normed, "head", axis=0, tiled=True),
         stacked_weight,
@@ -103,12 +104,14 @@
 
     block_starts = jnp.arange(block_count, dtype=jnp.int32) * block_len
     heads_out = lax.map(query_block, block_starts).reshape(group_len, head_width)
-    attn_rows = lax.psum_scatter(
-        jnp.dot(heads_out, out_weight, preferred_element_type=jnp.float32).astype(jnp.bfloat16),
-        "head",
-        scatter_dimension=0,
-        tiled=True,
-    ).astype(jnp.float32)
+    head_count = lax.axis_size("head")
+    head_terms = jnp.dot(heads_out, out_weight, preferred_element_type=jnp.float32).astype(
+        jnp.bfloat16
+    )
+    head_terms = lax.all_to_all(
+        head_terms.reshape(head_count, local_rows, D), "head", split_axis=0, concat_axis=0, tiled=True
+    )
+    attn_rows = jnp.sum(head_terms.astype(jnp.float32), axis=0)
     stream = (tokens.astype(jnp.float32) + attn_rows).reshape(local_rows // 4, 4, D)
     average = jnp.sum(stream, axis=2, keepdims=True) / D
     variance = jnp.sum(stream * stream, axis=2, keepdims=True) / D - average * average
@@ -121,7 +124,7 @@
     merged_count = local_rows // 4
     column_terms = jnp.dot(
         merged_slice,
-        lax.all_gather(merge_weight, "tok", axis=1, tiled=True),
+        full_merge_weight,
         preferred_element_type=jnp.float32,
     )
     projected = lax.psum_scatter(

time: 258 us -> 223 us (0.86)
  waiting for transfers between devices: 146 us -> 103 us
  starting transfers between devices: 0.13 us -> 6.26 us
    all_gather x1, waiting for transfers between devices: 39.1 us -> 0.01 us  [body(): full_merge_weight = lax.all_gather(merge_weight, 'tok', axis=1, tiled=True)]
    all_to_all x0 -> x1, waiting for transfers between devices: none -> 38.5 us  [body(): lax.all_to_all(head_terms.reshape(head_count, local_rows, D), 'head', spl...]
    reduce_scatter x1 -> x0, waiting for transfers between devices: 38.2 us -> none  [body(): lax.psum_scatter(jnp.dot(heads_out, out_weight, preferred_element_type=jn...]
    all_to_all x0 -> x1, starting transfers between devices: none -> 6.21 us  [body(): lax.all_to_all(head_terms.reshape(head_count, local_rows, D), 'head', spl...]
    reduce_scatter x1, waiting for transfers between devices: 39.6 us -> 35.8 us  [body(): lax.psum_scatter(column_terms.astype(jnp.bfloat16), 'head', scatter_dimen...]
  transfers between devices with their start and end apart: 4 -> 4, of which waited for: 4 -> 3; matrix products, arithmetic and copies ran while one was open for 3% -> 19% of each run, Pallas kernels for 0% -> 0%
where the time goes in v3:
time: 223 us; the launch traced here: 222 us
  waiting for transfers between devices  103 us (46%)
  blocking collectives  39.3 us (18%)
  matrix products  31.1 us (14%)
  other arithmetic  17.7 us (8%)
  between operations  13.3 us (6%)
  local copies, waits for them, and re-layouts  7.22 us (3%)
  starting transfers between devices  6.26 us (3%)
  loops' own time  3.85 us (2%)
    all_to_all x1, waiting for transfers between devices, body(): lax.all_to_all(head_terms.reshape(head_count, local_rows, D), 'head', spl...  38.5 us
    reduce_scatter x1, waiting for transfers between devices, body(): lax.psum_scatter(column_terms.astype(jnp.bfloat16), 'head', scatter_dimen...  35.8 us
    all_gather x1, waiting for transfers between devices, body(): lax.all_gather(normed, 'head', axis=0, tiled=True)  28.1 us
    all_to_all x1, blocking collectives, body(): lax.all_to_all(send_rows, 'tok', split_axis=0, concat_axis=0, tiled=True)  27.3 us
    all_to_all x1, blocking collectives, body(): lax.all_to_all(window_rows.reshape(local_rows // 4, 4 * D), 'head', split...  12 us
    sub x2, matrix products, query_block(): exponent = jnp.where(allowed[None], jnp.exp(masked - row_top), 0.0)  9.3 us
    dot_general x1, matrix products, body(): jnp.dot(merged_slice, full_merge_weight, preferred_element_type=jnp.float32)  6.76 us
    dot_general x2, matrix products, query_block(): jnp.einsum('hqk,khd->qhd', exponent.astype(jnp.bfloat16), value_all, pref...  6.31 us
  transfers between devices with their start and end apart: 4, of which 3 were waited for; matrix products, arithmetic and copies ran while one was open for 19% of the time, Pallas kernels for 0%

profile of v3, /device:TPU:57, one launch (start us, length us, event | category | flops | bytes accessed | tf_op | source)
XLA Modules:
  0.0 221.9 jit_solution(6995561589576105391)
XLA Ops:
  6.5 1.3 convert_reduce_fusion.1
  7.8 1.3 fusion.46
  9.1 2.1 fusion.48
  15.0 1.0 multiply_cosine_fusion.1
  16.0 28.1 %all-gather.3.cloned.1.call-done = bf16[1024,1664]{1,0:T(8,128)(2,1)} async-done(((bf16[128,1664]{1,0:T(8,128)(2,1)}), bf16[1024,1664]{1,0:T(8,128)(2,1)}) %all-gather.3.cloned.1.call-update) | async-done | bytes 3407888 | tf_op jit(solution)/shard_map/all_gather | solution.py:67
  44.1 4.5 %fusion.39 = f32[1024,3,2,104]{0,3,2,1:T(8,128)S(1)} fusion(bf16[3,2,104,1664]{3,2,1,0:T(8,128)(2,1)S(1)} %bitcast.71, bf16[1024,1664]{1,0:T(8,128)(2,1)} %all-gather.3.cloned.1.call-done), kind=kOutput, calls=%fused_computation.28 | convolution fusion | flops 2126512128 | bytes 8040448 | tf_op jit(solution)/shard_map/dot_general | solution.py:66
  51.8 23.5 %while.10 = (s32[]{:T(128)}, bf16[2,512,2,104]{1,3,2,0:T(8,128)(2,1)}, s32[2]{0:T(128)S(1)}, s32[1024]{0:T(1024)S(1)}, pred[1024]{0:T(1024)(128)(4,1)S(1)}, /*in...) while((s32[]{:T(128)}, ...), condition=%wide.region_9.10_spmd, body=%wide.region_6.0_spmd.sunk | while | flops 443762176 | bytes 7069351 | solution.py:106
  55.8 4.6 %fusion.81 = (f32[2,512]{1,0:T(2,128)S(1)}, bf16[2,512,1024]{2,1,0:T(8,128)(2,1)}) fusion(pred[512,1024]{1,0:T(8,128)(4,1)S(1)} %fusion.80, bf16[1024,2,104]{0,2,1:T(8,128)(2,1)} %get-tuple-element.180, bf16[1024,2,104]{0,2,1:T(8,128)(2,1)} %get-tuple-element.179, s32[]{:T(128)S(6)} %select_n.34), kind=kOutput, calls=%fused_computation.85.clone.1 | convolution fusion | flops 223347712 | bytes 3788804 | tf_op jit(solution)/shard_map/while/body/eval_jaxpr/sub | solution.py:95
  60.4 3.2 %fusion.82 = bf16[2,512,2,104]{1,3,2,0:T(8,128)(2,1)} fusion(bf16[2,512,2,104]{1,3,2,0:T(8,128)(2,1)} %get-tuple-element.164, s32[]{:T(128)} %get-tuple-element.163, bf16[1024,2,104]{0,2,1:T(8,128)(2,1)} %get-tuple-element.181, bf16[2,512,1024]{2,1,0:T(8,128)(2,1)} %get-tuple-element.150, f32[512,2]{0,1:T(2,128)S(1)} %bitcast.82), kind=kOutput, calls=%fused_computation.15.clone.1 | convolution fusion | flops 218316800 | bytes 2740736 | tf_op jit(solution)/shard_map/while/body/eval_jaxpr/hqk,khd->qhd/dot_general | solution.py:97
  67.5 4.7 %fusion.81 = (f32[2,512]{1,0:T(2,128)S(1)}, bf16[2,512,1024]{2,1,0:T(8,128)(2,1)}) fusion(pred[512,1024]{1,0:T(8,128)(4,1)S(1)} %fusion.80, bf16[1024,2,104]{0,2,1:T(8,128)(2,1)} %get-tuple-element.180, bf16[1024,2,104]{0,2,1:T(8,128)(2,1)} %get-tuple-element.179, s32[]{:T(128)S(6)} %select_n.34), kind=kOutput, calls=%fused_computation.85.clone.1 | convolution fusion | flops 223347712 | bytes 3788804 | tf_op jit(solution)/shard_map/while/body/eval_jaxpr/sub | solution.py:95
  72.2 3.1 %fusion.82 = bf16[2,512,2,104]{1,3,2,0:T(8,128)(2,1)} fusion(bf16[2,512,2,104]{1,3,2,0:T(8,128)(2,1)} %get-tuple-element.164, s32[]{:T(128)} %get-tuple-element.163, bf16[1024,2,104]{0,2,1:T(8,128)(2,1)} %get-tuple-element.181, bf16[2,512,1024]{2,1,0:T(8,128)(2,1)} %get-tuple-element.150, f32[512,2]{0,1:T(2,128)S(1)} %bitcast.82), kind=kOutput, calls=%fused_computation.15.clone.1 | convolution fusion | flops 218316800 | bytes 2740736 | tf_op jit(solution)/shard_map/while/body/eval_jaxpr/hqk,khd->qhd/dot_general | solution.py:97
  75.3 1.4 copy.16
  76.9 3.0 %convolution_convert_fusion.2 = bf16[1024,1664]{1,0:T(8,128)(2,1)} fusion(bf16[1024,208]{0,1:T(8,128)(2,1)S(1)} %bitcast.73, bf16[208,1664]{1,0:T(8,128)(2,1)S(1)} %copy-done.2), kind=kOutput, calls=%fused_computation.27 | convolution fusion | flops 710541312 | bytes 4526080 | tf_op jit(solution)/shard_map/dot_general | solution.py:108
  79.9 6.2 %all-to-all-start = ((bf16[8,128,1664]{2,1,0:T(8,128)(2,1)}), bf16[8,128,1664]{2,1,0:T(8,128)(2,1)}, u32[]{:S(2)}, u32[]{:S(2)}) async-start(bf16[8,128,1664]{2,1,0:T(8,128)(2,1)} %bitcast.72), calls=%async_computation | async-start | bytes 6815744 | tf_op jit(solution)/shard_map/all_to_all | solution.py:111
  86.2 38.5 %all-to-all-done = bf16[8,128,1664]{2,1,0:T(8,128)(2,1)} async-done(((bf16[8,128,1664]{2,1,0:T(8,128)(2,1)}), bf16[8,128,1664]{2,1,0:T(8,128)(2,1)}, u32[]{:S(2)}, u32[]{:S(2)}) %all-to-all-start) | async-done | bytes 3407904 | tf_op jit(solution)/shard_map/all_to_all | solution.py:111
  124.7 2.5 %convert_reduce_fusion = f32[128,1664]{1,0:T(8,128)S(1)} fusion(bf16[8,128,1664]{2,1,0:T(8,128)(2,1)} %all-to-all-done), kind=kLoop, calls=%fused_computation.24 | loop fusion | flops 3194880 | bytes 4259840 | tf_op jit(solution)/shard_map/reduce_sum | solution.py:114
  127.3 1.1 fusion.53
  128.7 1.4 reshape.310
  130.5 12.0 %all_to_all.26 = bf16[32,8,832]{2,0,1:T(8,128)(2,1)S(1)} all-to-all(bf16[32,8,832]{2,0,1:T(8,128)(2,1)S(1)} %fusion.45), channel_id=1, replica_groups=mesh['tok'=32,'head'=8] {'head'}, dimensions={1} | all-to-all | bytes 851968 | tf_op jit(solution)/shard_map/all_to_all | solution.py:121
  142.5 6.8 %convolution_convert_fusion = bf16[256,4096]{1,0:T(8,128)(2,1)} fusion(bf16[256,832]{1,0:T(8,128)(2,1)S(1)} %bitcast.75, bf16[832,4096]{1,0:T(8,128)(2,1)} %all-gather.5.cloned.1.call-done), kind=kOutput, calls=%fused_computation.25 | convolution fusion | flops 1745879040 | bytes 9338880 | tf_op jit(solution)/shard_map/dot_general | solution.py:125
  149.7 35.8 %reduce-scatter.2.cloned.1.call-done = bf16[32,4096]{1,0:T(8,128)(2,1)} async-done(((bf16[256,4096]{1,0:T(8,128)(2,1)}), bf16[32,4096]{1,0:T(8,128)(2,1)}) %reduce-scatter.2.cloned.1.call-update) | async-done | bytes 262160 | tf_op jit(solution)/shard_map/reduce_scatter | solution.py:130
  185.5 1.2 convolution_convert_fusion.1
  187.0 27.3 %all_to_all.27 = bf16[32,2,4096]{2,1,0:T(2,128)(2,1)S(1)} all-to-all(bf16[32,2,4096]{2,1,0:T(2,128)(2,1)S(1)} %reshape.311), channel_id=1, replica_groups=mesh['tok'=32,'head'=8] {'tok'}, dimensions={0} | all-to-all | bytes 1048576 | tf_op jit(solution)/shard_map/all_to_all | solution.py:146
  214.4 1.0 reshape.312
  (64 shorter events, 12.6 us)
Async XLA Ops:
  6.5 37.5 %copy-start = (bf16[3,208,1664]{2,1,0:T(8,128)(2,1)S(1)}, bf16[3,208,1664]{2,1,0:T(8,128)(2,1)}, u32[]{:S(2)}) copy-start(bf16[3,208,1664]{2,1,0:T(8,128)(2,1)} %param.15) | copy-start | bytes 6230020
  6.5 37.5 %all-gather.3.cloned.1.call-start = ((), (), s32[]{:S(2)}) async-start(), calls=%async_computation.4 | async-start | bytes 3833856 | tf_op jit(solution)/shard_map/all_gather | solution.py:67
  11.2 131.3 %all-gather.5.cloned.1.call-start = ((), (), s32[]{:S(2)}) async-start(), calls=%async_computation.5 | async-start | bytes 7028736 | tf_op jit(solution)/shard_map/all_gather | solution.py:65
  49.0 2.9 %copy-start.3 = (s32[1024]{0:T(1024)S(1)}, s32[1024]{0:T(1024)}, u32[]{:S(2)}) copy-start(s32[1024]{0:T(1024)} %param.20) | copy-start | bytes 12292
  51.8 25.0 %copy-start.2 = (bf16[208,1664]{1,0:T(8,128)(2,1)S(1)}, bf16[208,1664]{1,0:T(8,128)(2,1)}, u32[]{:S(2)}) copy-start(bf16[208,1664]{1,0:T(8,128)(2,1)} %param.16) | copy-start | bytes 2076676
  79.9 6.2 %copy-start.4 = (f32[1664]{0:T(1024)S(1)}, f32[1664]{0:T(1024)}, u32[]{:S(2)}) copy-start(f32[1664]{0:T(1024)} %param.17) | copy-start | bytes 19972
  79.9 44.9 %all-to-all-start = ((bf16[8,128,1664]{2,1,0:T(8,128)(2,1)}), bf16[8,128,1664]{2,1,0:T(8,128)(2,1)}, u32[]{:S(2)}, u32[]{:S(2)}) async-start(bf16[8,128,1664]{2,1,0:T(8,128)(2,1)} %bitcast.72), calls=%async_computation | async-start | bytes 6815744 | tf_op jit(solution)/shard_map/all_to_all | solution.py:111
  86.1 41.2 %copy-start.1 = (bf16[128,1664]{1,0:T(8,128)(2,1)S(1)}, bf16[128,1664]{1,0:T(8,128)(2,1)}, u32[]{:S(2)}) copy-start(bf16[128,1664]{1,0:T(8,128)(2,1)} %param.13) | copy-start | bytes 1277956
  86.1 99.4 %reduce-scatter.2.cloned.1.call-start = ((), (), s32[]{:S(2)}) async-start(), calls=%async_computation.6 | async-start | bytes 2359296 | tf_op jit(solution)/shard_map/reduce_scatter | solution.py:130
  142.5 6.8 %copy-start.5 = (s32[32,1]{0,1:T(1,128)S(1)}, s32[32,1]{0,1:T(1,128)}, u32[]{:S(2)}) copy-start(s32[32,1]{0,1:T(1,128)} %param.23) | copy-start | bytes 388
Sparse Core Ops, SparseCore 0:
  11.3 32.6 all-gather.2
  46.5 90.8 all-gather.4
  149.4 35.9 reduce-scatter.1

commit v4 on v3

--- a/solution.py
+++ b/solution.py
@@ -6,6 +6,7 @@
 D = 1664
 HD = 104
 SIDE = 16
+QUERY_PARTS = 2
 
 
 EPSILON = 1e-06
@@ -75,20 +76,22 @@
     )
     key_all = rotate(projected_rows[:, 1], row_coord, col_coord).astype(jnp.bfloat16)
     value_all = projected_rows[:, 2].astype(jnp.bfloat16)
-    block_len = min(512, group_len)
-    block_count = group_len // block_len
     key_live = live_mask == 1
 
-    def allowed_pairs(query_start, span):
-        query_seg = lax.dynamic_slice_in_dim(segment_ids, query_start, block_len)
-        query_place = query_start + jnp.arange(block_len, dtype=jnp.int32)
-        key_place = jnp.arange(span, dtype=jnp.int32)
+    head_count = lax.axis_size("head")
+    key_live = live_mask == 1
+    part_rows = local_rows // QUERY_PARTS
+    attn_parts = []
+    for part in range(QUERY_PARTS):
+        picked = lambda values: values.reshape(
+            (head_count, QUERY_PARTS, part_rows) + values.shape[1:]
+        )[:, part].reshape((head_count * part_rows,) + values.shape[1:])
+        queries = picked(query_all)
+        query_seg = picked(segment_ids)
+        query_place = picked(jnp.arange(group_len, dtype=jnp.int32))
+        key_place = jnp.arange(group_len, dtype=jnp.int32)
         same_image = query_seg[:, None] == segment_ids[None, :]
-        return same_image & (key_live[None, :] | (query_place[:, None] == key_place[None, :]))
-
-    def query_block(query_start):
-        queries = lax.dynamic_slice_in_dim(query_all, query_start, block_len, 0)
-        allowed = allowed_pairs(query_start, group_len)
+        allowed = same_image & (key_live[None, :] | (query_place[:, None] == key_place[None, :]))
         scores = jnp.einsum("qhd,khd->hqk", queries, key_all, preferred_element_type=jnp.float32)
         masked = jnp.where(allowed[None], scores, NEGATIVE)
         row_top = jnp.max(masked, axis=2, keepdims=True)
@@ -100,18 +103,17 @@
             value_all,
             preferred_element_type=jnp.float32,
         )
-        return (numerator / denominator.T[:, :, None]).astype(jnp.bfloat16)
-
-    block_starts = jnp.arange(block_count, dtype=jnp.int32) * block_len
-    heads_out = lax.map(query_block, block_starts).reshape(group_len, head_width)
-    head_count = lax.axis_size("head")
-    head_terms = jnp.dot(heads_out, out_weight, preferred_element_type=jnp.float32).astype(
-        jnp.bfloat16
-    )
-    head_terms = lax.all_to_all(
-        head_terms.reshape(head_count, local_rows, D), "head", split_axis=0, concat_axis=0, tiled=True
-    )
-    attn_rows = jnp.sum(head_terms.astype(jnp.float32), axis=0)
+        part_out = (numerator / denominator.T[:, :, None]).astype(jnp.bfloat16)
+        part_terms = jnp.dot(
+            part_out.reshape(head_count * part_rows, head_width),
+            out_weight,
+            preferred_element_type=jnp.float32,
+        ).astype(jnp.bfloat16)
+        part_terms = lax.all_to_all(
+            part_terms.reshape(head_count, part_rows, D), "head", split_axis=0, concat_axis=0, tiled=True
+        )
+        attn_parts.append(jnp.sum(part_terms.astype(jnp.float32), axis=0))
+    attn_rows = jnp.concatenate(attn_parts, axis=0)
     stream = (tokens.astype(jnp.float32) + attn_rows).reshape(local_rows // 4, 4, D)
     average = jnp.sum(stream, axis=2, keepdims=True) / D
     variance = jnp.sum(stream * stream, axis=2, keepdims=True) / D - average * average
@@ -127,9 +129,14 @@
         full_merge_weight,
         preferred_element_type=jnp.float32,
     )
-    projected = lax.psum_scatter(
-        column_terms.astype(jnp.bfloat16), "head", scatter_dimension=0, tiled=True
+    column_terms = lax.all_to_all(
+        column_terms.astype(jnp.bfloat16).reshape(head_count, merged_count, -1),
+        "head",
+        split_axis=0,
+        concat_axis=0,
+        tiled=True,
     )
+    projected = jnp.sum(column_terms.astype(jnp.float32), axis=0).astype(jnp.bfloat16)
     slot_count = max(2, 2 * merged_count // tok_count)
     owner_col = owners[:, 0]
     owner_hot = (owner_col[:, None] == jnp.arange(tok_count, dtype=jnp.int32)[None, :]).astype(

time: 223 us -> 233 us (1.045)
  the two profiles are of different devices: /device:TPU:57 before, /device:TPU:32 now
where the time goes in v4:
time: 233 us; the launch traced here: 232 us
  waiting for transfers between devices  90.1 us (39%)
  blocking collectives  39.1 us (17%)
  matrix products  30.2 us (13%)
  local copies, waits for them, and re-layouts  25 us (11%)
  other arithmetic  19.8 us (8%)
  between operations  13.8 us (6%)
  starting transfers between devices  13.5 us (6%)
    all_to_all x2, waiting for transfers between devices, body(): lax.all_to_all(part_terms.reshape(head_count, part_rows, D), 'head', spli...  33 us
    all_gather x1, waiting for transfers between devices, body(): lax.all_gather(normed, 'head', axis=0, tiled=True)  29.6 us
    all_to_all x1, blocking collectives, body(): lax.all_to_all(send_rows, 'tok', split_axis=0, concat_axis=0, tiled=True)  27.1 us
    all_to_all x1, waiting for transfers between devices, body(): lax.all_to_all(column_terms.astype(jnp.bfloat16).reshape(head_count, merg...  26.8 us
    all_to_all x1, blocking collectives, body(): lax.all_to_all(window_rows.reshape(local_rows // 4, 4 * D), 'head', split...  12 us
    sub x2, matrix products, body(): exponent = jnp.where(allowed[None], jnp.exp(masked - row_top), 0.0)  9.51 us
    all_to_all x2, starting transfers between devices, body(): lax.all_to_all(part_terms.reshape(head_count, part_rows, D), 'head', spli...  8.95 us
    concatenate x4, local copies, waits for them, and re-layouts, rotate(): return jnp.concatenate(pieces, axis=-1)  7.59 us
  transfers between devices with their start and end apart: 5, of which 4 were waited for; matrix products, arithmetic and copies ran while one was open for 26% of the time, Pallas kernels for 0%

profile of v4, /device:TPU:32, one launch (start us, length us, event | category | flops | bytes accessed | tf_op | source)
XLA Modules:
  0.0 231.6 jit_solution(11975675755944856119)
XLA Ops:
  9.2 2.1 fusion.48
  13.7 2.1 fusion.17
  15.8 29.6 %all-gather.3.cloned.1.call-done = bf16[1024,1664]{1,0:T(8,128)(2,1)} async-done(((bf16[128,1664]{1,0:T(8,128)(2,1)}), bf16[1024,1664]{1,0:T(8,128)(2,1)}) %all-gather.3.cloned.1.call-update) | async-done | bytes 3407888 | tf_op jit(solution)/shard_map/all_gather | solution.py:68
  45.4 4.5 %fusion.4 = f32[1024,3,2,104]{0,3,2,1:T(8,128)S(1)} fusion(bf16[3,2,104,1664]{3,2,1,0:T(8,128)(2,1)S(1)} %bitcast.70, bf16[1024,1664]{1,0:T(8,128)(2,1)} %all-gather.3.cloned.1.call-done), kind=kOutput, calls=%fused_computation.10 | convolution fusion | flops 2126512128 | bytes 8040448 | tf_op jit(solution)/shard_map/dot_general | solution.py:67
  55.7 2.1 concatenate.20
  59.6 2.1 concatenate.21
  63.5 2.1 concatenate.22
  65.6 2.4 %fusion.22 = bf16[8,2,64,2,104]{2,1,0,3,4:T(2,128)(2,1)S(1)} fusion(f32[8,2,64,2,26]{2,1,0,3,4:T(2,128)} %concatenate.22, f32[8,2,64,2,26]{2,1,0,3,4:T(2,128)} %concatenate.21, f32[8,2,64,2,26]{2,1,0,3,4:T(2,128)} %concatenate.20, f32[8,2,64,2,26]{2,1,0,3,4:T(2,128)S(1)} %concatenate.19), kind=kLoop, calls=%fused_computation.31 | loop fusion | flops 1064960 | bytes 1277952 | tf_op jit(solution)/shard_map/convert_element_type | solution.py:74
  68.0 2.4 %fusion.61 = (bf16[8,1,64,2,104]{2,1,0,3,4:T(2,128)(2,1)}, bf16[8,1,64,2,104]{2,1,0,3,4:T(2,128)(2,1)}) fusion(bf16[8,2,64,2,104]{2,1,0,3,4:T(2,128)(2,1)S(1)} %fusion.22), kind=kLoop, calls=%fused_computation.99 | loop fusion | bytes 851968 | tf_op jit(solution)/shard_map/slice | solution.py:86
  70.4 2.9 %copy.27 = bf16[8,1,64,2,104]{4,2,0,3,1:T(8,128)(2,1)} copy(bf16[8,1,64,2,104]{2,1,0,3,4:T(2,128)(2,1)} %get-tuple-element.24) | data formatting | bytes 425984 | tf_op jit(solution)/shard_map/slice | solution.py:86
  74.2 4.9 %fusion.63 = (f32[2,512]{1,0:T(2,128)S(1)}, bf16[2,512,1024]{2,1,0:T(8,128)(2,1)}) fusion(pred[512,1024]{1,0:T(8,128)(4,1)} %get-tuple-element.32, bf16[512,2,104]{2,0,1:T(8,128)(2,1)} %bitcast.75, bf16[1024,2,26]{0,2,1:T(8,128)(2,1)} %get-tuple-element.26, bf16[1024,2,26]{0,2,1:T(8,128)(2,1)} %get-tuple-element.27, ...), kind=kOutput, calls=%fused_computation.101 | convolution fusion | flops 225051648 | bytes 3264512 | tf_op jit(solution)/shard_map/sub | solution.py:98
  79.2 2.7 %fusion.38 = bf16[512,2,104]{0,2,1:T(8,128)(2,1)S(1)} fusion(bf16[2,512,1024]{2,1,0:T(8,128)(2,1)} %get-tuple-element.45, f32[512,2]{0,1:T(2,128)S(1)} %bitcast.86, f32[1024,3,2,104]{0,3,2,1:T(8,128)} %copy-done.11), kind=kOutput, calls=%fused_computation.40 | convolution fusion | flops 218316800 | bytes 2740224 | tf_op jit(solution)/shard_map/hqk,khd->qhd/dot_general | solution.py:100
  83.8 4.6 %all-to-all-start = ((bf16[8,64,1664]{2,1,0:T(8,128)(2,1)}), bf16[8,64,1664]{2,1,0:T(8,128)(2,1)}, u32[]{:S(2)}, u32[]{:S(2)}) async-start(bf16[8,64,1664]{2,1,0:T(8,128)(2,1)} %bitcast.71), calls=%async_computation | async-start | bytes 3407872 | tf_op jit(solution)/shard_map/all_to_all | solution.py:112
  90.3 4.6 %fusion.62 = (f32[2,512]{1,0:T(2,128)S(1)}, bf16[2,512,1024]{2,1,0:T(8,128)(2,1)}) fusion(pred[512,1024]{1,0:T(8,128)(4,1)S(1)} %copy-done.12, bf16[512,2,104]{2,0,1:T(8,128)(2,1)} %bitcast.76, bf16[1024,2,26]{0,2,1:T(8,128)(2,1)} %get-tuple-element.26, bf16[1024,2,26]{0,2,1:T(8,128)(2,1)} %get-tuple-element.27, ...), kind=kOutput, calls=%fused_computation.100 | convolution fusion | flops 225051648 | bytes 3264512 | tf_op jit(solution)/shard_map/sub | solution.py:98
  94.8 2.7 %fusion.35 = bf16[512,2,104]{0,2,1:T(8,128)(2,1)S(1)} fusion(bf16[2,512,1024]{2,1,0:T(8,128)(2,1)} %get-tuple-element.43, f32[512,2]{0,1:T(2,128)S(1)} %bitcast.85, f32[1024,3,2,104]{0,3,2,1:T(8,128)} %copy-done.11), kind=kOutput, calls=%fused_computation.39 | convolution fusion | flops 218316800 | bytes 2740224 | tf_op jit(solution)/shard_map/hqk,khd->qhd/dot_general | solution.py:100
  99.4 11.9 %all-to-all-done = bf16[8,64,1664]{2,1,0:T(8,128)(2,1)} async-done(((bf16[8,64,1664]{2,1,0:T(8,128)(2,1)}), bf16[8,64,1664]{2,1,0:T(8,128)(2,1)}, u32[]{:S(2)}, u32[]{:S(2)}) %all-to-all-start) | async-done | bytes 1703968 | tf_op jit(solution)/shard_map/all_to_all | solution.py:112
  111.4 4.3 %all-to-all-start.1 = ((bf16[8,64,1664]{2,1,0:T(8,128)(2,1)}), bf16[8,64,1664]{2,1,0:T(8,128)(2,1)}, u32[]{:S(2)}, u32[]{:S(2)}) async-start(bf16[8,64,1664]{2,1,0:T(8,128)(2,1)} %bitcast.72), calls=%async_computation.1 | async-start | bytes 3407872 | tf_op jit(solution)/shard_map/all_to_all | solution.py:112
  117.6 21.0 %all-to-all-done.1 = bf16[8,64,1664]{2,1,0:T(8,128)(2,1)} async-done(((bf16[8,64,1664]{2,1,0:T(8,128)(2,1)}), bf16[8,64,1664]{2,1,0:T(8,128)(2,1)}, u32[]{:S(2)}, u32[]{:S(2)}) %all-to-all-start.1) | async-done | bytes 1703968 | tf_op jit(solution)/shard_map/all_to_all | solution.py:112
  143.6 12.0 %all_to_all.36 = bf16[32,8,832]{2,0,1:T(8,128)(2,1)S(1)} all-to-all(bf16[32,8,832]{2,0,1:T(8,128)(2,1)S(1)} %fusion.45), channel_id=1, replica_groups=mesh['tok'=32,'head'=8] {'head'}, dimensions={1} | all-to-all | bytes 851968 | tf_op jit(solution)/shard_map/all_to_all | solution.py:123
  155.7 6.8 %convolution_convert_fusion = bf16[256,4096]{1,0:T(8,128)(2,1)} fusion(bf16[256,832]{1,0:T(8,128)(2,1)S(1)} %bitcast.74, bf16[832,4096]{1,0:T(8,128)(2,1)} %all-gather.5.cloned.1.call-done), kind=kOutput, calls=%fused_computation.2 | convolution fusion | flops 1745879040 | bytes 9338880 | tf_op jit(solution)/shard_map/dot_general | solution.py:127
  162.4 4.5 %all-to-all-start.3 = ((bf16[8,32,4096]{2,1,0:T(8,128)(2,1)}), bf16[8,32,4096]{2,1,0:T(8,128)(2,1)}, u32[]{:S(2)}, u32[]{:S(2)}) async-start(bf16[8,32,4096]{2,1,0:T(8,128)(2,1)} %bitcast.73), calls=%async_computation.3 | async-start | bytes 4194304 | tf_op jit(solution)/shard_map/all_to_all | solution.py:132
  167.2 26.8 %all-to-all-done.3 = bf16[8,32,4096]{2,1,0:T(8,128)(2,1)} async-done(((bf16[8,32,4096]{2,1,0:T(8,128)(2,1)}), bf16[8,32,4096]{2,1,0:T(8,128)(2,1)}, u32[]{:S(2)}, u32[]{:S(2)}) %all-to-all-start.3) | async-done | bytes 2097184 | tf_op jit(solution)/shard_map/all_to_all | solution.py:132
  194.1 1.9 reduce_sum.122
  196.6 27.1 %all_to_all.37 = bf16[32,2,4096]{2,1,0:T(2,128)(2,1)S(1)} all-to-all(bf16[32,2,4096]{2,1,0:T(2,128)(2,1)S(1)} %reshape.429), channel_id=1, replica_groups=mesh['tok'=32,'head'=8] {'tok'}, dimensions={0} | all-to-all | bytes 1048576 | tf_op jit(solution)/shard_map/all_to_all | solution.py:153
  (99 shorter events, 29.6 us)
Async XLA Ops:
  6.5 38.9 %copy-start = (bf16[3,208,1664]{2,1,0:T(8,128)(2,1)S(1)}, bf16[3,208,1664]{2,1,0:T(8,128)(2,1)}, u32[]{:S(2)}) copy-start(bf16[3,208,1664]{2,1,0:T(8,128)(2,1)} %param.13) | copy-start | bytes 6230020
  6.5 5.5 %copy-start.18 = (s32[2,4]{1,0:T(2,128)S(1)}, s32[2,4]{1,0:T(2,128)}, u32[]{:S(2)}) copy-start(s32[2,4]{1,0:T(2,128)} %param.17) | copy-start | bytes 100
  6.5 5.5 %copy-start.13 = (s32[1024]{0:T(1024)S(1)}, s32[1024]{0:T(1024)}, u32[]{:S(2)}) copy-start(s32[1024]{0:T(1024)} %param.18) | copy-start | bytes 12292
  6.5 6.1 %copy-start.14 = (s32[2,1024]{1,0:T(2,128)S(1)}, s32[2,1024]{1,0:T(2,128)}, u32[]{:S(2)}) copy-start(s32[2,1024]{1,0:T(2,128)} %param.19) | copy-start | bytes 24580
  6.5 6.1 %copy-start.16 = (s32[1024]{0:T(1024)S(1)}, s32[1024]{0:T(1024)}, u32[]{:S(2)}) copy-start(s32[1024]{0:T(1024)} %param.20) | copy-start | bytes 12292
  6.5 38.9 %all-gather.3.cloned.1.call-start = ((), (), s32[]{:S(2)}) async-start(), calls=%async_computation.5 | async-start | bytes 3833856 | tf_op jit(solution)/shard_map/all_gather | solution.py:68
  11.3 144.4 %all-gather.5.cloned.1.call-start = ((), (), s32[]{:S(2)}) async-start(), calls=%async_computation.6 | async-start | bytes 7028736 | tf_op jit(solution)/shard_map/all_gather | solution.py:66
  13.7 36.4 %copy-start.5 = (f32[1024,26]{0,1:T(8,128)}, f32[1024,26]{0,1:T(8,128)S(1)}, u32[]{:S(2)}) copy-start(f32[1024,26]{0,1:T(8,128)S(1)} %get-tuple-element.35) | copy-start | bytes 319492
  13.7 36.4 %copy-start.7 = (f32[1024,26]{0,1:T(8,128)}, f32[1024,26]{0,1:T(8,128)S(1)}, u32[]{:S(2)}) copy-start(f32[1024,26]{0,1:T(8,128)S(1)} %get-tuple-element.40) | copy-start | bytes 319492
  13.7 36.4 %copy-start.9 = (f32[1024,26]{0,1:T(8,128)}, f32[1024,26]{0,1:T(8,128)S(1)}, u32[]{:S(2)}) copy-start(f32[1024,26]{0,1:T(8,128)S(1)} %get-tuple-element.41) | copy-start | bytes 319492
  49.9 1.8 copy-start.11
  68.0 5.3 %copy-start.6 = (f32[1024,26]{0,1:T(8,128)S(1)}, f32[1024,26]{0,1:T(8,128)}, u32[]{:S(2)}) copy-start(f32[1024,26]{0,1:T(8,128)} %copy-done.5) | copy-start | bytes 319492
  68.0 5.3 %copy-start.8 = (f32[1024,26]{0,1:T(8,128)S(1)}, f32[1024,26]{0,1:T(8,128)}, u32[]{:S(2)}) copy-start(f32[1024,26]{0,1:T(8,128)} %copy-done.7) | copy-start | bytes 319492
  68.0 5.3 %copy-start.10 = (f32[1024,26]{0,1:T(8,128)S(1)}, f32[1024,26]{0,1:T(8,128)}, u32[]{:S(2)}) copy-start(f32[1024,26]{0,1:T(8,128)} %copy-done.9) | copy-start | bytes 319492
  79.2 2.7 %copy-start.3 = (bf16[208,1664]{1,0:T(8,128)(2,1)S(1)}, bf16[208,1664]{1,0:T(8,128)(2,1)}, u32[]{:S(2)}) copy-start(bf16[208,1664]{1,0:T(8,128)(2,1)} %param.14) | copy-start | bytes 2076676
  83.8 4.6 %copy-start.2 = (bf16[8,1,64,2,104]{2,1,0,3,4:T(2,128)(2,1)S(1)}, bf16[8,1,64,2,104]{2,1,0,3,4:T(2,128)(2,1)}, u32[]{:S(2)}) copy-start(bf16[8,1,64,2,104]{2,1,0,3,4:T(2,128)(2,1)} %get-tuple-element.25) | copy-start | bytes 638980
  83.8 6.5 %copy-start.12 = (pred[512,1024]{1,0:T(8,128)(4,1)S(1)}, pred[512,1024]{1,0:T(8,128)(4,1)}, u32[]{:S(2)}) copy-start(pred[512,1024]{1,0:T(8,128)(4,1)} %get-tuple-element.33) | copy-start | bytes 1572868
  83.8 27.6 %all-to-all-start = ((bf16[8,64,1664]{2,1,0:T(8,128)(2,1)}), bf16[8,64,1664]{2,1,0:T(8,128)(2,1)}, u32[]{:S(2)}, u32[]{:S(2)}) async-start(bf16[8,64,1664]{2,1,0:T(8,128)(2,1)} %bitcast.71), calls=%async_computation | async-start | bytes 3407872 | tf_op jit(solution)/shard_map/all_to_all | solution.py:112
  94.8 2.7 %copy-start.4 = (bf16[208,1664]{1,0:T(8,128)(2,1)S(1)}, bf16[208,1664]{1,0:T(8,128)(2,1)}, u32[]{:S(2)}) copy-start(bf16[208,1664]{1,0:T(8,128)(2,1)} %param.14) | copy-start | bytes 2076676
  99.4 16.3 %copy-start.15 = (f32[1664]{0:T(1024)S(1)}, f32[1664]{0:T(1024)}, u32[]{:S(2)}) copy-start(f32[1664]{0:T(1024)} %param.15) | copy-start | bytes 19972
  111.4 27.3 %all-to-all-start.1 = ((bf16[8,64,1664]{2,1,0:T(8,128)(2,1)}), bf16[8,64,1664]{2,1,0:T(8,128)(2,1)}, u32[]{:S(2)}, u32[]{:S(2)}) async-start(bf16[8,64,1664]{2,1,0:T(8,128)(2,1)} %bitcast.72), calls=%async_computation.1 | async-start | bytes 3407872 | tf_op jit(solution)/shard_map/all_to_all | solution.py:112
  115.8 24.6 %copy-start.1 = (bf16[128,1664]{1,0:T(8,128)(2,1)S(1)}, bf16[128,1664]{1,0:T(8,128)(2,1)}, u32[]{:S(2)}) copy-start(bf16[128,1664]{1,0:T(8,128)(2,1)} %param.11) | copy-start | bytes 1277956
  162.4 4.5 %copy-start.17 = (s32[32,1]{0,1:T(1,128)S(1)}, s32[32,1]{0,1:T(1,128)}, u32[]{:S(2)}) copy-start(s32[32,1]{0,1:T(1,128)} %param.21) | copy-start | bytes 388
  162.4 31.6 %all-to-all-start.3 = ((bf16[8,32,4096]{2,1,0:T(8,128)(2,1)}), bf16[8,32,4096]{2,1,0:T(8,128)(2,1)}, u32[]{:S(2)}, u32[]{:S(2)}) async-start(bf16[8,32,4096]{2,1,0:T(8,128)(2,1)} %bitcast.73), calls=%async_computation.3 | async-start | bytes 4194304 | tf_op jit(solution)/shard_map/all_to_all | solution.py:132
Sparse Core Ops, SparseCore 0:
  11.4 33.9 all-gather.2
  47.9 94.6 all-gather.4

commit v5 on v3

--- a/solution.py
+++ b/solution.py
@@ -75,7 +75,7 @@
     )
     key_all = rotate(projected_rows[:, 1], row_coord, col_coord).astype(jnp.bfloat16)
     value_all = projected_rows[:, 2].astype(jnp.bfloat16)
-    block_len = min(512, group_len)
+    block_len = min(1024, group_len)
     block_count = group_len // block_len
     key_live = live_mask == 1
 
@@ -127,9 +127,14 @@
         full_merge_weight,
         preferred_element_type=jnp.float32,
     )
-    projected = lax.psum_scatter(
-        column_terms.astype(jnp.bfloat16), "head", scatter_dimension=0, tiled=True
+    column_terms = lax.all_to_all(
+        column_terms.astype(jnp.bfloat16).reshape(head_count, merged_count, -1),
+        "head",
+        split_axis=0,
+        concat_axis=0,
+        tiled=True,
     )
+    projected = jnp.sum(column_terms.astype(jnp.float32), axis=0).astype(jnp.bfloat16)
     slot_count = max(2, 2 * merged_count // tok_count)
     owner_col = owners[:, 0]
     owner_hot = (owner_col[:, None] == jnp.arange(tok_count, dtype=jnp.int32)[None, :]).astype(

time: 223 us -> 218 us (0.978)
  the two profiles are of different devices: /device:TPU:57 before, /device:TPU:32 now
where the time goes in v5:
time: 218 us; the launch traced here: 217 us
  waiting for transfers between devices  107 us (49%)
  blocking collectives  37.4 us (17%)
  matrix products  26.2 us (12%)
  other arithmetic  20.4 us (9%)
  between operations  13.6 us (6%)
  starting transfers between devices  9.33 us (4%)
  local copies, waits for them, and re-layouts  3.41 us (2%)
    all_to_all x1, waiting for transfers between devices, body(): lax.all_to_all(head_terms.reshape(head_count, local_rows, D), 'head', spl...  40.9 us
    all_to_all x1, waiting for transfers between devices, body(): lax.all_to_all(column_terms.astype(jnp.bfloat16).reshape(head_count, merg...  26.9 us
    all_gather x1, waiting for transfers between devices, body(): lax.all_gather(normed, 'head', axis=0, tiled=True)  26.2 us
    all_to_all x1, blocking collectives, body(): lax.all_to_all(send_rows, 'tok', split_axis=0, concat_axis=0, tiled=True)  25.4 us
    all_to_all x1, blocking collectives, body(): lax.all_to_all(window_rows.reshape(local_rows // 4, 4 * D), 'head', split...  12 us
    all_gather x1, waiting for transfers between devices, body(): full_merge_weight = lax.all_gather(merge_weight, 'tok', axis=1, tiled=True)  11.9 us
    sub x1, matrix products, query_block(): exponent = jnp.where(allowed[None], jnp.exp(masked - row_top), 0.0)  8.41 us
    dot_general x1, matrix products, body(): jnp.dot(merged_slice, full_merge_weight, preferred_element_type=jnp.float32)  6.74 us
  transfers between devices with their start and end apart: 4, of which 4 were waited for; matrix products, arithmetic and copies ran while one was open for 16% of the time, Pallas kernels for 0%

profile of v5, /device:TPU:32, one launch (start us, length us, event | category | flops | bytes accessed | tf_op | source)
XLA Modules:
  0.0 217.0 jit_solution(12523833280399862380)
XLA Ops:
  6.5 1.3 convert_reduce_fusion.1
  7.8 1.3 fusion.28
  9.1 2.1 fusion.30
  15.0 1.0 multiply_cosine_fusion.1
  16.0 3.1 %fusion.8 = pred[1024,1024]{0,1:T(8,128)(4,1)} fusion(s32[1024]{0:T(1024)} %param.18, pred[1024]{0:T(1024)(128)(4,1)S(1)} %broadcast_compare_fusion), kind=kLoop, calls=%fused_computation.12 | loop fusion | flops 4194304 | bytes 1053696 | tf_op jit(solution)/shard_map/while/body/eval_jaxpr/and | solution.py:87
  19.1 26.2 %all-gather.3.cloned.1.call-done = bf16[1024,1664]{1,0:T(8,128)(2,1)} async-done(((bf16[128,1664]{1,0:T(8,128)(2,1)}), bf16[1024,1664]{1,0:T(8,128)(2,1)}) %all-gather.3.cloned.1.call-update) | async-done | bytes 3407888 | tf_op jit(solution)/shard_map/all_gather | solution.py:67
  45.3 4.5 %fusion.10 = f32[1024,3,2,104]{0,3,2,1:T(8,128)S(1)} fusion(bf16[3,2,104,1664]{3,2,1,0:T(8,128)(2,1)S(1)} %bitcast.43, bf16[1024,1664]{1,0:T(8,128)(2,1)} %all-gather.3.cloned.1.call-done), kind=kOutput, calls=%fused_computation.15 | convolution fusion | flops 2126512128 | bytes 8040448 | tf_op jit(solution)/shard_map/dot_general | solution.py:66
  50.0 1.4 subtract_convert_fusion.1
  52.3 8.4 %fusion.47 = (f32[2,1024]{1,0:T(2,128)S(1)}, bf16[2,1024,1024]{1,2,0:T(8,128)(2,1)}) fusion(pred[1024,1024]{0,1:T(8,128)(4,1)} %fusion.8, bf16[1024,2,26]{0,2,1:T(8,128)(2,1)} %get-tuple-element.43, bf16[1024,2,26]{0,2,1:T(8,128)(2,1)} %get-tuple-element.44, bf16[1024,2,26]{0,2,1:T(8,128)(2,1)} %get-tuple-element.38, ...), kind=kOutput, calls=%fused_computation.79 | convolution fusion | flops 449463296 | bytes 6529024 | tf_op jit(solution)/shard_map/while/body/eval_jaxpr/sub | solution.py:95
  60.8 3.3 %fusion.18 = bf16[1024,2,104]{0,2,1:T(8,128)(2,1)S(1)} fusion(bf16[2,1024,1024]{1,2,0:T(8,128)(2,1)} %get-tuple-element.56, f32[1024,3,2,104]{0,3,2,1:T(8,128)} %copy-done.2, f32[1024,2]{0,1:T(2,128)S(1)} %bitcast.54), kind=kOutput, calls=%fused_computation.22 | convolution fusion | flops 436633600 | bytes 5054464 | tf_op jit(solution)/shard_map/while/body/eval_jaxpr/hqk,khd->qhd/dot_general | solution.py:97
  64.1 3.0 %convolution_convert_fusion.2 = bf16[1024,1664]{1,0:T(8,128)(2,1)} fusion(bf16[1024,208]{0,1:T(8,128)(2,1)S(1)} %bitcast.46, bf16[208,1664]{1,0:T(8,128)(2,1)S(1)} %copy-done.3), kind=kOutput, calls=%fused_computation.14 | convolution fusion | flops 710541312 | bytes 4526080 | tf_op jit(solution)/shard_map/dot_general | solution.py:108
  67.1 4.8 %all-to-all-start = ((bf16[8,128,1664]{2,1,0:T(8,128)(2,1)}), bf16[8,128,1664]{2,1,0:T(8,128)(2,1)}, u32[]{:S(2)}, u32[]{:S(2)}) async-start(bf16[8,128,1664]{2,1,0:T(8,128)(2,1)} %bitcast.44), calls=%async_computation | async-start | bytes 6815744 | tf_op jit(solution)/shard_map/all_to_all | solution.py:111
  72.0 40.9 %all-to-all-done = bf16[8,128,1664]{2,1,0:T(8,128)(2,1)} async-done(((bf16[8,128,1664]{2,1,0:T(8,128)(2,1)}), bf16[8,128,1664]{2,1,0:T(8,128)(2,1)}, u32[]{:S(2)}, u32[]{:S(2)}) %all-to-all-start) | async-done | bytes 3407904 | tf_op jit(solution)/shard_map/all_to_all | solution.py:111
  112.9 2.6 %convert_reduce_fusion = f32[128,1664]{1,0:T(8,128)S(1)} fusion(bf16[8,128,1664]{2,1,0:T(8,128)(2,1)} %all-to-all-done), kind=kLoop, calls=%fused_computation.4 | loop fusion | flops 3194880 | bytes 4259840 | tf_op jit(solution)/shard_map/reduce_sum | solution.py:114
  115.6 1.1 fusion.46
  117.0 1.4 reshape.308
  118.8 12.0 %all_to_all.31 = bf16[32,8,832]{2,0,1:T(8,128)(2,1)S(1)} all-to-all(bf16[32,8,832]{2,0,1:T(8,128)(2,1)S(1)} %fusion.27), channel_id=1, replica_groups=mesh['tok'=32,'head'=8] {'head'}, dimensions={1} | all-to-all | bytes 851968 | tf_op jit(solution)/shard_map/all_to_all | solution.py:121
  130.8 11.9 %all-gather.5.cloned.1.call-done = bf16[832,4096]{1,0:T(8,128)(2,1)} async-done(((bf16[832,128]{1,0:T(8,128)(2,1)}), bf16[832,4096]{1,0:T(8,128)(2,1)}) %all-gather.5.cloned.1.call-update) | async-done | bytes 6815760 | tf_op jit(solution)/shard_map/all_gather | solution.py:65
  142.7 6.7 %convolution_convert_fusion = bf16[256,4096]{1,0:T(8,128)(2,1)} fusion(bf16[256,832]{1,0:T(8,128)(2,1)S(1)} %bitcast.47, bf16[832,4096]{1,0:T(8,128)(2,1)} %all-gather.5.cloned.1.call-done), kind=kOutput, calls=%fused_computation.5 | convolution fusion | flops 1745879040 | bytes 9338880 | tf_op jit(solution)/shard_map/dot_general | solution.py:125
  149.5 4.5 %all-to-all-start.2 = ((bf16[8,32,4096]{2,1,0:T(8,128)(2,1)}), bf16[8,32,4096]{2,1,0:T(8,128)(2,1)}, u32[]{:S(2)}, u32[]{:S(2)}) async-start(bf16[8,32,4096]{2,1,0:T(8,128)(2,1)} %bitcast.45), calls=%async_computation.2 | async-start | bytes 4194304 | tf_op jit(solution)/shard_map/all_to_all | solution.py:130
  154.3 26.9 %all-to-all-done.2 = bf16[8,32,4096]{2,1,0:T(8,128)(2,1)} async-done(((bf16[8,32,4096]{2,1,0:T(8,128)(2,1)}), bf16[8,32,4096]{2,1,0:T(8,128)(2,1)}, u32[]{:S(2)}, u32[]{:S(2)}) %all-to-all-start.2) | async-done | bytes 2097184 | tf_op jit(solution)/shard_map/all_to_all | solution.py:130
  181.2 1.9 reduce_sum.103
  183.8 25.4 %all_to_all.32 = bf16[32,2,4096]{2,1,0:T(2,128)(2,1)S(1)} all-to-all(bf16[32,2,4096]{2,1,0:T(2,128)(2,1)S(1)} %reshape.310), channel_id=1, replica_groups=mesh['tok'=32,'head'=8] {'tok'}, dimensions={0} | all-to-all | bytes 1048576 | tf_op jit(solution)/shard_map/all_to_all | solution.py:151
  209.1 1.0 reshape.311
  (47 shorter events, 6.6 us)
Async XLA Ops:
  6.5 38.8 %copy-start = (bf16[3,208,1664]{2,1,0:T(8,128)(2,1)S(1)}, bf16[3,208,1664]{2,1,0:T(8,128)(2,1)}, u32[]{:S(2)}) copy-start(bf16[3,208,1664]{2,1,0:T(8,128)(2,1)} %param.13) | copy-start | bytes 6230020
  6.5 38.8 %all-gather.3.cloned.1.call-start = ((), (), s32[]{:S(2)}) async-start(), calls=%async_computation.4 | async-start | bytes 3833856 | tf_op jit(solution)/shard_map/all_gather | solution.py:67
  11.2 131.5 %all-gather.5.cloned.1.call-start = ((), (), s32[]{:S(2)}) async-start(), calls=%async_computation.5 | async-start | bytes 7028736 | tf_op jit(solution)/shard_map/all_gather | solution.py:65
  49.8 2.5 %copy-start.2 = (f32[1024,3,2,104]{0,3,2,1:T(8,128)}, f32[1024,3,2,104]{0,3,2,1:T(8,128)S(1)}, u32[]{:S(2)}) copy-start(f32[1024,3,2,104]{0,3,2,1:T(8,128)S(1)} %fusion.10) | copy-start | bytes 7667716
  60.8 3.3 %copy-start.3 = (bf16[208,1664]{1,0:T(8,128)(2,1)S(1)}, bf16[208,1664]{1,0:T(8,128)(2,1)}, u32[]{:S(2)}) copy-start(bf16[208,1664]{1,0:T(8,128)(2,1)} %param.14) | copy-start | bytes 2076676
  67.1 4.8 %copy-start.4 = (f32[1664]{0:T(1024)S(1)}, f32[1664]{0:T(1024)}, u32[]{:S(2)}) copy-start(f32[1664]{0:T(1024)} %param.15) | copy-start | bytes 19972
  67.1 48.5 %copy-start.1 = (bf16[128,1664]{1,0:T(8,128)(2,1)S(1)}, bf16[128,1664]{1,0:T(8,128)(2,1)}, u32[]{:S(2)}) copy-start(bf16[128,1664]{1,0:T(8,128)(2,1)} %param.11) | copy-start | bytes 1277956
  67.1 45.8 %all-to-all-start = ((bf16[8,128,1664]{2,1,0:T(8,128)(2,1)}), bf16[8,128,1664]{2,1,0:T(8,128)(2,1)}, u32[]{:S(2)}, u32[]{:S(2)}) async-start(bf16[8,128,1664]{2,1,0:T(8,128)(2,1)} %bitcast.44), calls=%async_computation | async-start | bytes 6815744 | tf_op jit(solution)/shard_map/all_to_all | solution.py:111
  149.5 4.5 %copy-start.5 = (s32[32,1]{0,1:T(1,128)S(1)}, s32[32,1]{0,1:T(1,128)}, u32[]{:S(2)}) copy-start(s32[32,1]{0,1:T(1,128)} %param.21) | copy-start | bytes 388
  149.5 31.8 %all-to-all-start.2 = ((bf16[8,32,4096]{2,1,0:T(8,128)(2,1)}), bf16[8,32,4096]{2,1,0:T(8,128)(2,1)}, u32[]{:S(2)}, u32[]{:S(2)}) async-start(bf16[8,32,4096]{2,1,0:T(8,128)(2,1)} %bitcast.45), calls=%async_computation.2 | async-start | bytes 4194304 | tf_op jit(solution)/shard_map/all_to_all | solution.py:130
Sparse Core Ops, SparseCore 0:
  11.3 33.9 all-gather.2
  47.8 94.8 all-gather.4

commit v6 on v2

--- a/solution.py
+++ b/solution.py
@@ -65,6 +65,7 @@
     col_coord = patch_pos[1].astype(jnp.float32) * SIDE / col_size
     stacked_weight = qkv_weight.reshape(3 * head_width, D)
     normed = layer_norm(tokens.astype(jnp.float32), attn_gain).astype(jnp.bfloat16)
+    full_merge_weight = lax.all_gather(merge_weight, TOK, axis=1, tiled=True)
     projected_rows = lax.dot_general(
         lax.all_gather(normed, HEAD, axis=0, tiled=True),
         stacked_weight,
@@ -77,7 +78,7 @@
     )
     key_all = rotate(projected_rows[:, 1], row_coord, col_coord).astype(jnp.bfloat16)
     value_all = projected_rows[:, 2].astype(jnp.bfloat16)
-    block_len = min(512, group_len)
+    block_len = min(1024, group_len)
     block_count = group_len // block_len
     key_live = live_mask == 1
 
@@ -106,12 +107,14 @@
 
     block_starts = jnp.arange(block_count, dtype=jnp.int32) * block_len
     heads_out = lax.map(query_block, block_starts).reshape(group_len, head_width)
-    attn_rows = lax.psum_scatter(
-        jnp.dot(heads_out, out_weight, preferred_element_type=jnp.float32).astype(jnp.bfloat16),
-        HEAD,
-        scatter_dimension=0,
-        tiled=True,
-    ).astype(jnp.float32)
+    head_count = lax.axis_size(HEAD)
+    head_terms = jnp.dot(heads_out, out_weight, preferred_element_type=jnp.float32).astype(
+        jnp.bfloat16
+    )
+    head_terms = lax.all_to_all(
+        head_terms.reshape(head_count, local_rows, D), HEAD, split_axis=0, concat_axis=0, tiled=True
+    )
+    attn_rows = jnp.sum(head_terms.astype(jnp.float32), axis=0)
     stream = (tokens.astype(jnp.float32) + attn_rows).reshape(local_rows // 4, 4, D)
     average = jnp.sum(stream, axis=2, keepdims=True) / D
     variance = jnp.sum(stream * stream, axis=2, keepdims=True) / D - average * average
@@ -124,14 +127,17 @@
     merged_count = local_rows // 4
     column_terms = jnp.dot(
         merged_slice,
-        lax.all_gather(
-            lax.all_gather(merge_weight, "tz", axis=1, tiled=True), "tx", axis=1, tiled=True
-        ),
+        full_merge_weight,
         preferred_element_type=jnp.float32,
     )
-    projected = lax.psum_scatter(
-        column_terms.astype(jnp.bfloat16), HEAD, scatter_dimension=0, tiled=True
+    column_terms = lax.all_to_all(
+        column_terms.astype(jnp.bfloat16).reshape(head_count, merged_count, -1),
+        HEAD,
+        split_axis=0,
+        concat_axis=0,
+        tiled=True,
     )
+    projected = jnp.sum(column_terms.astype(jnp.float32), axis=0).astype(jnp.bfloat16)
     slot_count = max(2, 2 * merged_count // tok_count)
     owner_col = owners[:, 0]
     owner_hot = (owner_col[:, None] == jnp.arange(tok_count, dtype=jnp.int32)[None, :]).astype(
@@ -139,13 +145,19 @@
     )
     earlier = jnp.cumsum(owner_hot, axis=0, dtype=jnp.int32) - owner_hot
     slot_index = jnp.sum(earlier * owner_hot, axis=1, dtype=jnp.int32)
-    target = owner_col * slot_count + slot_index
+    x_count = lax.axis_size("tx")
+    z_count = lax.axis_size("tz")
+    owner_x = owner_col // z_count
+    owner_z = owner_col % z_count
+    target = (owner_z * x_count + owner_x) * slot_count + slot_index
     select = (
         jnp.arange(tok_count * slot_count, dtype=jnp.int32)[:, None] == target[None, :]
     ).astype(jnp.bfloat16)
     send_rows = jnp.dot(select, projected, preferred_element_type=jnp.float32).astype(jnp.bfloat16)
-    send_rows = send_rows.reshape(tok_count, slot_count, -1)
-    received = lax.all_to_all(send_rows, TOK, split_axis=0, concat_axis=0, tiled=True)
+    send_rows = send_rows.reshape(z_count, x_count, slot_count, -1)
+    by_z = lax.all_to_all(send_rows, "tz", split_axis=0, concat_axis=0, tiled=True)
+    by_z = jnp.swapaxes(by_z, 0, 1)
+    received = lax.all_to_all(by_z, "tx", split_axis=0, concat_axis=0, tiled=True)
     return received.reshape(tok_count * slot_count, -1)
 
 

time: 284 us -> 227 us (0.80)
  the two profiles are of different devices: /device:TPU:57 before, /device:TPU:2 now
where the time goes in v6:
time: 227 us; the launch traced here: 226 us
  waiting for transfers between devices  106 us (47%)
  blocking collectives  46.1 us (20%)
  matrix products  26.2 us (12%)
  other arithmetic  20.3 us (9%)
  between operations  13.6 us (6%)
  starting transfers between devices  9.72 us (4%)
  local copies, waits for them, and re-layouts  3.88 us (2%)
    all_to_all x1, waiting for transfers between devices, body(): lax.all_to_all(head_terms.reshape(head_count, local_rows, D), HEAD, split...  40.9 us
    all_to_all x1, waiting for transfers between devices, body(): lax.all_to_all(column_terms.astype(jnp.bfloat16).reshape(head_count, merg...  26.9 us
    all_gather x1, waiting for transfers between devices, body(): lax.all_gather(normed, HEAD, axis=0, tiled=True)  26.6 us
    all_to_all x1, blocking collectives, body(): lax.all_to_all(send_rows, 'tz', split_axis=0, concat_axis=0, tiled=True)  22.5 us
    all_to_all x1, blocking collectives, body(): lax.all_to_all(window_rows.reshape(local_rows // 4, 4 * D), HEAD, split_a...  12 us
    all_to_all x1, blocking collectives, body(): lax.all_to_all(by_z, 'tx', split_axis=0, concat_axis=0, tiled=True)  11.6 us
    all_gather x1, waiting for transfers between devices, body(): full_merge_weight = lax.all_gather(merge_weight, TOK, axis=1, tiled=True)  10.9 us
    sub x1, matrix products, query_block(): exponent = jnp.where(allowed[None], jnp.exp(masked - row_top), 0.0)  8.4 us
  transfers between devices with their start and end apart: 4, of which 4 were waited for; matrix products, arithmetic and copies ran while one was open for 15% of the time, Pallas kernels for 0%

profile of v6, /device:TPU:2, one launch (start us, length us, event | category | flops | bytes accessed | tf_op | source)
XLA Modules:
  0.0 225.8 jit_solution(822586971466887395)
XLA Ops:
  6.5 1.3 convert_reduce_fusion.1
  7.8 1.3 fusion.28
  9.1 2.1 fusion.30
  16.0 3.1 %fusion.8 = pred[1024,1024]{0,1:T(8,128)(4,1)} fusion(s32[1024]{0:T(1024)} %param.18, pred[1024]{0:T(1024)(128)(4,1)S(1)} %broadcast_compare_fusion), kind=kLoop, calls=%fused_computation.12 | loop fusion | flops 4194304 | bytes 1053696 | tf_op jit(solution)/shard_map/while/body/eval_jaxpr/and | solution.py:90
  19.1 26.6 %all-gather.3.cloned.1.call-done = bf16[1024,1664]{1,0:T(8,128)(2,1)} async-done(((bf16[128,1664]{1,0:T(8,128)(2,1)}), bf16[1024,1664]{1,0:T(8,128)(2,1)}) %all-gather.3.cloned.1.call-update) | async-done | bytes 3407888 | tf_op jit(solution)/shard_map/all_gather | solution.py:70
  45.7 4.5 %fusion.10 = f32[1024,3,2,104]{0,3,2,1:T(8,128)S(1)} fusion(bf16[3,2,104,1664]{3,2,1,0:T(8,128)(2,1)S(1)} %bitcast.44, bf16[1024,1664]{1,0:T(8,128)(2,1)} %all-gather.3.cloned.1.call-done), kind=kOutput, calls=%fused_computation.15 | convolution fusion | flops 2126512128 | bytes 8040448 | tf_op jit(solution)/shard_map/dot_general | solution.py:69
  50.4 1.4 subtract_convert_fusion.1
  52.7 8.4 %fusion.49 = (f32[2,1024]{1,0:T(2,128)S(1)}, bf16[2,1024,1024]{1,2,0:T(8,128)(2,1)}) fusion(pred[1024,1024]{0,1:T(8,128)(4,1)} %fusion.8, bf16[1024,2,26]{0,2,1:T(8,128)(2,1)} %get-tuple-element.43, bf16[1024,2,26]{0,2,1:T(8,128)(2,1)} %get-tuple-element.44, bf16[1024,2,26]{0,2,1:T(8,128)(2,1)} %get-tuple-element.38, ...), kind=kOutput, calls=%fused_computation.86 | convolution fusion | flops 449463296 | bytes 6529024 | tf_op jit(solution)/shard_map/while/body/eval_jaxpr/sub | solution.py:98
  61.1 3.3 %fusion.18 = bf16[1024,2,104]{0,2,1:T(8,128)(2,1)S(1)} fusion(bf16[2,1024,1024]{1,2,0:T(8,128)(2,1)} %get-tuple-element.56, f32[1024,3,2,104]{0,3,2,1:T(8,128)} %copy-done.2, f32[1024,2]{0,1:T(2,128)S(1)} %bitcast.56), kind=kOutput, calls=%fused_computation.22 | convolution fusion | flops 436633600 | bytes 5054464 | tf_op jit(solution)/shard_map/while/body/eval_jaxpr/hqk,khd->qhd/dot_general | solution.py:100
  64.4 3.0 %convolution_convert_fusion.2 = bf16[1024,1664]{1,0:T(8,128)(2,1)} fusion(bf16[1024,208]{0,1:T(8,128)(2,1)S(1)} %bitcast.48, bf16[208,1664]{1,0:T(8,128)(2,1)S(1)} %copy-done.3), kind=kOutput, calls=%fused_computation.14 | convolution fusion | flops 710541312 | bytes 4526080 | tf_op jit(solution)/shard_map/dot_general | solution.py:111
  67.4 4.8 %all-to-all-start = ((bf16[8,128,1664]{2,1,0:T(8,128)(2,1)}), bf16[8,128,1664]{2,1,0:T(8,128)(2,1)}, u32[]{:S(2)}, u32[]{:S(2)}) async-start(bf16[8,128,1664]{2,1,0:T(8,128)(2,1)} %bitcast.45), calls=%async_computation | async-start | bytes 6815744 | tf_op jit(solution)/shard_map/all_to_all | solution.py:114
  72.4 40.9 %all-to-all-done = bf16[8,128,1664]{2,1,0:T(8,128)(2,1)} async-done(((bf16[8,128,1664]{2,1,0:T(8,128)(2,1)}), bf16[8,128,1664]{2,1,0:T(8,128)(2,1)}, u32[]{:S(2)}, u32[]{:S(2)}) %all-to-all-start) | async-done | bytes 3407904 | tf_op jit(solution)/shard_map/all_to_all | solution.py:114
  113.3 2.6 %convert_reduce_fusion = f32[128,1664]{1,0:T(8,128)S(1)} fusion(bf16[8,128,1664]{2,1,0:T(8,128)(2,1)} %all-to-all-done), kind=kLoop, calls=%fused_computation.4 | loop fusion | flops 3194880 | bytes 4259840 | tf_op jit(solution)/shard_map/reduce_sum | solution.py:117
  115.9 1.1 fusion.48
  117.3 1.4 reshape.354
  119.1 12.0 %all_to_all.36 = bf16[32,8,832]{2,0,1:T(8,128)(2,1)S(1)} all-to-all(bf16[32,8,832]{2,0,1:T(8,128)(2,1)S(1)} %fusion.27), channel_id=1, replica_groups=mesh['tx'=4,'tz'=8,'hy'=4,'hc'=2] {'hy','hc'}, dimensions={1} | all-to-all | bytes 851968 | tf_op jit(solution)/shard_map/all_to_all | solution.py:124
  131.1 10.9 %all-gather.5.cloned.1.call-done = bf16[832,4096]{1,0:T(8,128)(2,1)} async-done(((bf16[832,128]{1,0:T(8,128)(2,1)}), bf16[832,4096]{1,0:T(8,128)(2,1)}) %all-gather.5.cloned.1.call-update) | async-done | bytes 6815760 | tf_op jit(solution)/shard_map/all_gather | solution.py:68
  141.9 6.7 %convolution_convert_fusion = bf16[256,4096]{1,0:T(8,128)(2,1)} fusion(bf16[256,832]{1,0:T(8,128)(2,1)S(1)} %bitcast.49, bf16[832,4096]{1,0:T(8,128)(2,1)} %all-gather.5.cloned.1.call-done), kind=kOutput, calls=%fused_computation.5 | convolution fusion | flops 1745879040 | bytes 9338880 | tf_op jit(solution)/shard_map/dot_general | solution.py:128
  148.7 4.9 %all-to-all-start.2 = ((bf16[8,32,4096]{2,1,0:T(8,128)(2,1)}), bf16[8,32,4096]{2,1,0:T(8,128)(2,1)}, u32[]{:S(2)}, u32[]{:S(2)}) async-start(bf16[8,32,4096]{2,1,0:T(8,128)(2,1)} %bitcast.46), calls=%async_computation.2 | async-start | bytes 4194304 | tf_op jit(solution)/shard_map/all_to_all | solution.py:133
  153.9 26.9 %all-to-all-done.2 = bf16[8,32,4096]{2,1,0:T(8,128)(2,1)} async-done(((bf16[8,32,4096]{2,1,0:T(8,128)(2,1)}), bf16[8,32,4096]{2,1,0:T(8,128)(2,1)}, u32[]{:S(2)}, u32[]{:S(2)}) %all-to-all-start.2) | async-done | bytes 2097184 | tf_op jit(solution)/shard_map/all_to_all | solution.py:133
  180.8 1.9 reduce_sum.103
  183.4 22.5 %all_to_all.37 = bf16[8,4,2,4096]{3,2,1,0:T(2,128)(2,1)S(1)} all-to-all(bf16[8,4,2,4096]{3,2,1,0:T(2,128)(2,1)S(1)} %reshape.356), channel_id=1, replica_groups=mesh['tx'=4,'tz'=8,'hy'=4,'hc'=2] {'tz'}, dimensions={0} | all-to-all | bytes 1048576 | tf_op jit(solution)/shard_map/all_to_all | solution.py:158
  206.4 11.6 %all_to_all.38 = bf16[4,8,2,4096]{3,2,1,0:T(2,128)(2,1)S(1)} all-to-all(bf16[4,8,2,4096]{3,2,1,0:T(2,128)(2,1)S(1)} %copy.33), channel_id=1, replica_groups=mesh['tx'=4,'tz'=8,'hy'=4,'hc'=2] {'tx'}, dimensions={0} | all-to-all | bytes 1048576 | tf_op jit(solution)/shard_map/all_to_all | solution.py:160
  218.0 1.0 reshape.357
  (49 shorter events, 8.1 us)
Async XLA Ops:
  6.5 39.1 %copy-start = (bf16[3,208,1664]{2,1,0:T(8,128)(2,1)S(1)}, bf16[3,208,1664]{2,1,0:T(8,128)(2,1)}, u32[]{:S(2)}) copy-start(bf16[3,208,1664]{2,1,0:T(8,128)(2,1)} %param.13) | copy-start | bytes 6230020
  6.5 39.1 %all-gather.3.cloned.1.call-start = ((), (), s32[]{:S(2)}) async-start(), calls=%async_computation.5 | async-start | bytes 3833856 | tf_op jit(solution)/shard_map/all_gather | solution.py:70
  11.2 130.7 %all-gather.5.cloned.1.call-start = ((), (), s32[]{:S(2)}) async-start(), calls=%async_computation.6 | async-start | bytes 7028736 | tf_op jit(solution)/shard_map/all_gather | solution.py:68
  50.2 2.5 %copy-start.2 = (f32[1024,3,2,104]{0,3,2,1:T(8,128)}, f32[1024,3,2,104]{0,3,2,1:T(8,128)S(1)}, u32[]{:S(2)}) copy-start(f32[1024,3,2,104]{0,3,2,1:T(8,128)S(1)} %fusion.10) | copy-start | bytes 7667716
  61.1 3.3 %copy-start.3 = (bf16[208,1664]{1,0:T(8,128)(2,1)S(1)}, bf16[208,1664]{1,0:T(8,128)(2,1)}, u32[]{:S(2)}) copy-start(bf16[208,1664]{1,0:T(8,128)(2,1)} %param.14) | copy-start | bytes 2076676
  67.4 4.8 %copy-start.4 = (f32[1664]{0:T(1024)S(1)}, f32[1664]{0:T(1024)}, u32[]{:S(2)}) copy-start(f32[1664]{0:T(1024)} %param.15) | copy-start | bytes 19972
  67.4 48.4 %copy-start.1 = (bf16[128,1664]{1,0:T(8,128)(2,1)S(1)}, bf16[128,1664]{1,0:T(8,128)(2,1)}, u32[]{:S(2)}) copy-start(bf16[128,1664]{1,0:T(8,128)(2,1)} %param.11) | copy-start | bytes 1277956
  67.4 45.8 %all-to-all-start = ((bf16[8,128,1664]{2,1,0:T(8,128)(2,1)}), bf16[8,128,1664]{2,1,0:T(8,128)(2,1)}, u32[]{:S(2)}, u32[]{:S(2)}) async-start(bf16[8,128,1664]{2,1,0:T(8,128)(2,1)} %bitcast.45), calls=%async_computation | async-start | bytes 6815744 | tf_op jit(solution)/shard_map/all_to_all | solution.py:114
  148.7 4.9 %copy-start.5 = (s32[32,1]{0,1:T(1,128)S(1)}, s32[32,1]{0,1:T(1,128)}, u32[]{:S(2)}) copy-start(s32[32,1]{0,1:T(1,128)} %param.21) | copy-start | bytes 388
  148.7 32.2 %all-to-all-start.2 = ((bf16[8,32,4096]{2,1,0:T(8,128)(2,1)}), bf16[8,32,4096]{2,1,0:T(8,128)(2,1)}, u32[]{:S(2)}, u32[]{:S(2)}) async-start(bf16[8,32,4096]{2,1,0:T(8,128)(2,1)} %bitcast.46), calls=%async_computation.2 | async-start | bytes 4194304 | tf_op jit(solution)/shard_map/all_to_all | solution.py:133
Sparse Core Ops, SparseCore 0:
  11.3 34.2 all-gather.2
  48.1 93.7 all-gather.4

commit v7 on v5

--- a/solution.py
+++ b/solution.py
@@ -61,10 +61,11 @@
     row_coord = patch_pos[0].astype(jnp.float32) * SIDE / row_size
     col_coord = patch_pos[1].astype(jnp.float32) * SIDE / col_size
     stacked_weight = qkv_weight.reshape(3 * head_width, D)
-    normed = layer_norm(tokens.astype(jnp.float32), attn_gain).astype(jnp.bfloat16)
     full_merge_weight = lax.all_gather(merge_weight, "tok", axis=1, tiled=True)
     projected_rows = lax.dot_general(
-        lax.all_gather(normed, "head", axis=0, tiled=True),
+        layer_norm(
+            lax.all_gather(tokens, "head", axis=0, tiled=True).astype(jnp.float32), attn_gain
+        ).astype(jnp.bfloat16),
         stacked_weight,
         (((1,), (1,)), ((), ())),
         preferred_element_type=jnp.float32,

time: 218 us -> 216 us (level)
  transfers between devices with their start and end apart: 4 -> 4, of which waited for: 4 -> 4; matrix products, arithmetic and copies ran while one was open for 16% -> 17% of each run, Pallas kernels for 0% -> 0%
where the time goes in v7:
time: 216 us; the launch traced here: 215 us
  waiting for transfers between devices  107 us (50%)
  blocking collectives  37.2 us (17%)
  matrix products  24.4 us (11%)
  other arithmetic  19.1 us (9%)
  between operations  13.6 us (6%)
  starting transfers between devices  9.72 us (5%)
  local copies, waits for them, and re-layouts  3.7 us (2%)
    all_to_all x1, waiting for transfers between devices, body(): lax.all_to_all(head_terms.reshape(head_count, local_rows, D), 'head', spl...  40.9 us
    all_gather x1, waiting for transfers between devices, body(): lax.all_gather(tokens, 'head', axis=0, tiled=True).astype(jnp.float32)  28 us
    all_to_all x1, waiting for transfers between devices, body(): lax.all_to_all(column_terms.astype(jnp.bfloat16).reshape(head_count, merg...  26.9 us
    all_to_all x1, blocking collectives, body(): lax.all_to_all(send_rows, 'tok', split_axis=0, concat_axis=0, tiled=True)  25.2 us
    all_to_all x1, blocking collectives, body(): lax.all_to_all(window_rows.reshape(local_rows // 4, 4 * D), 'head', split...  12 us
    all_gather x1, waiting for transfers between devices, body(): full_merge_weight = lax.all_gather(merge_weight, 'tok', axis=1, tiled=True)  9.82 us
    sub x1, matrix products, query_block(): exponent = jnp.where(allowed[None], jnp.exp(masked - row_top), 0.0)  8.45 us
    dot_general x1, matrix products, body(): jnp.dot(merged_slice, full_merge_weight, preferred_element_type=jnp.float32)  6.75 us
  transfers between devices with their start and end apart: 4, of which 4 were waited for; matrix products, arithmetic and copies ran while one was open for 17% of the time, Pallas kernels for 0%

profile of v7, /device:TPU:32, one launch (start us, length us, event | category | flops | bytes accessed | tf_op | source)
XLA Modules:
  0.0 214.9 jit_solution(17551492727759619733)
XLA Ops:
  11.0 1.0 multiply_cosine_fusion.1
  12.0 3.1 %fusion.13 = pred[1024,1024]{0,1:T(8,128)(4,1)} fusion(s32[1024]{0:T(1024)} %param.18, pred[1024]{0:T(1024)(128)(4,1)S(1)} %broadcast_compare_fusion), kind=kLoop, calls=%fused_computation.19 | loop fusion | flops 4194304 | bytes 1053696 | tf_op jit(solution)/shard_map/while/body/eval_jaxpr/and | solution.py:88
  15.1 28.0 %all-gather.3.cloned.1.call-done = bf16[1024,1664]{1,0:T(8,128)(2,1)} async-done(((bf16[128,1664]{1,0:T(8,128)(2,1)}), bf16[1024,1664]{1,0:T(8,128)(2,1)}) %all-gather.3.cloned.1.call-update) | async-done | bytes 3407888 | tf_op jit(solution)/shard_map/all_gather | solution.py:67
  43.2 2.6 %convert_reduce_fusion = f32[1024]{0:T(1024)S(1)} fusion(bf16[1024,1664]{1,0:T(8,128)(2,1)} %all-gather.3.cloned.1.call-done), kind=kLoop, calls=%fused_computation.2 | loop fusion | flops 3406848 | bytes 3411968 | tf_op jit(solution)/shard_map/reduce_sum | solution.py:16
  46.1 1.0 fusion.4
  47.2 2.7 %fusion.16 = f32[1024,3,2,104]{0,3,2,1:T(8,128)S(1)} fusion(bf16[3,2,104,1664]{3,2,1,0:T(8,128)(2,1)S(1)} %bitcast.43, bf16[1024,1664]{1,0:T(8,128)(2,1)S(1)} %copy-done.1, f32[1664]{0:T(1024)S(1)} %copy-done.7, f32[1024]{0:T(1024)S(1)} %add_rsqrt_fusion.1, f32[1024]{0:T(1024)S(1)} %broadcast_multiply_fusion), kind=kOutput, calls=%fused_computation.23 | convolution fusion | flops 2135031808 | bytes 8055296 | tf_op jit(solution)/shard_map/dot_general | solution.py:65
  50.0 1.3 subtract_convert_fusion.1
  51.3 0.9 multiply_subtract_fusion.1
  52.2 8.4 %fusion.51 = (f32[2,1024]{1,0:T(2,128)S(1)}, bf16[2,1024,1024]{1,2,0:T(8,128)(2,1)}) fusion(pred[1024,1024]{0,1:T(8,128)(4,1)} %fusion.13, bf16[1024,2,26]{0,2,1:T(8,128)(2,1)} %get-tuple-element.43, bf16[1024,2,26]{0,2,1:T(8,128)(2,1)} %get-tuple-element.44, bf16[1024,2,26]{0,2,1:T(8,128)(2,1)} %get-tuple-element.38, ...), kind=kOutput, calls=%fused_computation.82 | convolution fusion | flops 449463296 | bytes 6529024 | tf_op jit(solution)/shard_map/while/body/eval_jaxpr/sub | solution.py:96
  60.7 3.3 %fusion.27 = bf16[1024,2,104]{0,2,1:T(8,128)(2,1)S(1)} fusion(bf16[2,1024,1024]{1,2,0:T(8,128)(2,1)} %get-tuple-element.56, f32[1024,3,2,104]{0,3,2,1:T(8,128)} %copy-done.3, f32[1024,2]{0,1:T(2,128)S(1)} %bitcast.54), kind=kOutput, calls=%fused_computation.29 | convolution fusion | flops 436633600 | bytes 5054464 | tf_op jit(solution)/shard_map/while/body/eval_jaxpr/hqk,khd->qhd/dot_general | solution.py:98
  64.0 3.0 %convolution_convert_fusion.2 = bf16[1024,1664]{1,0:T(8,128)(2,1)} fusion(bf16[1024,208]{0,1:T(8,128)(2,1)S(1)} %bitcast.46, bf16[208,1664]{1,0:T(8,128)(2,1)S(1)} %copy-done.4), kind=kOutput, calls=%fused_computation.21 | convolution fusion | flops 710541312 | bytes 4526080 | tf_op jit(solution)/shard_map/dot_general | solution.py:109
  67.0 4.8 %all-to-all-start = ((bf16[8,128,1664]{2,1,0:T(8,128)(2,1)}), bf16[8,128,1664]{2,1,0:T(8,128)(2,1)}, u32[]{:S(2)}, u32[]{:S(2)}) async-start(bf16[8,128,1664]{2,1,0:T(8,128)(2,1)} %bitcast.44), calls=%async_computation | async-start | bytes 6815744 | tf_op jit(solution)/shard_map/all_to_all | solution.py:112
  71.9 40.9 %all-to-all-done = bf16[8,128,1664]{2,1,0:T(8,128)(2,1)} async-done(((bf16[8,128,1664]{2,1,0:T(8,128)(2,1)}), bf16[8,128,1664]{2,1,0:T(8,128)(2,1)}, u32[]{:S(2)}, u32[]{:S(2)}) %all-to-all-start) | async-done | bytes 3407904 | tf_op jit(solution)/shard_map/all_to_all | solution.py:112
  112.8 2.5 %convert_reduce_fusion.1 = f32[128,1664]{1,0:T(8,128)S(1)} fusion(bf16[8,128,1664]{2,1,0:T(8,128)(2,1)} %all-to-all-done), kind=kLoop, calls=%fused_computation.11 | loop fusion | flops 3194880 | bytes 4259840 | tf_op jit(solution)/shard_map/reduce_sum | solution.py:115
  115.3 1.1 fusion.50
  116.8 1.4 reshape.308
  118.5 12.0 %all_to_all.31 = bf16[32,8,832]{2,0,1:T(8,128)(2,1)S(1)} all-to-all(bf16[32,8,832]{2,0,1:T(8,128)(2,1)S(1)} %fusion.34), channel_id=1, replica_groups=mesh['tok'=32,'head'=8] {'head'}, dimensions={1} | all-to-all | bytes 851968 | tf_op jit(solution)/shard_map/all_to_all | solution.py:122
  130.6 9.8 %all-gather.5.cloned.1.call-done = bf16[832,4096]{1,0:T(8,128)(2,1)} async-done(((bf16[832,128]{1,0:T(8,128)(2,1)}), bf16[832,4096]{1,0:T(8,128)(2,1)}) %all-gather.5.cloned.1.call-update) | async-done | bytes 6815760 | tf_op jit(solution)/shard_map/all_gather | solution.py:64
  140.4 6.8 %convolution_convert_fusion = bf16[256,4096]{1,0:T(8,128)(2,1)} fusion(bf16[256,832]{1,0:T(8,128)(2,1)S(1)} %bitcast.47, bf16[832,4096]{1,0:T(8,128)(2,1)} %all-gather.5.cloned.1.call-done), kind=kOutput, calls=%fused_computation.12 | convolution fusion | flops 1745879040 | bytes 9338880 | tf_op jit(solution)/shard_map/dot_general | solution.py:126
  147.1 4.9 %all-to-all-start.2 = ((bf16[8,32,4096]{2,1,0:T(8,128)(2,1)}), bf16[8,32,4096]{2,1,0:T(8,128)(2,1)}, u32[]{:S(2)}, u32[]{:S(2)}) async-start(bf16[8,32,4096]{2,1,0:T(8,128)(2,1)} %bitcast.45), calls=%async_computation.2 | async-start | bytes 4194304 | tf_op jit(solution)/shard_map/all_to_all | solution.py:131
  152.4 26.9 %all-to-all-done.2 = bf16[8,32,4096]{2,1,0:T(8,128)(2,1)} async-done(((bf16[8,32,4096]{2,1,0:T(8,128)(2,1)}), bf16[8,32,4096]{2,1,0:T(8,128)(2,1)}, u32[]{:S(2)}, u32[]{:S(2)}) %all-to-all-start.2) | async-done | bytes 2097184 | tf_op jit(solution)/shard_map/all_to_all | solution.py:131
  179.3 1.9 reduce_sum.103
  181.8 25.2 %all_to_all.32 = bf16[32,2,4096]{2,1,0:T(2,128)(2,1)S(1)} all-to-all(bf16[32,2,4096]{2,1,0:T(2,128)(2,1)S(1)} %reshape.310), channel_id=1, replica_groups=mesh['tok'=32,'head'=8] {'tok'}, dimensions={0} | all-to-all | bytes 1048576 | tf_op jit(solution)/shard_map/all_to_all | solution.py:152
  207.1 1.0 reshape.311
  (50 shorter events, 6.7 us)
Async XLA Ops:
  6.5 40.7 %copy-start = (bf16[3,208,1664]{2,1,0:T(8,128)(2,1)S(1)}, bf16[3,208,1664]{2,1,0:T(8,128)(2,1)}, u32[]{:S(2)}) copy-start(bf16[3,208,1664]{2,1,0:T(8,128)(2,1)} %param.13) | copy-start | bytes 6230020
  6.5 36.6 %all-gather.3.cloned.1.call-start = ((), (), s32[]{:S(2)}) async-start(), calls=%async_computation.4 | async-start | bytes 3833856 | tf_op jit(solution)/shard_map/all_gather | solution.py:67
  7.3 133.1 %all-gather.5.cloned.1.call-start = ((), (), s32[]{:S(2)}) async-start(), calls=%async_computation.5 | async-start | bytes 7028736 | tf_op jit(solution)/shard_map/all_gather | solution.py:64
  11.0 36.2 %copy-start.7 = (f32[1664]{0:T(1024)S(1)}, f32[1664]{0:T(1024)}, u32[]{:S(2)}) copy-start(f32[1664]{0:T(1024)} %param.12) | copy-start | bytes 19972
  43.2 3.0 %copy-start.1 = (bf16[1024,1664]{1,0:T(8,128)(2,1)S(1)}, bf16[1024,1664]{1,0:T(8,128)(2,1)}, u32[]{:S(2)}) copy-start(bf16[1024,1664]{1,0:T(8,128)(2,1)} %all-gather.3.cloned.1.call-done) | copy-start | bytes 10223620
  49.9 2.3 %copy-start.3 = (f32[1024,3,2,104]{0,3,2,1:T(8,128)}, f32[1024,3,2,104]{0,3,2,1:T(8,128)S(1)}, u32[]{:S(2)}) copy-start(f32[1024,3,2,104]{0,3,2,1:T(8,128)S(1)} %fusion.16) | copy-start | bytes 7667716
  60.7 3.3 %copy-start.4 = (bf16[208,1664]{1,0:T(8,128)(2,1)S(1)}, bf16[208,1664]{1,0:T(8,128)(2,1)}, u32[]{:S(2)}) copy-start(bf16[208,1664]{1,0:T(8,128)(2,1)} %param.14) | copy-start | bytes 2076676
  67.0 4.8 %copy-start.5 = (f32[1664]{0:T(1024)S(1)}, f32[1664]{0:T(1024)}, u32[]{:S(2)}) copy-start(f32[1664]{0:T(1024)} %param.15) | copy-start | bytes 19972
  67.0 48.4 %copy-start.2 = (bf16[128,1664]{1,0:T(8,128)(2,1)S(1)}, bf16[128,1664]{1,0:T(8,128)(2,1)}, u32[]{:S(2)}) copy-start(bf16[128,1664]{1,0:T(8,128)(2,1)} %param.11) | copy-start | bytes 1277956
  67.0 45.8 %all-to-all-start = ((bf16[8,128,1664]{2,1,0:T(8,128)(2,1)}), bf16[8,128,1664]{2,1,0:T(8,128)(2,1)}, u32[]{:S(2)}, u32[]{:S(2)}) async-start(bf16[8,128,1664]{2,1,0:T(8,128)(2,1)} %bitcast.44), calls=%async_computation | async-start | bytes 6815744 | tf_op jit(solution)/shard_map/all_to_all | solution.py:112
  147.1 4.9 %copy-start.6 = (s32[32,1]{0,1:T(1,128)S(1)}, s32[32,1]{0,1:T(1,128)}, u32[]{:S(2)}) copy-start(s32[32,1]{0,1:T(1,128)} %param.21) | copy-start | bytes 388
  147.1 32.2 %all-to-all-start.2 = ((bf16[8,32,4096]{2,1,0:T(8,128)(2,1)}), bf16[8,32,4096]{2,1,0:T(8,128)(2,1)}, u32[]{:S(2)}, u32[]{:S(2)}) async-start(bf16[8,32,4096]{2,1,0:T(8,128)(2,1)} %bitcast.45), calls=%async_computation.2 | async-start | bytes 4194304 | tf_op jit(solution)/shard_map/all_to_all | solution.py:131
Sparse Core Ops, SparseCore 0:
  9.2 33.9 all-gather.2
  45.6 94.7 all-gather.4

commit v8 on v6

--- a/solution.py
+++ b/solution.py
@@ -64,10 +64,11 @@
     row_coord = patch_pos[0].astype(jnp.float32) * SIDE / row_size
     col_coord = patch_pos[1].astype(jnp.float32) * SIDE / col_size
     stacked_weight = qkv_weight.reshape(3 * head_width, D)
-    normed = layer_norm(tokens.astype(jnp.float32), attn_gain).astype(jnp.bfloat16)
     full_merge_weight = lax.all_gather(merge_weight, TOK, axis=1, tiled=True)
     projected_rows = lax.dot_general(
-        lax.all_gather(normed, HEAD, axis=0, tiled=True),
+        layer_norm(
+            lax.all_gather(tokens, HEAD, axis=0, tiled=True).astype(jnp.float32), attn_gain
+        ).astype(jnp.bfloat16),
         stacked_weight,
         (((1,), (1,)), ((), ())),
         preferred_element_type=jnp.float32,
@@ -125,19 +126,23 @@
         window_rows.reshape(local_rows // 4, 4 * D), HEAD, split_axis=1, concat_axis=0, tiled=True
     )
     merged_count = local_rows // 4
-    column_terms = jnp.dot(
-        merged_slice,
-        full_merge_weight,
-        preferred_element_type=jnp.float32,
-    )
+    y_count = lax.axis_size("hy")
+    core_count = lax.axis_size("hc")
+    by_core = merged_slice.reshape(y_count, core_count, merged_count, -1)
+    by_core = jnp.swapaxes(by_core, 0, 1).reshape(head_count * merged_count, -1)
+    column_terms = jnp.dot(by_core, full_merge_weight, preferred_element_type=jnp.float32)
     column_terms = lax.all_to_all(
-        column_terms.astype(jnp.bfloat16).reshape(head_count, merged_count, -1),
-        HEAD,
+        column_terms.astype(jnp.bfloat16).reshape(core_count, y_count * merged_count, -1),
+        "hc",
         split_axis=0,
         concat_axis=0,
         tiled=True,
     )
-    projected = jnp.sum(column_terms.astype(jnp.float32), axis=0).astype(jnp.bfloat16)
+    chip_terms = jnp.sum(column_terms.astype(jnp.float32), axis=0).astype(jnp.bfloat16)
+    chip_terms = lax.all_to_all(
+        chip_terms.reshape(y_count, merged_count, -1), "hy", split_axis=0, concat_axis=0, tiled=True
+    )
+    projected = jnp.sum(chip_terms.astype(jnp.float32), axis=0).astype(jnp.bfloat16)
     slot_count = max(2, 2 * merged_count // tok_count)
     owner_col = owners[:, 0]
     owner_hot = (owner_col[:, None] == jnp.arange(tok_count, dtype=jnp.int32)[None, :]).astype(
@@ -145,19 +150,13 @@
     )
     earlier = jnp.cumsum(owner_hot, axis=0, dtype=jnp.int32) - owner_hot
     slot_index = jnp.sum(earlier * owner_hot, axis=1, dtype=jnp.int32)
-    x_count = lax.axis_size("tx")
-    z_count = lax.axis_size("tz")
-    owner_x = owner_col // z_count
-    owner_z = owner_col % z_count
-    target = (owner_z * x_count + owner_x) * slot_count + slot_index
+    target = owner_col * slot_count + slot_index
     select = (
         jnp.arange(tok_count * slot_count, dtype=jnp.int32)[:, None] == target[None, :]
     ).astype(jnp.bfloat16)
     send_rows = jnp.dot(select, projected, preferred_element_type=jnp.float32).astype(jnp.bfloat16)
-    send_rows = send_rows.reshape(z_count, x_count, slot_count, -1)
-    by_z = lax.all_to_all(send_rows, "tz", split_axis=0, concat_axis=0, tiled=True)
-    by_z = jnp.swapaxes(by_z, 0, 1)
-    received = lax.all_to_all(by_z, "tx", split_axis=0, concat_axis=0, tiled=True)
+    send_rows = send_rows.reshape(tok_count, slot_count, -1)
+    received = lax.all_to_all(send_rows, TOK, split_axis=0, concat_axis=0, tiled=True)
     return received.reshape(tok_count * slot_count, -1)
 
 

time: 227 us -> 209 us (0.921)
  the two profiles are of different devices: /device:TPU:2 before, /device:TPU:32 now
where the time goes in v8:
time: 209 us
  waiting for transfers between devices  95.1 us (46%)
  blocking collectives  43.1 us (21%)
  matrix products  23 us (11%)
  other arithmetic  20.5 us (10%)
  between operations  13.6 us (7%)
  starting transfers between devices  9.44 us (5%)
  local copies, waits for them, and re-layouts  3.96 us (2%)
    all_to_all x1, waiting for transfers between devices, body(): lax.all_to_all(head_terms.reshape(head_count, local_rows, D), HEAD, split...  40.9 us
    all_gather x1, waiting for transfers between devices, body(): lax.all_gather(tokens, HEAD, axis=0, tiled=True).astype(jnp.float32)  28 us
    all_to_all x1, blocking collectives, body(): lax.all_to_all(send_rows, TOK, split_axis=0, concat_axis=0, tiled=True)  24.8 us
    all_to_all x1, waiting for transfers between devices, body(): lax.all_to_all(chip_terms.reshape(y_count, merged_count, -1), 'hy', split...  15.1 us
    all_to_all x1, blocking collectives, body(): lax.all_to_all(window_rows.reshape(local_rows // 4, 4 * D), HEAD, split_a...  12 us
    all_gather x1, waiting for transfers between devices, body(): full_merge_weight = lax.all_gather(merge_weight, TOK, axis=1, tiled=True)  9.71 us
    sub x1, matrix products, query_block(): exponent = jnp.where(allowed[None], jnp.exp(masked - row_top), 0.0)  8.45 us
    all_to_all x1, blocking collectives, body(): lax.all_to_all(column_terms.astype(jnp.bfloat16).reshape(core_count, y_co...  6.31 us
  transfers between devices with their start and end apart: 4, of which 4 were waited for; matrix products, arithmetic and copies ran while one was open for 18% of the time, Pallas kernels for 0%

profile of v8, /device:TPU:32, one launch (start us, length us, event | category | flops | bytes accessed | tf_op | source)
XLA Modules:
  0.0 208.8 jit_solution(3028065695344027418)
XLA Ops:
  11.0 1.0 multiply_cosine_fusion.1
  12.0 3.1 %fusion.13 = pred[1024,1024]{0,1:T(8,128)(4,1)} fusion(s32[1024]{0:T(1024)} %param.18, pred[1024]{0:T(1024)(128)(4,1)S(1)} %broadcast_compare_fusion), kind=kLoop, calls=%fused_computation.19 | loop fusion | flops 4194304 | bytes 1053696 | tf_op jit(solution)/shard_map/while/body/eval_jaxpr/and | solution.py:91
  15.1 28.0 %all-gather.3.cloned.1.call-done = bf16[1024,1664]{1,0:T(8,128)(2,1)} async-done(((bf16[128,1664]{1,0:T(8,128)(2,1)}), bf16[1024,1664]{1,0:T(8,128)(2,1)}) %all-gather.3.cloned.1.call-update) | async-done | bytes 3407888 | tf_op jit(solution)/shard_map/all_gather | solution.py:70
  43.2 2.6 %convert_reduce_fusion = f32[1024]{0:T(1024)S(1)} fusion(bf16[1024,1664]{1,0:T(8,128)(2,1)} %all-gather.3.cloned.1.call-done), kind=kLoop, calls=%fused_computation.2 | loop fusion | flops 3406848 | bytes 3411968 | tf_op jit(solution)/shard_map/reduce_sum | solution.py:19
  46.1 1.0 fusion.4
  47.2 2.7 %fusion.16 = f32[1024,3,2,104]{0,3,2,1:T(8,128)S(1)} fusion(bf16[3,2,104,1664]{3,2,1,0:T(8,128)(2,1)S(1)} %bitcast.47, bf16[1024,1664]{1,0:T(8,128)(2,1)S(1)} %copy-done.1, f32[1664]{0:T(1024)S(1)} %copy-done.7, f32[1024]{0:T(1024)S(1)} %add_rsqrt_fusion.1, f32[1024]{0:T(1024)S(1)} %broadcast_multiply_fusion), kind=kOutput, calls=%fused_computation.23 | convolution fusion | flops 2135031808 | bytes 8055296 | tf_op jit(solution)/shard_map/dot_general | solution.py:68
  50.0 1.3 subtract_convert_fusion.1
  52.2 8.4 %fusion.48 = (f32[2,1024]{1,0:T(2,128)S(1)}, bf16[2,1024,1024]{1,2,0:T(8,128)(2,1)}) fusion(pred[1024,1024]{0,1:T(8,128)(4,1)} %fusion.13, bf16[1024,2,26]{0,2,1:T(8,128)(2,1)} %get-tuple-element.43, bf16[1024,2,26]{0,2,1:T(8,128)(2,1)} %get-tuple-element.44, bf16[1024,2,26]{0,2,1:T(8,128)(2,1)} %get-tuple-element.38, ...), kind=kOutput, calls=%fused_computation.79 | convolution fusion | flops 449463296 | bytes 6529024 | tf_op jit(solution)/shard_map/while/body/eval_jaxpr/sub | solution.py:99
  60.7 3.3 %fusion.27 = bf16[1024,2,104]{0,2,1:T(8,128)(2,1)S(1)} fusion(bf16[2,1024,1024]{1,2,0:T(8,128)(2,1)} %get-tuple-element.56, f32[1024,3,2,104]{0,3,2,1:T(8,128)} %copy-done.3, f32[1024,2]{0,1:T(2,128)S(1)} %bitcast.60), kind=kOutput, calls=%fused_computation.29 | convolution fusion | flops 436633600 | bytes 5054464 | tf_op jit(solution)/shard_map/while/body/eval_jaxpr/hqk,khd->qhd/dot_general | solution.py:101
  64.0 3.0 %convolution_convert_fusion.2 = bf16[1024,1664]{1,0:T(8,128)(2,1)} fusion(bf16[1024,208]{0,1:T(8,128)(2,1)S(1)} %bitcast.52, bf16[208,1664]{1,0:T(8,128)(2,1)S(1)} %copy-done.4), kind=kOutput, calls=%fused_computation.21 | convolution fusion | flops 710541312 | bytes 4526080 | tf_op jit(solution)/shard_map/dot_general | solution.py:112
  67.0 4.8 %all-to-all-start = ((bf16[8,128,1664]{2,1,0:T(8,128)(2,1)}), bf16[8,128,1664]{2,1,0:T(8,128)(2,1)}, u32[]{:S(2)}, u32[]{:S(2)}) async-start(bf16[8,128,1664]{2,1,0:T(8,128)(2,1)} %bitcast.48), calls=%async_computation | async-start | bytes 6815744 | tf_op jit(solution)/shard_map/all_to_all | solution.py:115
  71.9 40.9 %all-to-all-done = bf16[8,128,1664]{2,1,0:T(8,128)(2,1)} async-done(((bf16[8,128,1664]{2,1,0:T(8,128)(2,1)}), bf16[8,128,1664]{2,1,0:T(8,128)(2,1)}, u32[]{:S(2)}, u32[]{:S(2)}) %all-to-all-start) | async-done | bytes 3407904 | tf_op jit(solution)/shard_map/all_to_all | solution.py:115
  112.8 2.5 %convert_reduce_fusion.1 = f32[128,1664]{1,0:T(8,128)S(1)} fusion(bf16[8,128,1664]{2,1,0:T(8,128)(2,1)} %all-to-all-done), kind=kLoop, calls=%fused_computation.11 | loop fusion | flops 3194880 | bytes 4259840 | tf_op jit(solution)/shard_map/reduce_sum | solution.py:118
  115.3 1.1 fusion.47
  116.9 1.4 reshape.318
  118.6 12.0 %all_to_all.33 = bf16[32,8,832]{2,0,1:T(8,128)(2,1)S(1)} all-to-all(bf16[32,8,832]{2,0,1:T(8,128)(2,1)S(1)} %copy.41), channel_id=1, replica_groups=mesh['tx'=4,'tz'=8,'hy'=4,'hc'=2] {'hy','hc'}, dimensions={1} | all-to-all | bytes 851968 | tf_op jit(solution)/shard_map/all_to_all | solution.py:125
  130.7 9.7 %all-gather.5.cloned.1.call-done = bf16[832,4096]{1,0:T(8,128)(2,1)} async-done(((bf16[832,128]{1,0:T(8,128)(2,1)}), bf16[832,4096]{1,0:T(8,128)(2,1)}) %all-gather.5.cloned.1.call-update) | async-done | bytes 6815760 | tf_op jit(solution)/shard_map/all_gather | solution.py:67
  140.4 5.4 %convolution_convert_fusion = bf16[256,4096]{1,0:T(8,128)(2,1)S(1)} fusion(bf16[256,832]{1,0:T(8,128)(2,1)S(1)} %bitcast.53, bf16[832,4096]{1,0:T(8,128)(2,1)} %all-gather.5.cloned.1.call-done), kind=kOutput, calls=%fused_computation.12 | convolution fusion | flops 1745879040 | bytes 9338880 | tf_op jit(solution)/shard_map/dot_general | solution.py:133
  145.8 6.3 %all_to_all.34 = bf16[2,128,4096]{2,1,0:T(8,128)(2,1)} all-to-all(bf16[2,128,4096]{2,1,0:T(8,128)(2,1)S(1)} %bitcast.50), channel_id=1, replica_groups=mesh['tx'=4,'tz'=8,'hy'=4,'hc'=2] {'hc'}, dimensions={0} | all-to-all | bytes 4194304 | tf_op jit(solution)/shard_map/all_to_all | solution.py:134
  152.1 3.3 %reduce_sum.115 = bf16[128,4096]{1,0:T(8,128)(2,1)} reduce(bf16[2,128,4096]{2,1,0:T(8,128)(2,1)} %all_to_all.34, bf16[]{:T(256)} %constant.68.clone.1), dimensions={0}, to_apply=%region_11.12 | reduce | flops 524288 | bytes 3145730 | tf_op jit(solution)/shard_map/reduce_sum | solution.py:141
  155.3 4.6 %all-to-all-start.3 = ((bf16[4,32,4096]{2,1,0:T(8,128)(2,1)}), bf16[4,32,4096]{2,1,0:T(8,128)(2,1)S(1)}, u32[]{:S(2)}, u32[]{:S(2)}) async-start(bf16[4,32,4096]{2,1,0:T(8,128)(2,1)} %bitcast.49), calls=%async_computation.3 | async-start | bytes 2097152 | tf_op jit(solution)/shard_map/all_to_all | solution.py:142
  160.3 15.1 %all-to-all-done.3 = bf16[4,32,4096]{2,1,0:T(8,128)(2,1)S(1)} async-done(((bf16[4,32,4096]{2,1,0:T(8,128)(2,1)}), bf16[4,32,4096]{2,1,0:T(8,128)(2,1)S(1)}, u32[]{:S(2)}, u32[]{:S(2)}) %all-to-all-start.3) | async-done | bytes 1048608 | tf_op jit(solution)/shard_map/all_to_all | solution.py:142
  176.2 24.8 %all_to_all.35 = bf16[32,2,4096]{2,1,0:T(2,128)(2,1)S(1)} all-to-all(bf16[32,2,4096]{2,1,0:T(2,128)(2,1)S(1)} %reshape.323), channel_id=1, replica_groups=mesh['tx'=4,'tz'=8,'hy'=4,'hc'=2] {'tx','tz'}, dimensions={0} | all-to-all | bytes 1048576 | tf_op jit(solution)/shard_map/all_to_all | solution.py:159
  201.0 1.0 reshape.324
  (56 shorter events, 7.9 us)
Async XLA Ops:
  6.5 40.7 %copy-start = (bf16[3,208,1664]{2,1,0:T(8,128)(2,1)S(1)}, bf16[3,208,1664]{2,1,0:T(8,128)(2,1)}, u32[]{:S(2)}) copy-start(bf16[3,208,1664]{2,1,0:T(8,128)(2,1)} %param.13) | copy-start | bytes 6230020
  6.5 36.6 %all-gather.3.cloned.1.call-start = ((), (), s32[]{:S(2)}) async-start(), calls=%async_computation.5 | async-start | bytes 3833856 | tf_op jit(solution)/shard_map/all_gather | solution.py:70
  7.3 133.1 %all-gather.5.cloned.1.call-start = ((), (), s32[]{:S(2)}) async-start(), calls=%async_computation.6 | async-start | bytes 7028736 | tf_op jit(solution)/shard_map/all_gather | solution.py:67
  11.0 36.2 %copy-start.7 = (f32[1664]{0:T(1024)S(1)}, f32[1664]{0:T(1024)}, u32[]{:S(2)}) copy-start(f32[1664]{0:T(1024)} %param.12) | copy-start | bytes 19972
  43.2 3.0 %copy-start.1 = (bf16[1024,1664]{1,0:T(8,128)(2,1)S(1)}, bf16[1024,1664]{1,0:T(8,128)(2,1)}, u32[]{:S(2)}) copy-start(bf16[1024,1664]{1,0:T(8,128)(2,1)} %all-gather.3.cloned.1.call-done) | copy-start | bytes 10223620
  49.9 2.3 %copy-start.3 = (f32[1024,3,2,104]{0,3,2,1:T(8,128)}, f32[1024,3,2,104]{0,3,2,1:T(8,128)S(1)}, u32[]{:S(2)}) copy-start(f32[1024,3,2,104]{0,3,2,1:T(8,128)S(1)} %fusion.16) | copy-start | bytes 7667716
  60.7 3.3 %copy-start.4 = (bf16[208,1664]{1,0:T(8,128)(2,1)S(1)}, bf16[208,1664]{1,0:T(8,128)(2,1)}, u32[]{:S(2)}) copy-start(bf16[208,1664]{1,0:T(8,128)(2,1)} %param.14) | copy-start | bytes 2076676
  67.0 4.8 %copy-start.5 = (f32[1664]{0:T(1024)S(1)}, f32[1664]{0:T(1024)}, u32[]{:S(2)}) copy-start(f32[1664]{0:T(1024)} %param.15) | copy-start | bytes 19972
  67.0 48.4 %copy-start.2 = (bf16[128,1664]{1,0:T(8,128)(2,1)S(1)}, bf16[128,1664]{1,0:T(8,128)(2,1)}, u32[]{:S(2)}) copy-start(bf16[128,1664]{1,0:T(8,128)(2,1)} %param.11) | copy-start | bytes 1277956
  67.0 45.8 %all-to-all-start = ((bf16[8,128,1664]{2,1,0:T(8,128)(2,1)}), bf16[8,128,1664]{2,1,0:T(8,128)(2,1)}, u32[]{:S(2)}, u32[]{:S(2)}) async-start(bf16[8,128,1664]{2,1,0:T(8,128)(2,1)} %bitcast.48), calls=%async_computation | async-start | bytes 6815744 | tf_op jit(solution)/shard_map/all_to_all | solution.py:115
  145.7 14.2 %copy-start.6 = (s32[32,1]{0,1:T(1,128)S(1)}, s32[32,1]{0,1:T(1,128)}, u32[]{:S(2)}) copy-start(s32[32,1]{0,1:T(1,128)} %param.21) | copy-start | bytes 388
  155.3 20.0 %all-to-all-start.3 = ((bf16[4,32,4096]{2,1,0:T(8,128)(2,1)}), bf16[4,32,4096]{2,1,0:T(8,128)(2,1)S(1)}, u32[]{:S(2)}, u32[]{:S(2)}) async-start(bf16[4,32,4096]{2,1,0:T(8,128)(2,1)} %bitcast.49), calls=%async_computation.3 | async-start | bytes 2097152 | tf_op jit(solution)/shard_map/all_to_all | solution.py:142
Sparse Core Ops, SparseCore 0:
  9.2 33.9 all-gather.2
  45.6 94.7 all-gather.4

commit v9 on v8

--- a/solution.py
+++ b/solution.py
@@ -65,10 +65,17 @@
     col_coord = patch_pos[1].astype(jnp.float32) * SIDE / col_size
     stacked_weight = qkv_weight.reshape(3 * head_width, D)
     full_merge_weight = lax.all_gather(merge_weight, TOK, axis=1, tiled=True)
+    y_count = lax.axis_size("hy")
+    core_count = lax.axis_size("hc")
+    by_y = lax.all_to_all(
+        jnp.broadcast_to(tokens[None], (y_count,) + tokens.shape), "hy", split_axis=0, concat_axis=0, tiled=True
+    )
+    by_core = lax.all_to_all(
+        jnp.broadcast_to(by_y[None], (core_count,) + by_y.shape), "hc", split_axis=0, concat_axis=0, tiled=True
+    )
+    gathered_tokens = jnp.swapaxes(by_core, 0, 1).reshape(group_len, D)
     projected_rows = lax.dot_general(
-        layer_norm(
-            lax.all_gather(tokens, HEAD, axis=0, tiled=True).astype(jnp.float32), attn_gain
-        ).astype(jnp.bfloat16),
+        layer_norm(gathered_tokens.astype(jnp.float32), attn_gain).astype(jnp.bfloat16),
         stacked_weight,
         (((1,), (1,)), ((), ())),
         preferred_element_type=jnp.float32,
@@ -109,13 +116,19 @@
     block_starts = jnp.arange(block_count, dtype=jnp.int32) * block_len
     heads_out = lax.map(query_block, block_starts).reshape(group_len, head_width)
     head_count = lax.axis_size(HEAD)
-    head_terms = jnp.dot(heads_out, out_weight, preferred_element_type=jnp.float32).astype(
+    heads_by_core = heads_out.reshape(y_count, core_count, local_rows, head_width)
+    heads_by_core = jnp.swapaxes(heads_by_core, 0, 1).reshape(group_len, head_width)
+    head_terms = jnp.dot(heads_by_core, out_weight, preferred_element_type=jnp.float32).astype(
         jnp.bfloat16
     )
     head_terms = lax.all_to_all(
-        head_terms.reshape(head_count, local_rows, D), HEAD, split_axis=0, concat_axis=0, tiled=True
+        head_terms.reshape(core_count, y_count * local_rows, D), "hc", split_axis=0, concat_axis=0, tiled=True
     )
-    attn_rows = jnp.sum(head_terms.astype(jnp.float32), axis=0)
+    chip_rows = jnp.sum(head_terms.astype(jnp.float32), axis=0).astype(jnp.bfloat16)
+    chip_rows = lax.all_to_all(
+        chip_rows.reshape(y_count, local_rows, D), "hy", split_axis=0, concat_axis=0, tiled=True
+    )
+    attn_rows = jnp.sum(chip_rows.astype(jnp.float32), axis=0)
     stream = (tokens.astype(jnp.float32) + attn_rows).reshape(local_rows // 4, 4, D)
     average = jnp.sum(stream, axis=2, keepdims=True) / D
     variance = jnp.sum(stream * stream, axis=2, keepdims=True) / D - average * average
@@ -126,8 +139,6 @@
         window_rows.reshape(local_rows // 4, 4 * D), HEAD, split_axis=1, concat_axis=0, tiled=True
     )
     merged_count = local_rows // 4
-    y_count = lax.axis_size("hy")
-    core_count = lax.axis_size("hc")
     by_core = merged_slice.reshape(y_count, core_count, merged_count, -1)
     by_core = jnp.swapaxes(by_core, 0, 1).reshape(head_count * merged_count, -1)
     column_terms = jnp.dot(by_core, full_merge_weight, preferred_element_type=jnp.float32)
@@ -178,6 +189,4 @@
         P(TOK),
         P(TOK + HEAD, None),
     )
-    return jax.shard_map(
-        body, mesh=split_mesh, in_specs=placed, out_specs=P(TOK + HEAD, None), check_vma=False
-    )
+    return jax.shard_map(body, mesh=split_mesh, in_specs=placed, out_specs=P(TOK + HEAD, None), check_vma=False)

time: 209 us -> 196 us (0.938)
  waiting for transfers between devices: 95.1 us -> 57.7 us
  blocking collectives: 43.1 us -> 60.4 us
  local copies, waits for them, and re-layouts: 3.96 us -> 8.49 us
  starting transfers between devices: 9.44 us -> 12.5 us
    all_gather x1 -> x0, waiting for transfers between devices: 28 us -> none  [body(): lax.all_gather(tokens, HEAD, axis=0, tiled=True).astype(jnp.float32)]
    all_to_all x0 -> x2, blocking collectives: none -> 13.9 us  [the longest x1 7.47 us: body(): lax.all_to_all(head_terms.reshape(core_count, y_count * local_rows, D), '...]
    all_gather x1, waiting for transfers between devices: 9.71 us -> 0.02 us  [body(): full_merge_weight = lax.all_gather(merge_weight, TOK, axis=1, tiled=True)]
    all_to_all x1 -> x2, starting transfers between devices: 4.79 us -> 8.97 us  [the longest x1 4.51 us: body(): lax.all_to_all(chip_rows.reshape(y_count, local_rows, D), 'hy', split_axi...]
    broadcast_in_dim x0 -> x2, local copies, waits for them, and re-layouts: none -> 4.08 us  [the longest x1 2.37 us: body(): jnp.broadcast_to(tokens[None], (y_count,) + tokens.shape)]
    reduce_sum x1 -> x2, other arithmetic: 2.5 us -> 6.13 us  [the longest x1 4.33 us: body(): jnp.sum(head_terms.astype(jnp.float32), axis=0).astype(jnp.bfloat16)]
    all_to_all x1, blocking collectives: 24.8 us -> 28.1 us  [body(): lax.all_to_all(send_rows, TOK, split_axis=0, concat_axis=0, tiled=True)]
    reduce_sum x1, other arithmetic: 2.62 us -> 0.52 us  [layer_norm(): average = jnp.mean(values, axis=-1, keepdims=True)]
  transfers between devices with their start and end apart: 4 -> 4, of which waited for: 4 -> 3; matrix products, arithmetic and copies ran while one was open for 18% -> 21% of each run, Pallas kernels for 0% -> 0%
where the time goes in v9:
time: 196 us; the launch traced here: 195 us
  blocking collectives  60.4 us (31%)
  waiting for transfers between devices  57.7 us (29%)
  matrix products  22.2 us (11%)
  other arithmetic  19.7 us (10%)
  between operations  13.7 us (7%)
  starting transfers between devices  12.5 us (6%)
  local copies, waits for them, and re-layouts  8.49 us (4%)
    all_to_all x1, blocking collectives, body(): lax.all_to_all(send_rows, TOK, split_axis=0, concat_axis=0, tiled=True)  28.1 us
    all_to_all x1, waiting for transfers between devices, body(): lax.all_to_all(chip_rows.reshape(y_count, local_rows, D), 'hy', split_axi...  22.8 us
    all_to_all x1, waiting for transfers between devices, body(): lax.all_to_all(jnp.broadcast_to(tokens[None], (y_count,) + tokens.shape),...  18.9 us
    all_to_all x1, waiting for transfers between devices, body(): lax.all_to_all(chip_terms.reshape(y_count, merged_count, -1), 'hy', split...  15.3 us
    all_to_all x1, blocking collectives, body(): lax.all_to_all(window_rows.reshape(local_rows // 4, 4 * D), HEAD, split_a...  12 us
    sub x1, matrix products, query_block(): exponent = jnp.where(allowed[None], jnp.exp(masked - row_top), 0.0)  8.44 us
    all_to_all x1, blocking collectives, body(): lax.all_to_all(head_terms.reshape(core_count, y_count * local_rows, D), '...  7.47 us
    all_to_all x1, blocking collectives, body(): lax.all_to_all(jnp.broadcast_to(by_y[None], (core_count,) + by_y.shape),...  6.47 us
  transfers between devices with their start and end apart: 4, of which 3 were waited for; matrix products, arithmetic and copies ran while one was open for 21% of the time, Pallas kernels for 0%

profile of v9, /device:TPU:32, one launch (start us, length us, event | category | flops | bytes accessed | tf_op | source)
XLA Modules:
  0.0 194.7 jit_solution(14200134837164620286)
XLA Ops:
  7.3 2.4 %broadcast_in_dim.97 = bf16[4,128,1664]{2,1,0:T(8,128)(2,1)} broadcast(bf16[128,1664]{1,0:T(8,128)(2,1)} %param.11), dimensions={1,2} | broadcast | bytes 2129920 | tf_op jit(solution)/shard_map/broadcast_in_dim | solution.py:71
  9.7 4.5 %all-to-all-start = ((bf16[4,128,1664]{2,1,0:T(8,128)(2,1)}), bf16[4,128,1664]{2,1,0:T(8,128)(2,1)}, u32[]{:S(2)}, u32[]{:S(2)}) async-start(bf16[4,128,1664]{2,1,0:T(8,128)(2,1)} %broadcast_in_dim.97), calls=%async_computation | async-start | bytes 3407872 | tf_op jit(solution)/shard_map/all_to_all | solution.py:70
  15.3 2.3 %fusion.13 = pred[1024,1024]{0,1:T(8,128)(4,1)} fusion(s32[1024]{0:T(1024)S(1)} %copy-done.3, pred[1024]{0:T(1024)(128)(4,1)S(1)} %broadcast_compare_fusion), kind=kLoop, calls=%fused_computation.18 | loop fusion | flops 4194304 | bytes 1053696 | tf_op jit(solution)/shard_map/while/body/eval_jaxpr/and | solution.py:98
  17.6 18.9 %all-to-all-done = bf16[4,128,1664]{2,1,0:T(8,128)(2,1)} async-done(((bf16[4,128,1664]{2,1,0:T(8,128)(2,1)}), bf16[4,128,1664]{2,1,0:T(8,128)(2,1)}, u32[]{:S(2)}, u32[]{:S(2)}) %all-to-all-start) | async-done | bytes 1703968 | tf_op jit(solution)/shard_map/all_to_all | solution.py:70
  36.5 1.7 broadcast_in_dim.98
  38.2 6.5 %all_to_all.48 = bf16[2,4,128,1664]{3,2,1,0:T(8,128)(2,1)S(1)} all-to-all(bf16[2,4,128,1664]{3,2,1,0:T(8,128)(2,1)S(1)} %broadcast_in_dim.98), channel_id=1, replica_groups=mesh['tx'=4,'tz'=8,'hy'=4,'hc'=2] {'hc'}, dimensions={0} | all-to-all | bytes 6815744 | tf_op jit(solution)/shard_map/all_to_all | solution.py:73
  47.5 2.5 %fusion.47 = f32[1024,3,2,104]{0,3,2,1:T(8,128)S(1)} fusion(bf16[1024,1664,1,1]{1,0,3,2:T(8,128)(2,1)S(1)} %bitcast.72, bf16[3,2,104,1664]{3,2,1,0:T(8,128)(2,1)S(1)} %bitcast.68), kind=kOutput, calls=%fused_computation.76 | convolution fusion | flops 2126512128 | bytes 8040448 | tf_op jit(solution)/shard_map/dot_general | solution.py:77
  50.3 1.4 subtract_convert_fusion.1
  52.6 8.4 %fusion.42 = (f32[2,1024]{1,0:T(2,128)S(1)}, bf16[2,1024,1024]{1,2,0:T(8,128)(2,1)}) fusion(pred[1024,1024]{0,1:T(8,128)(4,1)} %fusion.13, bf16[1024,2,26]{0,2,1:T(8,128)(2,1)} %get-tuple-element.43, bf16[1024,2,26]{0,2,1:T(8,128)(2,1)} %get-tuple-element.44, bf16[1024,2,26]{0,2,1:T(8,128)(2,1)} %get-tuple-element.38, ...), kind=kOutput, calls=%fused_computation.75 | convolution fusion | flops 449463296 | bytes 6529024 | tf_op jit(solution)/shard_map/while/body/eval_jaxpr/sub | solution.py:106
  61.0 3.3 %fusion.21 = bf16[1024,2,104]{0,2,1:T(8,128)(2,1)S(1)} fusion(bf16[2,1024,1024]{1,2,0:T(8,128)(2,1)} %get-tuple-element.56, f32[1024,3,2,104]{0,3,2,1:T(8,128)} %copy-done.2, f32[1024,2]{0,1:T(2,128)S(1)} %bitcast.83), kind=kOutput, calls=%fused_computation.24 | convolution fusion | flops 436633600 | bytes 5054464 | tf_op jit(solution)/shard_map/while/body/eval_jaxpr/hqk,khd->qhd/dot_general | solution.py:108
  65.1 2.3 %convolution_convert_fusion.2 = bf16[1024,1664]{1,0:T(8,128)(2,1)S(1)} fusion(bf16[1024,208]{0,1:T(8,128)(2,1)S(1)} %reshape.349, bf16[208,1664]{1,0:T(8,128)(2,1)} %param.14), kind=kOutput, calls=%fused_computation.20 | convolution fusion | flops 710541312 | bytes 4526080 | tf_op jit(solution)/shard_map/dot_general | solution.py:121
  67.4 7.5 %all_to_all.49 = bf16[2,512,1664]{2,1,0:T(8,128)(2,1)} all-to-all(bf16[2,512,1664]{2,1,0:T(8,128)(2,1)S(1)} %bitcast.69), channel_id=1, replica_groups=mesh['tx'=4,'tz'=8,'hy'=4,'hc'=2] {'hc'}, dimensions={0} | all-to-all | bytes 6815744 | tf_op jit(solution)/shard_map/all_to_all | solution.py:124
  74.9 4.3 %reduce_sum.124 = bf16[512,1664]{1,0:T(8,128)(2,1)} reduce(bf16[2,512,1664]{2,1,0:T(8,128)(2,1)} %all_to_all.49, bf16[]{:T(256)} %constant.69.clone.1), dimensions={0}, to_apply=%region_8.9 | reduce | flops 851968 | bytes 5111810 | tf_op jit(solution)/shard_map/reduce_sum | solution.py:127
  79.2 4.5 %all-to-all-start.3 = ((bf16[4,128,1664]{2,1,0:T(8,128)(2,1)}), bf16[4,128,1664]{2,1,0:T(8,128)(2,1)}, u32[]{:S(2)}, u32[]{:S(2)}) async-start(bf16[4,128,1664]{2,1,0:T(8,128)(2,1)} %bitcast.70), calls=%async_computation.3 | async-start | bytes 3407872 | tf_op jit(solution)/shard_map/all_to_all | solution.py:128
  83.9 22.8 %all-to-all-done.3 = bf16[4,128,1664]{2,1,0:T(8,128)(2,1)} async-done(((bf16[4,128,1664]{2,1,0:T(8,128)(2,1)}), bf16[4,128,1664]{2,1,0:T(8,128)(2,1)}, u32[]{:S(2)}, u32[]{:S(2)}) %all-to-all-start.3) | async-done | bytes 1703968 | tf_op jit(solution)/shard_map/all_to_all | solution.py:128
  106.6 1.8 convert_reduce_fusion
  110.1 1.4 reshape.352
  111.7 12.0 %all_to_all.50 = bf16[32,8,832]{2,0,1:T(8,128)(2,1)S(1)} all-to-all(bf16[32,8,832]{2,0,1:T(8,128)(2,1)S(1)} %copy.56), channel_id=1, replica_groups=mesh['tx'=4,'tz'=8,'hy'=4,'hc'=2] {'hy','hc'}, dimensions={1} | all-to-all | bytes 851968 | tf_op jit(solution)/shard_map/all_to_all | solution.py:138
  123.8 5.4 %convolution_convert_fusion = bf16[256,4096]{1,0:T(8,128)(2,1)S(1)} fusion(bf16[256,832]{1,0:T(8,128)(2,1)S(1)} %bitcast.76, bf16[832,4096]{1,0:T(8,128)(2,1)} %all-gather.2.cloned.1.call-done), kind=kOutput, calls=%fused_computation.11 | convolution fusion | flops 1745879040 | bytes 9338880 | tf_op jit(solution)/shard_map/dot_general | solution.py:144
  129.2 6.3 %all_to_all.51 = bf16[2,128,4096]{2,1,0:T(8,128)(2,1)} all-to-all(bf16[2,128,4096]{2,1,0:T(8,128)(2,1)S(1)} %bitcast.73), channel_id=1, replica_groups=mesh['tx'=4,'tz'=8,'hy'=4,'hc'=2] {'hc'}, dimensions={0} | all-to-all | bytes 4194304 | tf_op jit(solution)/shard_map/all_to_all | solution.py:145
  135.5 3.3 %reduce_sum.128 = bf16[128,4096]{1,0:T(8,128)(2,1)} reduce(bf16[2,128,4096]{2,1,0:T(8,128)(2,1)} %all_to_all.51, bf16[]{:T(256)} %constant.69.clone.1), dimensions={0}, to_apply=%region_12.13 | reduce | flops 524288 | bytes 3145730 | tf_op jit(solution)/shard_map/reduce_sum | solution.py:152
  138.8 3.5 %all-to-all-start.6 = ((bf16[4,32,4096]{2,1,0:T(8,128)(2,1)}), bf16[4,32,4096]{2,1,0:T(8,128)(2,1)S(1)}, u32[]{:S(2)}, u32[]{:S(2)}) async-start(bf16[4,32,4096]{2,1,0:T(8,128)(2,1)} %bitcast.71), calls=%async_computation.6 | async-start | bytes 2097152 | tf_op jit(solution)/shard_map/all_to_all | solution.py:153
  142.6 15.3 %all-to-all-done.6 = bf16[4,32,4096]{2,1,0:T(8,128)(2,1)S(1)} async-done(((bf16[4,32,4096]{2,1,0:T(8,128)(2,1)}), bf16[4,32,4096]{2,1,0:T(8,128)(2,1)S(1)}, u32[]{:S(2)}, u32[]{:S(2)}) %all-to-all-start.6) | async-done | bytes 1048608 | tf_op jit(solution)/shard_map/all_to_all | solution.py:153
  158.8 28.1 %all_to_all.52 = bf16[32,2,4096]{2,1,0:T(2,128)(2,1)S(1)} all-to-all(bf16[32,2,4096]{2,1,0:T(2,128)(2,1)S(1)} %reshape.357), channel_id=1, replica_groups=mesh['tx'=4,'tz'=8,'hy'=4,'hc'=2] {'tx','tz'}, dimensions={0} | all-to-all | bytes 1048576 | tf_op jit(solution)/shard_map/all_to_all | solution.py:170
  (68 shorter events, 10.7 us)
Async XLA Ops:
  6.5 41.0 %copy-start = (bf16[3,208,1664]{2,1,0:T(8,128)(2,1)S(1)}, bf16[3,208,1664]{2,1,0:T(8,128)(2,1)}, u32[]{:S(2)}) copy-start(bf16[3,208,1664]{2,1,0:T(8,128)(2,1)} %param.13) | copy-start | bytes 6230020
  6.5 7.6 %copy-start.9 = (s32[2,4]{1,0:T(2,128)S(1)}, s32[2,4]{1,0:T(2,128)}, u32[]{:S(2)}) copy-start(s32[2,4]{1,0:T(2,128)} %param.17) | copy-start | bytes 100
  6.5 7.6 %copy-start.3 = (s32[1024]{0:T(1024)S(1)}, s32[1024]{0:T(1024)}, u32[]{:S(2)}) copy-start(s32[1024]{0:T(1024)} %param.18) | copy-start | bytes 12292
  6.5 7.7 %copy-start.5 = (s32[2,1024]{1,0:T(2,128)S(1)}, s32[2,1024]{1,0:T(2,128)}, u32[]{:S(2)}) copy-start(s32[2,1024]{1,0:T(2,128)} %param.19) | copy-start | bytes 24580
  6.5 7.8 %copy-start.7 = (s32[1024]{0:T(1024)S(1)}, s32[1024]{0:T(1024)}, u32[]{:S(2)}) copy-start(s32[1024]{0:T(1024)} %param.20) | copy-start | bytes 12292
  6.5 117.2 %all-gather.2.cloned.1.call-start = ((), (), s32[]{:S(2)}) async-start(), calls=%async_computation.8 | async-start | bytes 7028736 | tf_op jit(solution)/shard_map/all_gather | solution.py:67
  9.7 26.8 %all-to-all-start = ((bf16[4,128,1664]{2,1,0:T(8,128)(2,1)}), bf16[4,128,1664]{2,1,0:T(8,128)(2,1)}, u32[]{:S(2)}, u32[]{:S(2)}) async-start(bf16[4,128,1664]{2,1,0:T(8,128)(2,1)} %broadcast_in_dim.97), calls=%async_computation | async-start | bytes 3407872 | tf_op jit(solution)/shard_map/all_to_all | solution.py:70
  44.7 1.6 copy-start.4
  50.1 2.5 %copy-start.2 = (f32[1024,3,2,104]{0,3,2,1:T(8,128)}, f32[1024,3,2,104]{0,3,2,1:T(8,128)S(1)}, u32[]{:S(2)}) copy-start(f32[1024,3,2,104]{0,3,2,1:T(8,128)S(1)} %fusion.47) | copy-start | bytes 7667716
  74.9 8.9 %copy-start.6 = (f32[1664]{0:T(1024)S(1)}, f32[1664]{0:T(1024)}, u32[]{:S(2)}) copy-start(f32[1664]{0:T(1024)} %param.15) | copy-start | bytes 19972
  79.2 29.2 %copy-start.1 = (bf16[128,1664]{1,0:T(8,128)(2,1)S(1)}, bf16[128,1664]{1,0:T(8,128)(2,1)}, u32[]{:S(2)}) copy-start(bf16[128,1664]{1,0:T(8,128)(2,1)} %param.11) | copy-start | bytes 1277956
  79.2 27.4 %all-to-all-start.3 = ((bf16[4,128,1664]{2,1,0:T(8,128)(2,1)}), bf16[4,128,1664]{2,1,0:T(8,128)(2,1)}, u32[]{:S(2)}, u32[]{:S(2)}) async-start(bf16[4,128,1664]{2,1,0:T(8,128)(2,1)} %bitcast.70), calls=%async_computation.3 | async-start | bytes 3407872 | tf_op jit(solution)/shard_map/all_to_all | solution.py:128
  129.2 13.1 %copy-start.8 = (s32[32,1]{0,1:T(1,128)S(1)}, s32[32,1]{0,1:T(1,128)}, u32[]{:S(2)}) copy-start(s32[32,1]{0,1:T(1,128)} %param.21) | copy-start | bytes 388
  138.8 19.2 %all-to-all-start.6 = ((bf16[4,32,4096]{2,1,0:T(8,128)(2,1)}), bf16[4,32,4096]{2,1,0:T(8,128)(2,1)S(1)}, u32[]{:S(2)}, u32[]{:S(2)}) async-start(bf16[4,32,4096]{2,1,0:T(8,128)(2,1)} %bitcast.71), calls=%async_computation.6 | async-start | bytes 2097152 | tf_op jit(solution)/shard_map/all_to_all | solution.py:153
Sparse Core Ops, SparseCore 0:
  9.8 97.2 all-gather.1

commit v10 on v9

--- a/solution.py
+++ b/solution.py
@@ -135,9 +135,12 @@
     window_rows = ((stream - average) * lax.rsqrt(variance + EPSILON) * merge_gain).astype(
         jnp.bfloat16
     )
-    merged_slice = lax.all_to_all(
-        window_rows.reshape(local_rows // 4, 4 * D), HEAD, split_axis=1, concat_axis=0, tiled=True
-    )
+    window_rows = window_rows.reshape(local_rows // 4, y_count, core_count, -1)
+    window_rows = jnp.transpose(window_rows, (2, 1, 0, 3))
+    window_rows = lax.all_to_all(window_rows, "hc", split_axis=0, concat_axis=0, tiled=True)
+    window_rows = jnp.swapaxes(window_rows, 0, 1)
+    merged_slice = lax.all_to_all(window_rows, "hy", split_axis=0, concat_axis=0, tiled=True)
+    merged_slice = merged_slice.reshape(head_count * (local_rows // 4), -1)
     merged_count = local_rows // 4
     by_core = merged_slice.reshape(y_count, core_count, merged_count, -1)
     by_core = jnp.swapaxes(by_core, 0, 1).reshape(head_count * merged_count, -1)

time: 196 us -> 200 us (1.020)
  blocking collectives: 60.4 us -> 64.2 us
    all_to_all x1 -> x2, blocking collectives: 12 us -> 15.8 us  [the longest x1 11.7 us: body(): lax.all_to_all(window_rows, 'hy', split_axis=0, concat_axis=0, tiled=True)]
  transfers between devices with their start and end apart: 4 -> 4, of which waited for: 3 -> 3; matrix products, arithmetic and copies ran while one was open for 21% -> 20% of each run, Pallas kernels for 0% -> 0%
where the time goes in v10:
time: 200 us; the launch traced here: 199 us
  blocking collectives  64.2 us (32%)
  waiting for transfers between devices  57.7 us (29%)
  matrix products  22.2 us (11%)
  other arithmetic  20.1 us (10%)
  between operations  13.7 us (7%)
  starting transfers between devices  12.5 us (6%)
  local copies, waits for them, and re-layouts  8.74 us (4%)
    all_to_all x1, blocking collectives, body(): lax.all_to_all(send_rows, TOK, split_axis=0, concat_axis=0, tiled=True)  28.1 us
    all_to_all x1, waiting for transfers between devices, body(): lax.all_to_all(chip_rows.reshape(y_count, local_rows, D), 'hy', split_axi...  22.8 us
    all_to_all x1, waiting for transfers between devices, body(): lax.all_to_all(jnp.broadcast_to(tokens[None], (y_count,) + tokens.shape),...  18.9 us
    all_to_all x1, waiting for transfers between devices, body(): lax.all_to_all(chip_terms.reshape(y_count, merged_count, -1), 'hy', split...  15.3 us
    all_to_all x1, blocking collectives, body(): lax.all_to_all(window_rows, 'hy', split_axis=0, concat_axis=0, tiled=True)  11.7 us
    sub x1, matrix products, query_block(): exponent = jnp.where(allowed[None], jnp.exp(masked - row_top), 0.0)  8.44 us
    all_to_all x1, blocking collectives, body(): lax.all_to_all(head_terms.reshape(core_count, y_count * local_rows, D), '...  7.47 us
    all_to_all x1, blocking collectives, body(): lax.all_to_all(jnp.broadcast_to(by_y[None], (core_count,) + by_y.shape),...  6.47 us
  transfers between devices with their start and end apart: 4, of which 3 were waited for; matrix products, arithmetic and copies ran while one was open for 20% of the time, Pallas kernels for 0%

profile of v10, /device:TPU:32, one launch (start us, length us, event | category | flops | bytes accessed | tf_op | source)
XLA Modules:
  0.0 199.3 jit_solution(10565875028469033110)
XLA Ops:
  7.3 2.4 %broadcast_in_dim.97 = bf16[4,128,1664]{2,1,0:T(8,128)(2,1)} broadcast(bf16[128,1664]{1,0:T(8,128)(2,1)} %param.11), dimensions={1,2} | broadcast | bytes 2129920 | tf_op jit(solution)/shard_map/broadcast_in_dim | solution.py:71
  9.7 4.5 %all-to-all-start = ((bf16[4,128,1664]{2,1,0:T(8,128)(2,1)}), bf16[4,128,1664]{2,1,0:T(8,128)(2,1)}, u32[]{:S(2)}, u32[]{:S(2)}) async-start(bf16[4,128,1664]{2,1,0:T(8,128)(2,1)} %broadcast_in_dim.97), calls=%async_computation | async-start | bytes 3407872 | tf_op jit(solution)/shard_map/all_to_all | solution.py:70
  15.3 2.3 %fusion.13 = pred[1024,1024]{0,1:T(8,128)(4,1)} fusion(s32[1024]{0:T(1024)S(1)} %copy-done.3, pred[1024]{0:T(1024)(128)(4,1)S(1)} %broadcast_compare_fusion), kind=kLoop, calls=%fused_computation.18 | loop fusion | flops 4194304 | bytes 1053696 | tf_op jit(solution)/shard_map/while/body/eval_jaxpr/and | solution.py:98
  17.6 18.9 %all-to-all-done = bf16[4,128,1664]{2,1,0:T(8,128)(2,1)} async-done(((bf16[4,128,1664]{2,1,0:T(8,128)(2,1)}), bf16[4,128,1664]{2,1,0:T(8,128)(2,1)}, u32[]{:S(2)}, u32[]{:S(2)}) %all-to-all-start) | async-done | bytes 1703968 | tf_op jit(solution)/shard_map/all_to_all | solution.py:70
  36.5 1.7 broadcast_in_dim.98
  38.2 6.5 %all_to_all.45 = bf16[2,4,128,1664]{3,2,1,0:T(8,128)(2,1)S(1)} all-to-all(bf16[2,4,128,1664]{3,2,1,0:T(8,128)(2,1)S(1)} %broadcast_in_dim.98), channel_id=1, replica_groups=mesh['tx'=4,'tz'=8,'hy'=4,'hc'=2] {'hc'}, dimensions={0} | all-to-all | bytes 6815744 | tf_op jit(solution)/shard_map/all_to_all | solution.py:73
  47.5 2.5 %fusion.48 = f32[1024,3,2,104]{0,3,2,1:T(8,128)S(1)} fusion(bf16[1024,1664,1,1]{1,0,3,2:T(8,128)(2,1)S(1)} %bitcast.69, bf16[3,2,104,1664]{3,2,1,0:T(8,128)(2,1)S(1)} %bitcast.65), kind=kOutput, calls=%fused_computation.77 | convolution fusion | flops 2126512128 | bytes 8040448 | tf_op jit(solution)/shard_map/dot_general | solution.py:77
  52.6 8.4 %fusion.43 = (f32[2,1024]{1,0:T(2,128)S(1)}, bf16[2,1024,1024]{1,2,0:T(8,128)(2,1)}) fusion(pred[1024,1024]{0,1:T(8,128)(4,1)} %fusion.13, bf16[1024,2,26]{0,2,1:T(8,128)(2,1)} %get-tuple-element.43, bf16[1024,2,26]{0,2,1:T(8,128)(2,1)} %get-tuple-element.44, bf16[1024,2,26]{0,2,1:T(8,128)(2,1)} %get-tuple-element.38, ...), kind=kOutput, calls=%fused_computation.76 | convolution fusion | flops 449463296 | bytes 6529024 | tf_op jit(solution)/shard_map/while/body/eval_jaxpr/sub | solution.py:106
  61.0 3.3 %fusion.21 = bf16[1024,2,104]{0,2,1:T(8,128)(2,1)S(1)} fusion(bf16[2,1024,1024]{1,2,0:T(8,128)(2,1)} %get-tuple-element.56, f32[1024,3,2,104]{0,3,2,1:T(8,128)} %copy-done.2, f32[1024,2]{0,1:T(2,128)S(1)} %bitcast.79), kind=kOutput, calls=%fused_computation.24 | convolution fusion | flops 436633600 | bytes 5054464 | tf_op jit(solution)/shard_map/while/body/eval_jaxpr/hqk,khd->qhd/dot_general | solution.py:108
  65.1 2.3 %convolution_convert_fusion.2 = bf16[1024,1664]{1,0:T(8,128)(2,1)S(1)} fusion(bf16[1024,208]{0,1:T(8,128)(2,1)S(1)} %reshape.329, bf16[208,1664]{1,0:T(8,128)(2,1)} %param.14), kind=kOutput, calls=%fused_computation.20 | convolution fusion | flops 710541312 | bytes 4526080 | tf_op jit(solution)/shard_map/dot_general | solution.py:121
  67.4 7.5 %all_to_all.46 = bf16[2,512,1664]{2,1,0:T(8,128)(2,1)} all-to-all(bf16[2,512,1664]{2,1,0:T(8,128)(2,1)S(1)} %bitcast.66), channel_id=1, replica_groups=mesh['tx'=4,'tz'=8,'hy'=4,'hc'=2] {'hc'}, dimensions={0} | all-to-all | bytes 6815744 | tf_op jit(solution)/shard_map/all_to_all | solution.py:124
  74.9 4.3 %reduce_sum.124 = bf16[512,1664]{1,0:T(8,128)(2,1)} reduce(bf16[2,512,1664]{2,1,0:T(8,128)(2,1)} %all_to_all.46, bf16[]{:T(256)} %constant.69.clone.1), dimensions={0}, to_apply=%region_8.9 | reduce | flops 851968 | bytes 5111810 | tf_op jit(solution)/shard_map/reduce_sum | solution.py:127
  79.2 4.5 %all-to-all-start.3 = ((bf16[4,128,1664]{2,1,0:T(8,128)(2,1)}), bf16[4,128,1664]{2,1,0:T(8,128)(2,1)}, u32[]{:S(2)}, u32[]{:S(2)}) async-start(bf16[4,128,1664]{2,1,0:T(8,128)(2,1)} %bitcast.67), calls=%async_computation.3 | async-start | bytes 3407872 | tf_op jit(solution)/shard_map/all_to_all | solution.py:128
  83.8 22.8 %all-to-all-done.3 = bf16[4,128,1664]{2,1,0:T(8,128)(2,1)} async-done(((bf16[4,128,1664]{2,1,0:T(8,128)(2,1)}), bf16[4,128,1664]{2,1,0:T(8,128)(2,1)}, u32[]{:S(2)}, u32[]{:S(2)}) %all-to-all-start.3) | async-done | bytes 1703968 | tf_op jit(solution)/shard_map/all_to_all | solution.py:128
  106.6 1.8 convert_reduce_fusion
  109.5 1.8 reshape.332
  112.4 4.1 %all_to_all.47 = bf16[2,4,32,832]{3,1,2,0:T(4,128)(2,1)S(1)} all-to-all(bf16[2,4,32,832]{3,1,2,0:T(4,128)(2,1)S(1)} %copy.37), channel_id=1, replica_groups=mesh['tx'=4,'tz'=8,'hy'=4,'hc'=2] {'hc'}, dimensions={0} | all-to-all | bytes 851968 | tf_op jit(solution)/shard_map/all_to_all | solution.py:140
  116.5 11.7 %all_to_all.48 = bf16[4,2,32,832]{3,2,1,0:T(8,128)(2,1)S(1)} all-to-all(bf16[4,2,32,832]{3,2,1,0:T(8,128)(2,1)S(1)} %copy.38), channel_id=1, replica_groups=mesh['tx'=4,'tz'=8,'hy'=4,'hc'=2] {'hy'}, dimensions={0} | all-to-all | bytes 851968 | tf_op jit(solution)/shard_map/all_to_all | solution.py:142
  128.3 5.4 %convolution_convert_fusion = bf16[256,4096]{1,0:T(8,128)(2,1)S(1)} fusion(bf16[256,832]{1,0:T(8,128)(2,1)S(1)} %bitcast.74, bf16[832,4096]{1,0:T(8,128)(2,1)} %all-gather.2.cloned.1.call-done), kind=kOutput, calls=%fused_computation.11 | convolution fusion | flops 1745879040 | bytes 9338880 | tf_op jit(solution)/shard_map/dot_general | solution.py:147
  133.7 6.3 %all_to_all.49 = bf16[2,128,4096]{2,1,0:T(8,128)(2,1)} all-to-all(bf16[2,128,4096]{2,1,0:T(8,128)(2,1)S(1)} %bitcast.70), channel_id=1, replica_groups=mesh['tx'=4,'tz'=8,'hy'=4,'hc'=2] {'hc'}, dimensions={0} | all-to-all | bytes 4194304 | tf_op jit(solution)/shard_map/all_to_all | solution.py:148
  140.0 3.3 %reduce_sum.128 = bf16[128,4096]{1,0:T(8,128)(2,1)} reduce(bf16[2,128,4096]{2,1,0:T(8,128)(2,1)} %all_to_all.49, bf16[]{:T(256)} %constant.69.clone.1), dimensions={0}, to_apply=%region_12.13 | reduce | flops 524288 | bytes 3145730 | tf_op jit(solution)/shard_map/reduce_sum | solution.py:155
  143.3 3.5 %all-to-all-start.7 = ((bf16[4,32,4096]{2,1,0:T(8,128)(2,1)}), bf16[4,32,4096]{2,1,0:T(8,128)(2,1)S(1)}, u32[]{:S(2)}, u32[]{:S(2)}) async-start(bf16[4,32,4096]{2,1,0:T(8,128)(2,1)} %bitcast.68), calls=%async_computation.7 | async-start | bytes 2097152 | tf_op jit(solution)/shard_map/all_to_all | solution.py:156
  147.1 15.3 %all-to-all-done.7 = bf16[4,32,4096]{2,1,0:T(8,128)(2,1)S(1)} async-done(((bf16[4,32,4096]{2,1,0:T(8,128)(2,1)}), bf16[4,32,4096]{2,1,0:T(8,128)(2,1)S(1)}, u32[]{:S(2)}, u32[]{:S(2)}) %all-to-all-start.7) | async-done | bytes 1048608 | tf_op jit(solution)/shard_map/all_to_all | solution.py:156
  163.3 28.1 %all_to_all.50 = bf16[32,2,4096]{2,1,0:T(2,128)(2,1)S(1)} all-to-all(bf16[32,2,4096]{2,1,0:T(2,128)(2,1)S(1)} %reshape.336), channel_id=1, replica_groups=mesh['tx'=4,'tz'=8,'hy'=4,'hc'=2] {'tx','tz'}, dimensions={0} | all-to-all | bytes 1048576 | tf_op jit(solution)/shard_map/all_to_all | solution.py:173
  (62 shorter events, 12.3 us)
Async XLA Ops:
  6.5 41.0 %copy-start = (bf16[3,208,1664]{2,1,0:T(8,128)(2,1)S(1)}, bf16[3,208,1664]{2,1,0:T(8,128)(2,1)}, u32[]{:S(2)}) copy-start(bf16[3,208,1664]{2,1,0:T(8,128)(2,1)} %param.13) | copy-start | bytes 6230020
  6.5 7.6 %copy-start.9 = (s32[2,4]{1,0:T(2,128)S(1)}, s32[2,4]{1,0:T(2,128)}, u32[]{:S(2)}) copy-start(s32[2,4]{1,0:T(2,128)} %param.17) | copy-start | bytes 100
  6.5 7.6 %copy-start.3 = (s32[1024]{0:T(1024)S(1)}, s32[1024]{0:T(1024)}, u32[]{:S(2)}) copy-start(s32[1024]{0:T(1024)} %param.18) | copy-start | bytes 12292
  6.5 7.7 %copy-start.5 = (s32[2,1024]{1,0:T(2,128)S(1)}, s32[2,1024]{1,0:T(2,128)}, u32[]{:S(2)}) copy-start(s32[2,1024]{1,0:T(2,128)} %param.19) | copy-start | bytes 24580
  6.5 7.8 %copy-start.7 = (s32[1024]{0:T(1024)S(1)}, s32[1024]{0:T(1024)}, u32[]{:S(2)}) copy-start(s32[1024]{0:T(1024)} %param.20) | copy-start | bytes 12292
  6.5 121.8 %all-gather.2.cloned.1.call-start = ((), (), s32[]{:S(2)}) async-start(), calls=%async_computation.9 | async-start | bytes 7028736 | tf_op jit(solution)/shard_map/all_gather | solution.py:67
  9.7 26.8 %all-to-all-start = ((bf16[4,128,1664]{2,1,0:T(8,128)(2,1)}), bf16[4,128,1664]{2,1,0:T(8,128)(2,1)}, u32[]{:S(2)}, u32[]{:S(2)}) async-start(bf16[4,128,1664]{2,1,0:T(8,128)(2,1)} %broadcast_in_dim.97), calls=%async_computation | async-start | bytes 3407872 | tf_op jit(solution)/shard_map/all_to_all | solution.py:70
  44.7 1.6 copy-start.4
  50.1 2.5 %copy-start.2 = (f32[1024,3,2,104]{0,3,2,1:T(8,128)}, f32[1024,3,2,104]{0,3,2,1:T(8,128)S(1)}, u32[]{:S(2)}) copy-start(f32[1024,3,2,104]{0,3,2,1:T(8,128)S(1)} %fusion.48) | copy-start | bytes 7667716
  74.9 8.9 %copy-start.6 = (f32[1664]{0:T(1024)S(1)}, f32[1664]{0:T(1024)}, u32[]{:S(2)}) copy-start(f32[1664]{0:T(1024)} %param.15) | copy-start | bytes 19972
  79.2 29.2 %copy-start.1 = (bf16[128,1664]{1,0:T(8,128)(2,1)S(1)}, bf16[128,1664]{1,0:T(8,128)(2,1)}, u32[]{:S(2)}) copy-start(bf16[128,1664]{1,0:T(8,128)(2,1)} %param.11) | copy-start | bytes 1277956
  79.2 27.4 %all-to-all-start.3 = ((bf16[4,128,1664]{2,1,0:T(8,128)(2,1)}), bf16[4,128,1664]{2,1,0:T(8,128)(2,1)}, u32[]{:S(2)}, u32[]{:S(2)}) async-start(bf16[4,128,1664]{2,1,0:T(8,128)(2,1)} %bitcast.67), calls=%async_computation.3 | async-start | bytes 3407872 | tf_op jit(solution)/shard_map/all_to_all | solution.py:128
  133.7 13.1 %copy-start.8 = (s32[32,1]{0,1:T(1,128)S(1)}, s32[32,1]{0,1:T(1,128)}, u32[]{:S(2)}) copy-start(s32[32,1]{0,1:T(1,128)} %param.21) | copy-start | bytes 388
  143.3 19.2 %all-to-all-start.7 = ((bf16[4,32,4096]{2,1,0:T(8,128)(2,1)}), bf16[4,32,4096]{2,1,0:T(8,128)(2,1)S(1)}, u32[]{:S(2)}, u32[]{:S(2)}) async-start(bf16[4,32,4096]{2,1,0:T(8,128)(2,1)} %bitcast.68), calls=%async_computation.7 | async-start | bytes 2097152 | tf_op jit(solution)/shard_map/all_to_all | solution.py:156
Sparse Core Ops, SparseCore 0:
  9.8 97.2 all-gather.1

commit v11 on v9

--- a/solution.py
+++ b/solution.py
@@ -70,10 +70,12 @@
     by_y = lax.all_to_all(
         jnp.broadcast_to(tokens[None], (y_count,) + tokens.shape), "hy", split_axis=0, concat_axis=0, tiled=True
     )
-    by_core = lax.all_to_all(
-        jnp.broadcast_to(by_y[None], (core_count,) + by_y.shape), "hc", split_axis=0, concat_axis=0, tiled=True
+    partner = lax.ppermute(by_y, "hc", [(0, 1), (1, 0)])
+    first_core = lax.axis_index("hc") == 0
+    pair = jnp.stack(
+        [jnp.where(first_core, by_y, partner), jnp.where(first_core, partner, by_y)], axis=1
     )
-    gathered_tokens = jnp.swapaxes(by_core, 0, 1).reshape(group_len, D)
+    gathered_tokens = pair.reshape(group_len, D)
     projected_rows = lax.dot_general(
         layer_norm(gathered_tokens.astype(jnp.float32), attn_gain).astype(jnp.bfloat16),
         stacked_weight,

time: 196 us -> 193 us (0.985)
  blocking collectives: 60.4 us -> 54 us
  waiting for transfers between devices: 57.7 us -> 62.1 us
    all_to_all x1 -> x0, blocking collectives: 6.47 us -> none  [body(): lax.all_to_all(jnp.broadcast_to(by_y[None], (core_count,) + by_y.shape),...]
    all_to_all x1, waiting for transfers between devices: 18.9 us -> 22.4 us  [body(): lax.all_to_all(jnp.broadcast_to(tokens[None], (y_count,) + tokens.shape),...]
  transfers between devices with their start and end apart: 4 -> 5, of which waited for: 3 -> 4; matrix products, arithmetic and copies ran while one was open for 21% -> 20% of each run, Pallas kernels for 0% -> 0%
where the time goes in v11:
time: 193 us; the launch traced here: 192 us
  waiting for transfers between devices  62.1 us (32%)
  blocking collectives  54 us (28%)
  matrix products  21.6 us (11%)
  other arithmetic  21.2 us (11%)
  between operations  13.7 us (7%)
  starting transfers between devices  12.5 us (6%)
  local copies, waits for them, and re-layouts  6.8 us (4%)
    all_to_all x1, blocking collectives, body(): lax.all_to_all(send_rows, TOK, split_axis=0, concat_axis=0, tiled=True)  28.2 us
    all_to_all x1, waiting for transfers between devices, body(): lax.all_to_all(chip_rows.reshape(y_count, local_rows, D), 'hy', split_axi...  22.6 us
    all_to_all x1, waiting for transfers between devices, body(): lax.all_to_all(jnp.broadcast_to(tokens[None], (y_count,) + tokens.shape),...  22.4 us
    all_to_all x1, waiting for transfers between devices, body(): lax.all_to_all(chip_terms.reshape(y_count, merged_count, -1), 'hy', split...  15.3 us
    all_to_all x1, blocking collectives, body(): lax.all_to_all(window_rows.reshape(local_rows // 4, 4 * D), HEAD, split_a...  12 us
    sub x1, matrix products, query_block(): exponent = jnp.where(allowed[None], jnp.exp(masked - row_top), 0.0)  7.91 us
    all_to_all x1, blocking collectives, body(): lax.all_to_all(head_terms.reshape(core_count, y_count * local_rows, D), '...  7.47 us
    all_to_all x1, blocking collectives, body(): lax.all_to_all(column_terms.astype(jnp.bfloat16).reshape(core_count, y_co...  6.31 us
  transfers between devices with their start and end apart: 5, of which 4 were waited for; matrix products, arithmetic and copies ran while one was open for 20% of the time, Pallas kernels for 0%

profile of v11, /device:TPU:32, one launch (start us, length us, event | category | flops | bytes accessed | tf_op | source)
XLA Modules:
  0.0 191.9 jit_solution(17434539769837475775)
XLA Ops:
  7.3 2.4 %broadcast_in_dim.91 = bf16[4,128,1664]{2,1,0:T(8,128)(2,1)} broadcast(bf16[128,1664]{1,0:T(8,128)(2,1)} %param.11), dimensions={1,2} | broadcast | bytes 2129920 | tf_op jit(solution)/shard_map/broadcast_in_dim | solution.py:71
  9.7 4.5 %all-to-all-start = ((bf16[4,128,1664]{2,1,0:T(8,128)(2,1)}), bf16[4,128,1664]{2,1,0:T(8,128)(2,1)}, u32[]{:S(2)}, u32[]{:S(2)}) async-start(bf16[4,128,1664]{2,1,0:T(8,128)(2,1)} %broadcast_in_dim.91), calls=%async_computation | async-start | bytes 3407872 | tf_op jit(solution)/shard_map/all_to_all | solution.py:70
  14.1 22.4 %all-to-all-done = bf16[4,128,1664]{2,1,0:T(8,128)(2,1)} async-done(((bf16[4,128,1664]{2,1,0:T(8,128)(2,1)}), bf16[4,128,1664]{2,1,0:T(8,128)(2,1)}, u32[]{:S(2)}, u32[]{:S(2)}) %all-to-all-start) | async-done | bytes 1703968 | tf_op jit(solution)/shard_map/all_to_all | solution.py:70
  37.7 1.5 fusion.13
  40.3 1.9 select_bitcast_fusion.1
  44.0 1.4 fusion.6
  45.4 2.5 %fusion.47 = f32[1024,3,2,104]{0,3,2,1:T(8,128)S(1)} fusion(bf16[1024,1664,1,1]{1,0,3,2:T(8,128)(2,1)S(1)} %bitcast.65, bf16[3,2,104,1664]{3,2,1,0:T(8,128)(2,1)S(1)} %bitcast.61), kind=kOutput, calls=%fused_computation.79 | convolution fusion | flops 2126512128 | bytes 8040448 | tf_op jit(solution)/shard_map/dot_general | solution.py:79
  48.1 1.4 subtract_convert_fusion.1
  50.6 7.9 %fusion.42 = (f32[2,1024]{1,0:T(2,128)S(1)}, bf16[2,1024,1024]{1,2,0:T(8,128)(2,1)}) fusion(pred[1024,1024]{0,1:T(8,128)(4,1)S(1)} %fusion.13, bf16[1024,2,26]{0,2,1:T(8,128)(2,1)} %get-tuple-element.45, bf16[1024,2,26]{0,2,1:T(8,128)(2,1)} %get-tuple-element.46, bf16[1024,2,26]{0,2,1:T(8,128)(2,1)} %get-tuple-element.40, ...), kind=kOutput, calls=%fused_computation.78 | convolution fusion | flops 449463296 | bytes 6529024 | tf_op jit(solution)/shard_map/while/body/eval_jaxpr/sub | solution.py:108
  58.5 3.2 %fusion.21 = bf16[1024,2,104]{0,2,1:T(8,128)(2,1)S(1)} fusion(bf16[2,1024,1024]{1,2,0:T(8,128)(2,1)} %get-tuple-element.58, f32[1024,3,2,104]{0,3,2,1:T(8,128)} %copy-done.2, f32[1024,2]{0,1:T(2,128)S(1)} %bitcast.76), kind=kOutput, calls=%fused_computation.27 | convolution fusion | flops 436633600 | bytes 5054464 | tf_op jit(solution)/shard_map/while/body/eval_jaxpr/hqk,khd->qhd/dot_general | solution.py:110
  62.5 2.3 %convolution_convert_fusion.2 = bf16[1024,1664]{1,0:T(8,128)(2,1)S(1)} fusion(bf16[1024,208]{0,1:T(8,128)(2,1)S(1)} %reshape.402, bf16[208,1664]{1,0:T(8,128)(2,1)} %param.14), kind=kOutput, calls=%fused_computation.20 | convolution fusion | flops 710541312 | bytes 4526080 | tf_op jit(solution)/shard_map/dot_general | solution.py:123
  64.8 7.5 %all_to_all.43 = bf16[2,512,1664]{2,1,0:T(8,128)(2,1)} all-to-all(bf16[2,512,1664]{2,1,0:T(8,128)(2,1)S(1)} %bitcast.62), channel_id=1, replica_groups=mesh['tx'=4,'tz'=8,'hy'=4,'hc'=2] {'hc'}, dimensions={0} | all-to-all | bytes 6815744 | tf_op jit(solution)/shard_map/all_to_all | solution.py:126
  72.2 4.3 %reduce_sum.124 = bf16[512,1664]{1,0:T(8,128)(2,1)} reduce(bf16[2,512,1664]{2,1,0:T(8,128)(2,1)} %all_to_all.43, bf16[]{:T(256)} %constant.73.clone.1), dimensions={0}, to_apply=%region_8.9 | reduce | flops 851968 | bytes 5111810 | tf_op jit(solution)/shard_map/reduce_sum | solution.py:129
  76.5 4.5 %all-to-all-start.2 = ((bf16[4,128,1664]{2,1,0:T(8,128)(2,1)}), bf16[4,128,1664]{2,1,0:T(8,128)(2,1)}, u32[]{:S(2)}, u32[]{:S(2)}) async-start(bf16[4,128,1664]{2,1,0:T(8,128)(2,1)} %bitcast.63), calls=%async_computation.2 | async-start | bytes 3407872 | tf_op jit(solution)/shard_map/all_to_all | solution.py:130
  81.2 22.6 %all-to-all-done.2 = bf16[4,128,1664]{2,1,0:T(8,128)(2,1)} async-done(((bf16[4,128,1664]{2,1,0:T(8,128)(2,1)}), bf16[4,128,1664]{2,1,0:T(8,128)(2,1)}, u32[]{:S(2)}, u32[]{:S(2)}) %all-to-all-start.2) | async-done | bytes 1703968 | tf_op jit(solution)/shard_map/all_to_all | solution.py:130
  103.8 1.8 convert_reduce_fusion.1
  107.2 1.4 reshape.405
  108.9 12.0 %all_to_all.44 = bf16[32,8,832]{2,0,1:T(8,128)(2,1)S(1)} all-to-all(bf16[32,8,832]{2,0,1:T(8,128)(2,1)S(1)} %copy.52), channel_id=1, replica_groups=mesh['tx'=4,'tz'=8,'hy'=4,'hc'=2] {'hy','hc'}, dimensions={1} | all-to-all | bytes 851968 | tf_op jit(solution)/shard_map/all_to_all | solution.py:140
  121.0 5.4 %convolution_convert_fusion = bf16[256,4096]{1,0:T(8,128)(2,1)S(1)} fusion(bf16[256,832]{1,0:T(8,128)(2,1)S(1)} %bitcast.69, bf16[832,4096]{1,0:T(8,128)(2,1)} %all-gather.2.cloned.1.call-done), kind=kOutput, calls=%fused_computation.11 | convolution fusion | flops 1745879040 | bytes 9338880 | tf_op jit(solution)/shard_map/dot_general | solution.py:146
  126.3 6.3 %all_to_all.45 = bf16[2,128,4096]{2,1,0:T(8,128)(2,1)} all-to-all(bf16[2,128,4096]{2,1,0:T(8,128)(2,1)S(1)} %bitcast.66), channel_id=1, replica_groups=mesh['tx'=4,'tz'=8,'hy'=4,'hc'=2] {'hc'}, dimensions={0} | all-to-all | bytes 4194304 | tf_op jit(solution)/shard_map/all_to_all | solution.py:147
  132.6 3.3 %reduce_sum.128 = bf16[128,4096]{1,0:T(8,128)(2,1)} reduce(bf16[2,128,4096]{2,1,0:T(8,128)(2,1)} %all_to_all.45, bf16[]{:T(256)} %constant.73.clone.1), dimensions={0}, to_apply=%region_12.13 | reduce | flops 524288 | bytes 3145730 | tf_op jit(solution)/shard_map/reduce_sum | solution.py:154
  135.9 3.5 %all-to-all-start.5 = ((bf16[4,32,4096]{2,1,0:T(8,128)(2,1)}), bf16[4,32,4096]{2,1,0:T(8,128)(2,1)S(1)}, u32[]{:S(2)}, u32[]{:S(2)}) async-start(bf16[4,32,4096]{2,1,0:T(8,128)(2,1)} %bitcast.64), calls=%async_computation.5 | async-start | bytes 2097152 | tf_op jit(solution)/shard_map/all_to_all | solution.py:155
  139.8 15.3 %all-to-all-done.5 = bf16[4,32,4096]{2,1,0:T(8,128)(2,1)S(1)} async-done(((bf16[4,32,4096]{2,1,0:T(8,128)(2,1)}), bf16[4,32,4096]{2,1,0:T(8,128)(2,1)S(1)}, u32[]{:S(2)}, u32[]{:S(2)}) %all-to-all-start.5) | async-done | bytes 1048608 | tf_op jit(solution)/shard_map/all_to_all | solution.py:155
  155.9 28.2 %all_to_all.46 = bf16[32,2,4096]{2,1,0:T(2,128)(2,1)S(1)} all-to-all(bf16[32,2,4096]{2,1,0:T(2,128)(2,1)S(1)} %reshape.410), channel_id=1, replica_groups=mesh['tx'=4,'tz'=8,'hy'=4,'hc'=2] {'tx','tz'}, dimensions={0} | all-to-all | bytes 1048576 | tf_op jit(solution)/shard_map/all_to_all | solution.py:172
  (69 shorter events, 10.8 us)
Async XLA Ops:
  6.5 38.9 %copy-start = (bf16[3,208,1664]{2,1,0:T(8,128)(2,1)S(1)}, bf16[3,208,1664]{2,1,0:T(8,128)(2,1)}, u32[]{:S(2)}) copy-start(bf16[3,208,1664]{2,1,0:T(8,128)(2,1)} %param.13) | copy-start | bytes 6230020
  6.5 7.6 %copy-start.9 = (s32[2,4]{1,0:T(2,128)S(1)}, s32[2,4]{1,0:T(2,128)}, u32[]{:S(2)}) copy-start(s32[2,4]{1,0:T(2,128)} %param.17) | copy-start | bytes 100
  6.5 30.0 %copy-start.3 = (s32[1024]{0:T(1024)S(1)}, s32[1024]{0:T(1024)}, u32[]{:S(2)}) copy-start(s32[1024]{0:T(1024)} %param.18) | copy-start | bytes 12292
  6.5 30.1 %copy-start.5 = (s32[2,1024]{1,0:T(2,128)S(1)}, s32[2,1024]{1,0:T(2,128)}, u32[]{:S(2)}) copy-start(s32[2,1024]{1,0:T(2,128)} %param.19) | copy-start | bytes 24580
  6.5 30.2 %copy-start.7 = (s32[1024]{0:T(1024)S(1)}, s32[1024]{0:T(1024)}, u32[]{:S(2)}) copy-start(s32[1024]{0:T(1024)} %param.20) | copy-start | bytes 12292
  6.5 114.4 %all-gather.2.cloned.1.call-start = ((), (), s32[]{:S(2)}) async-start(), calls=%async_computation.7 | async-start | bytes 7028736 | tf_op jit(solution)/shard_map/all_gather | solution.py:67
  9.7 26.8 %all-to-all-start = ((bf16[4,128,1664]{2,1,0:T(8,128)(2,1)}), bf16[4,128,1664]{2,1,0:T(8,128)(2,1)}, u32[]{:S(2)}, u32[]{:S(2)}) async-start(bf16[4,128,1664]{2,1,0:T(8,128)(2,1)} %broadcast_in_dim.91), calls=%async_computation | async-start | bytes 3407872 | tf_op jit(solution)/shard_map/all_to_all | solution.py:70
  36.5 3.8 %collective-permute-start = (bf16[4,128,1664]{2,1,0:T(8,128)(2,1)}, bf16[4,128,1664]{2,1,0:T(8,128)(2,1)S(1)}, u32[]{:S(2)}, u32[]{:S(2)}) collective-permute-start(bf16[4,128,1664]{2,1,0:T(8,128)(2,1)} %all-to-all-done), channel_id=1, source_target_pairs={{0,1},{1,0},{2,3},{3,2},{4,5},{5,4},{6,7},{7,6},{8,9},{9,8},{10,11... | collective-permute-start | bytes 5111816 | tf_op jit(solution)/shard_map/ppermute | solution.py:73
  42.2 1.7 copy-start.4
  47.9 2.6 %copy-start.2 = (f32[1024,3,2,104]{0,3,2,1:T(8,128)}, f32[1024,3,2,104]{0,3,2,1:T(8,128)S(1)}, u32[]{:S(2)}) copy-start(f32[1024,3,2,104]{0,3,2,1:T(8,128)S(1)} %fusion.47) | copy-start | bytes 7667716
  72.2 8.8 %copy-start.6 = (f32[1664]{0:T(1024)S(1)}, f32[1664]{0:T(1024)}, u32[]{:S(2)}) copy-start(f32[1664]{0:T(1024)} %param.15) | copy-start | bytes 19972
  76.5 29.1 %copy-start.1 = (bf16[128,1664]{1,0:T(8,128)(2,1)S(1)}, bf16[128,1664]{1,0:T(8,128)(2,1)}, u32[]{:S(2)}) copy-start(bf16[128,1664]{1,0:T(8,128)(2,1)} %param.11) | copy-start | bytes 1277956
  76.5 27.3 %all-to-all-start.2 = ((bf16[4,128,1664]{2,1,0:T(8,128)(2,1)}), bf16[4,128,1664]{2,1,0:T(8,128)(2,1)}, u32[]{:S(2)}, u32[]{:S(2)}) async-start(bf16[4,128,1664]{2,1,0:T(8,128)(2,1)} %bitcast.63), calls=%async_computation.2 | async-start | bytes 3407872 | tf_op jit(solution)/shard_map/all_to_all | solution.py:130
  132.6 6.8 %copy-start.8 = (s32[32,1]{0,1:T(1,128)S(1)}, s32[32,1]{0,1:T(1,128)}, u32[]{:S(2)}) copy-start(s32[32,1]{0,1:T(1,128)} %param.21) | copy-start | bytes 388
  135.9 19.2 %all-to-all-start.5 = ((bf16[4,32,4096]{2,1,0:T(8,128)(2,1)}), bf16[4,32,4096]{2,1,0:T(8,128)(2,1)S(1)}, u32[]{:S(2)}, u32[]{:S(2)}) async-start(bf16[4,32,4096]{2,1,0:T(8,128)(2,1)} %bitcast.64), calls=%async_computation.5 | async-start | bytes 2097152 | tf_op jit(solution)/shard_map/all_to_all | solution.py:155
Sparse Core Ops, SparseCore 0:
  9.8 97.3 all-gather.1

commit v12 on v11

--- a/solution.py
+++ b/solution.py
@@ -35,6 +35,13 @@
         pieces.append(leading * cosine - trailing * sine_val)
         pieces.append(leading * sine_val + trailing * cosine)
     return jnp.concatenate(pieces, axis=-1)
+
+
+def pair_sum(terms, first_core):
+    away = jnp.where(first_core, terms[1], terms[0])
+    kept = jnp.where(first_core, terms[0], terms[1])
+    arrived = lax.ppermute(away, "hc", [(0, 1), (1, 0)])
+    return (kept.astype(jnp.float32) + arrived.astype(jnp.float32)).astype(jnp.bfloat16)
 
 
 def body(
@@ -123,10 +130,8 @@
     head_terms = jnp.dot(heads_by_core, out_weight, preferred_element_type=jnp.float32).astype(
         jnp.bfloat16
     )
-    head_terms = lax.all_to_all(
-        head_terms.reshape(core_count, y_count * local_rows, D), "hc", split_axis=0, concat_axis=0, tiled=True
-    )
-    chip_rows = jnp.sum(head_terms.astype(jnp.float32), axis=0).astype(jnp.bfloat16)
+    head_terms = head_terms.reshape(core_count, y_count * local_rows, D)
+    chip_rows = pair_sum(head_terms, first_core)
     chip_rows = lax.all_to_all(
         chip_rows.reshape(y_count, local_rows, D), "hy", split_axis=0, concat_axis=0, tiled=True
     )
@@ -144,14 +149,8 @@
     by_core = merged_slice.reshape(y_count, core_count, merged_count, -1)
     by_core = jnp.swapaxes(by_core, 0, 1).reshape(head_count * merged_count, -1)
     column_terms = jnp.dot(by_core, full_merge_weight, preferred_element_type=jnp.float32)
-    column_terms = lax.all_to_all(
-        column_terms.astype(jnp.bfloat16).reshape(core_count, y_count * merged_count, -1),
-        "hc",
-        split_axis=0,
-        concat_axis=0,
-        tiled=True,
-    )
-    chip_terms = jnp.sum(column_terms.astype(jnp.float32), axis=0).astype(jnp.bfloat16)
+    column_terms = column_terms.astype(jnp.bfloat16).reshape(core_count, y_count * merged_count, -1)
+    chip_terms = pair_sum(column_terms, first_core)
     chip_terms = lax.all_to_all(
         chip_terms.reshape(y_count, merged_count, -1), "hy", split_axis=0, concat_axis=0, tiled=True
     )
@@ -191,4 +190,6 @@
         P(TOK),
         P(TOK + HEAD, None),
     )
-    return jax.shard_map(body, mesh=split_mesh, in_specs=placed, out_specs=P(TOK + HEAD, None), check_vma=False)
+    return jax.shard_map(
+        body, mesh=split_mesh, in_specs=placed, out_specs=P(TOK + HEAD, None), check_vma=False
+    )

time: 193 us -> 181 us (0.938)
  blocking collectives: 54 us -> 39.6 us
  waiting for transfers between devices: 62.1 us -> 67.4 us
  other arithmetic: 21.2 us -> 17.4 us
    all_to_all x2 -> x0, blocking collectives: 13.8 us -> none  [the longest x1 7.47 us: body(): lax.all_to_all(head_terms.reshape(core_count, y_count * local_rows, D), '...]
    reduce_sum x2 -> x0, other arithmetic: 7.53 us -> none  [the longest x1 4.26 us: body(): jnp.sum(head_terms.astype(jnp.float32), axis=0).astype(jnp.bfloat16)]
    ppermute x0 -> x2, waiting for transfers between devices: none -> 6.15 us  [pair_sum(): arrived = lax.ppermute(away, 'hc', [(0, 1), (1, 0)])]
    convert_element_type x0 -> x2, other arithmetic: none -> 3.37 us  [pair_sum(): (kept.astype(jnp.float32) + arrived.astype(jnp.float32)).astype(jnp.bfloa...]
  transfers between devices with their start and end apart: 5 -> 7, of which waited for: 4 -> 7; matrix products, arithmetic and copies ran while one was open for 20% -> 19% of each run, Pallas kernels for 0% -> 0%
where the time goes in v12:
time: 181 us; the launch traced here: 180 us
  waiting for transfers between devices  67.4 us (37%)
  blocking collectives  39.6 us (22%)
  matrix products  21.6 us (12%)
  other arithmetic  17.4 us (10%)
  between operations  13.8 us (8%)
  starting transfers between devices  13.5 us (7%)
  local copies, waits for them, and re-layouts  6.93 us (4%)
    all_to_all x1, blocking collectives, body(): lax.all_to_all(send_rows, TOK, split_axis=0, concat_axis=0, tiled=True)  27.4 us
    all_to_all x1, waiting for transfers between devices, body(): lax.all_to_all(chip_rows.reshape(y_count, local_rows, D), 'hy', split_axi...  22.6 us
    all_to_all x1, waiting for transfers between devices, body(): lax.all_to_all(jnp.broadcast_to(tokens[None], (y_count,) + tokens.shape),...  21.6 us
    all_to_all x1, waiting for transfers between devices, body(): lax.all_to_all(chip_terms.reshape(y_count, merged_count, -1), 'hy', split...  15.1 us
    all_to_all x1, blocking collectives, body(): lax.all_to_all(window_rows.reshape(local_rows // 4, 4 * D), HEAD, split_a...  12.2 us
    sub x1, matrix products, query_block(): exponent = jnp.where(allowed[None], jnp.exp(masked - row_top), 0.0)  7.9 us
    ppermute x2, waiting for transfers between devices, pair_sum(): arrived = lax.ppermute(away, 'hc', [(0, 1), (1, 0)])  6.15 us
    dot_general x1, matrix products, body(): jnp.dot(by_core, full_merge_weight, preferred_element_type=jnp.float32)  5.35 us
  transfers between devices with their start and end apart: 7, of which 7 were waited for; matrix products, arithmetic and copies ran while one was open for 19% of the time, Pallas kernels for 0%

profile of v12, /device:TPU:32, one launch (start us, length us, event | category | flops | bytes accessed | tf_op | source)
XLA Modules:
  0.0 180.2 jit_solution(1228726160815660547)
XLA Ops:
  6.5 2.5 %broadcast_in_dim.91 = bf16[4,128,1664]{2,1,0:T(8,128)(2,1)} broadcast(bf16[128,1664]{1,0:T(8,128)(2,1)} %param.11), dimensions={1,2} | broadcast | bytes 2129920 | tf_op jit(solution)/shard_map/broadcast_in_dim | solution.py:78
  9.1 4.5 %all-to-all-start = ((bf16[4,128,1664]{2,1,0:T(8,128)(2,1)}), bf16[4,128,1664]{2,1,0:T(8,128)(2,1)}, u32[]{:S(2)}, u32[]{:S(2)}) async-start(bf16[4,128,1664]{2,1,0:T(8,128)(2,1)} %broadcast_in_dim.91), calls=%async_computation | async-start | bytes 3407872 | tf_op jit(solution)/shard_map/all_to_all | solution.py:77
  14.3 21.6 %all-to-all-done = bf16[4,128,1664]{2,1,0:T(8,128)(2,1)} async-done(((bf16[4,128,1664]{2,1,0:T(8,128)(2,1)}), bf16[4,128,1664]{2,1,0:T(8,128)(2,1)}, u32[]{:S(2)}, u32[]{:S(2)}) %all-to-all-start) | async-done | bytes 1703968 | tf_op jit(solution)/shard_map/all_to_all | solution.py:77
  37.1 1.5 fusion.13
  39.7 1.9 %select_bitcast_fusion.1 = (bf16[4,1,128,1664]{3,2,1,0:T(8,128)(2,1)S(1)}, bf16[4,1,128,1664]{3,2,1,0:T(8,128)(2,1)S(1)}) fusion(bf16[4,128,1664]{2,1,0:T(8,128)(2,1)} %all-to-all-done, bf16[4,128,1664]{2,1,0:T(8,128)(2,1)S(1)} %collective-permute-done, pred[]{:T(512)S(6)} %eq.102), kind=kLoop, calls=%fused_computation.26 | loop fusion | flops 1703936 | bytes 6815745 | tf_op jit(solution)/shard_map/stack | solution.py:82
  43.4 1.4 fusion.6
  44.8 2.5 %fusion.47 = f32[1024,3,2,104]{0,3,2,1:T(8,128)S(1)} fusion(bf16[1024,1664,1,1]{1,0,3,2:T(8,128)(2,1)S(1)} %bitcast.61, bf16[3,2,104,1664]{3,2,1,0:T(8,128)(2,1)S(1)} %bitcast.59), kind=kOutput, calls=%fused_computation.83 | convolution fusion | flops 2126512128 | bytes 8040448 | tf_op jit(solution)/shard_map/dot_general | solution.py:86
  47.6 1.4 subtract_convert_fusion.1
  50.0 7.9 %fusion.42 = (f32[2,1024]{1,0:T(2,128)S(1)}, bf16[2,1024,1024]{1,2,0:T(8,128)(2,1)}) fusion(pred[1024,1024]{0,1:T(8,128)(4,1)S(1)} %fusion.13, bf16[1024,2,26]{0,2,1:T(8,128)(2,1)} %get-tuple-element.45, bf16[1024,2,26]{0,2,1:T(8,128)(2,1)} %get-tuple-element.46, bf16[1024,2,26]{0,2,1:T(8,128)(2,1)} %get-tuple-element.40, ...), kind=kOutput, calls=%fused_computation.82 | convolution fusion | flops 449463296 | bytes 6529024 | tf_op jit(solution)/shard_map/while/body/eval_jaxpr/sub | solution.py:115
  57.9 3.2 %fusion.21 = bf16[1024,2,104]{0,2,1:T(8,128)(2,1)S(1)} fusion(bf16[2,1024,1024]{1,2,0:T(8,128)(2,1)} %get-tuple-element.58, f32[1024,3,2,104]{0,3,2,1:T(8,128)} %copy-done.2, f32[1024,2]{0,1:T(2,128)S(1)} %bitcast.71), kind=kOutput, calls=%fused_computation.30 | convolution fusion | flops 436633600 | bytes 5054464 | tf_op jit(solution)/shard_map/while/body/eval_jaxpr/hqk,khd->qhd/dot_general | solution.py:117
  61.9 2.3 %convolution_convert_fusion.2 = bf16[1024,1664]{1,0:T(8,128)(2,1)S(1)} fusion(bf16[1024,208]{0,1:T(8,128)(2,1)S(1)} %reshape.406, bf16[208,1664]{1,0:T(8,128)(2,1)} %param.14), kind=kOutput, calls=%fused_computation.20 | convolution fusion | flops 710541312 | bytes 4526080 | tf_op jit(solution)/shard_map/dot_general | solution.py:130
  64.6 3.5 %collective-permute-done.1 = bf16[512,1664]{1,0:T(8,128)(2,1)S(1)} collective-permute-done((bf16[512,1664]{1,0:T(8,128)(2,1)S(1)}, bf16[512,1664]{1,0:T(8,128)(2,1)S(1)}, u32[]{:S(2)}, u32[]{:S(2)}) %collective-permute-start.1) | collective-permute-done | bytes 1703968 | tf_op jit(solution)/shard_map/ppermute | solution.py:43
  68.1 1.9 %add_convert_fusion = bf16[512,1664]{1,0:T(8,128)(2,1)} fusion(bf16[512,1664]{1,0:T(8,128)(2,1)S(1)} %collective-permute-done.1, pred[]{:T(512)S(6)} %eq.102, bf16[1024,1664]{1,0:T(8,128)(2,1)S(1)} %convolution_convert_fusion.2), kind=kLoop, calls=%fused_computation.23 | loop fusion | flops 4259840 | bytes 6815745 | tf_op jit(solution)/shard_map/convert_element_type | solution.py:44
  69.9 4.5 %all-to-all-start.1 = ((bf16[4,128,1664]{2,1,0:T(8,128)(2,1)}), bf16[4,128,1664]{2,1,0:T(8,128)(2,1)}, u32[]{:S(2)}, u32[]{:S(2)}) async-start(bf16[4,128,1664]{2,1,0:T(8,128)(2,1)} %bitcast.60), calls=%async_computation.1 | async-start | bytes 3407872 | tf_op jit(solution)/shard_map/all_to_all | solution.py:135
  74.6 22.6 %all-to-all-done.1 = bf16[4,128,1664]{2,1,0:T(8,128)(2,1)} async-done(((bf16[4,128,1664]{2,1,0:T(8,128)(2,1)}), bf16[4,128,1664]{2,1,0:T(8,128)(2,1)}, u32[]{:S(2)}, u32[]{:S(2)}) %all-to-all-start.1) | async-done | bytes 1703968 | tf_op jit(solution)/shard_map/all_to_all | solution.py:135
  97.2 1.9 %convert_reduce_fusion.1 = f32[128,1664]{1,0:T(8,128)S(1)} fusion(bf16[4,128,1664]{2,1,0:T(8,128)(2,1)} %all-to-all-done.1), kind=kLoop, calls=%fused_computation.22 | loop fusion | flops 1490944 | bytes 2555904 | tf_op jit(solution)/shard_map/reduce_sum | solution.py:138
  100.7 1.4 reshape.408
  102.4 12.2 %all_to_all.33 = bf16[32,8,832]{2,0,1:T(8,128)(2,1)S(1)} all-to-all(bf16[32,8,832]{2,0,1:T(8,128)(2,1)S(1)} %copy.52), channel_id=1, replica_groups=mesh['tx'=4,'tz'=8,'hy'=4,'hc'=2] {'hy','hc'}, dimensions={1} | all-to-all | bytes 851968 | tf_op jit(solution)/shard_map/all_to_all | solution.py:145
  114.8 5.4 %convolution_convert_fusion = bf16[256,4096]{1,0:T(8,128)(2,1)S(1)} fusion(bf16[256,832]{1,0:T(8,128)(2,1)S(1)} %bitcast.64, bf16[832,4096]{1,0:T(8,128)(2,1)} %all-gather.2.cloned.1.call-done), kind=kOutput, calls=%fused_computation.11 | convolution fusion | flops 1745879040 | bytes 9338880 | tf_op jit(solution)/shard_map/dot_general | solution.py:151
  120.4 2.6 %collective-permute-done.2 = bf16[128,4096]{1,0:T(8,128)(2,1)S(1)} collective-permute-done((bf16[128,4096]{1,0:T(8,128)(2,1)S(1)}, bf16[128,4096]{1,0:T(8,128)(2,1)S(1)}, u32[]{:S(2)}, u32[]{:S(2)}) %collective-permute-start.2) | collective-permute-done | bytes 1048608 | tf_op jit(solution)/shard_map/ppermute | solution.py:43
  123.1 1.5 add_convert_fusion.1
  124.5 4.2 %all-to-all-start.3 = ((bf16[4,32,4096]{2,1,0:T(8,128)(2,1)}), bf16[4,32,4096]{2,1,0:T(8,128)(2,1)S(1)}, u32[]{:S(2)}, u32[]{:S(2)}) async-start(bf16[4,32,4096]{2,1,0:T(8,128)(2,1)} %bitcast.25), calls=%async_computation.3 | async-start | bytes 2097152 | tf_op jit(solution)/shard_map/all_to_all | solution.py:154
  129.1 15.1 %all-to-all-done.3 = bf16[4,32,4096]{2,1,0:T(8,128)(2,1)S(1)} async-done(((bf16[4,32,4096]{2,1,0:T(8,128)(2,1)}), bf16[4,32,4096]{2,1,0:T(8,128)(2,1)S(1)}, u32[]{:S(2)}, u32[]{:S(2)}) %all-to-all-start.3) | async-done | bytes 1048608 | tf_op jit(solution)/shard_map/all_to_all | solution.py:154
  145.0 27.4 %all_to_all.34 = bf16[32,2,4096]{2,1,0:T(2,128)(2,1)S(1)} all-to-all(bf16[32,2,4096]{2,1,0:T(2,128)(2,1)S(1)} %reshape.412), channel_id=1, replica_groups=mesh['tx'=4,'tz'=8,'hy'=4,'hc'=2] {'tx','tz'}, dimensions={0} | all-to-all | bytes 1048576 | tf_op jit(solution)/shard_map/all_to_all | solution.py:171
  (73 shorter events, 11.5 us)
Async XLA Ops:
  6.5 38.3 %copy-start = (bf16[3,208,1664]{2,1,0:T(8,128)(2,1)S(1)}, bf16[3,208,1664]{2,1,0:T(8,128)(2,1)}, u32[]{:S(2)}) copy-start(bf16[3,208,1664]{2,1,0:T(8,128)(2,1)} %param.13) | copy-start | bytes 6230020
  6.5 7.7 %copy-start.9 = (s32[2,4]{1,0:T(2,128)S(1)}, s32[2,4]{1,0:T(2,128)}, u32[]{:S(2)}) copy-start(s32[2,4]{1,0:T(2,128)} %param.17) | copy-start | bytes 100
  6.5 29.4 %copy-start.3 = (s32[1024]{0:T(1024)S(1)}, s32[1024]{0:T(1024)}, u32[]{:S(2)}) copy-start(s32[1024]{0:T(1024)} %param.18) | copy-start | bytes 12292
  6.5 29.5 %copy-start.5 = (s32[2,1024]{1,0:T(2,128)S(1)}, s32[2,1024]{1,0:T(2,128)}, u32[]{:S(2)}) copy-start(s32[2,1024]{1,0:T(2,128)} %param.19) | copy-start | bytes 24580
  6.5 29.6 %copy-start.7 = (s32[1024]{0:T(1024)S(1)}, s32[1024]{0:T(1024)}, u32[]{:S(2)}) copy-start(s32[1024]{0:T(1024)} %param.20) | copy-start | bytes 12292
  9.1 26.8 %all-to-all-start = ((bf16[4,128,1664]{2,1,0:T(8,128)(2,1)}), bf16[4,128,1664]{2,1,0:T(8,128)(2,1)}, u32[]{:S(2)}, u32[]{:S(2)}) async-start(bf16[4,128,1664]{2,1,0:T(8,128)(2,1)} %broadcast_in_dim.91), calls=%async_computation | async-start | bytes 3407872 | tf_op jit(solution)/shard_map/all_to_all | solution.py:77
  13.5 101.3 %all-gather.2.cloned.1.call-start = ((), (), s32[]{:S(2)}) async-start(), calls=%async_computation.5 | async-start | bytes 7028736 | tf_op jit(solution)/shard_map/all_gather | solution.py:74
  35.9 3.8 %collective-permute-start = (bf16[4,128,1664]{2,1,0:T(8,128)(2,1)}, bf16[4,128,1664]{2,1,0:T(8,128)(2,1)S(1)}, u32[]{:S(2)}, u32[]{:S(2)}) collective-permute-start(bf16[4,128,1664]{2,1,0:T(8,128)(2,1)} %all-to-all-done), channel_id=1, source_target_pairs={{0,1},{1,0},{2,3},{3,2},{4,5},{5,4},{6,7},{7,6},{8,9},{9,8},{10,11... | collective-permute-start | bytes 5111816 | tf_op jit(solution)/shard_map/ppermute | solution.py:80
  41.6 1.7 copy-start.4
  47.4 2.6 %copy-start.2 = (f32[1024,3,2,104]{0,3,2,1:T(8,128)}, f32[1024,3,2,104]{0,3,2,1:T(8,128)S(1)}, u32[]{:S(2)}) copy-start(f32[1024,3,2,104]{0,3,2,1:T(8,128)S(1)} %fusion.47) | copy-start | bytes 7667716
  64.4 3.7 %collective-permute-start.1 = (bf16[512,1664]{1,0:T(8,128)(2,1)S(1)}, bf16[512,1664]{1,0:T(8,128)(2,1)S(1)}, u32[]{:S(2)}, u32[]{:S(2)}) collective-permute-start(bf16[512,1664]{1,0:T(8,128)(2,1)S(1)} %broadcast_select_fusion), channel_id=1, source_target_pairs={{0,1},{1,0},{2,3},{3,2},{4,5},{5,4},{6,7},{7,6},{8,9},{9,8},{10,11... | collective-permute-start | bytes 5111816 | tf_op jit(solution)/shard_map/ppermute | solution.py:43
  69.9 4.5 %copy-start.6 = (f32[1664]{0:T(1024)S(1)}, f32[1664]{0:T(1024)}, u32[]{:S(2)}) copy-start(f32[1664]{0:T(1024)} %param.15) | copy-start | bytes 19972
  69.9 29.2 %copy-start.1 = (bf16[128,1664]{1,0:T(8,128)(2,1)S(1)}, bf16[128,1664]{1,0:T(8,128)(2,1)}, u32[]{:S(2)}) copy-start(bf16[128,1664]{1,0:T(8,128)(2,1)} %param.11) | copy-start | bytes 1277956
  69.9 27.3 %all-to-all-start.1 = ((bf16[4,128,1664]{2,1,0:T(8,128)(2,1)}), bf16[4,128,1664]{2,1,0:T(8,128)(2,1)}, u32[]{:S(2)}, u32[]{:S(2)}) async-start(bf16[4,128,1664]{2,1,0:T(8,128)(2,1)} %bitcast.60), calls=%async_computation.1 | async-start | bytes 3407872 | tf_op jit(solution)/shard_map/all_to_all | solution.py:135
  120.3 8.5 %copy-start.8 = (s32[32,1]{0,1:T(1,128)S(1)}, s32[32,1]{0,1:T(1,128)}, u32[]{:S(2)}) copy-start(s32[32,1]{0,1:T(1,128)} %param.21) | copy-start | bytes 388
  120.3 2.7 %collective-permute-start.2 = (bf16[128,4096]{1,0:T(8,128)(2,1)S(1)}, bf16[128,4096]{1,0:T(8,128)(2,1)S(1)}, u32[]{:S(2)}, u32[]{:S(2)}) collective-permute-start(bf16[128,4096]{1,0:T(8,128)(2,1)S(1)} %broadcast_select_fusion.1), channel_id=1, source_target_pairs={{0,1},{1,0},{2,3},{3,2},{4,5},{5,4},{6,7},{7,6},{8,9},{9,8},{10,11... | collective-permute-start | bytes 3145736 | tf_op jit(solution)/shard_map/ppermute | solution.py:43
  124.5 19.6 %all-to-all-start.3 = ((bf16[4,32,4096]{2,1,0:T(8,128)(2,1)}), bf16[4,32,4096]{2,1,0:T(8,128)(2,1)S(1)}, u32[]{:S(2)}, u32[]{:S(2)}) async-start(bf16[4,32,4096]{2,1,0:T(8,128)(2,1)} %bitcast.25), calls=%async_computation.3 | async-start | bytes 2097152 | tf_op jit(solution)/shard_map/all_to_all | solution.py:154
Sparse Core Ops, SparseCore 0:
  16.8 97.9 all-gather.1

commit v13 on v12

--- a/solution.py
+++ b/solution.py
@@ -142,9 +142,18 @@
     window_rows = ((stream - average) * lax.rsqrt(variance + EPSILON) * merge_gain).astype(
         jnp.bfloat16
     )
-    merged_slice = lax.all_to_all(
-        window_rows.reshape(local_rows // 4, 4 * D), HEAD, split_axis=1, concat_axis=0, tiled=True
-    )
+    window_rows = window_rows.reshape(local_rows // 4, y_count, core_count, -1)
+    window_rows = jnp.transpose(window_rows, (2, 1, 0, 3))
+    kept_rows = jnp.where(first_core, window_rows[0], window_rows[1])
+    arrived_rows = lax.ppermute(
+        jnp.where(first_core, window_rows[1], window_rows[0]), "hc", [(0, 1), (1, 0)]
+    )
+    core_rows = jnp.stack(
+        [jnp.where(first_core, kept_rows, arrived_rows), jnp.where(first_core, arrived_rows, kept_rows)],
+        axis=1,
+    )
+    merged_slice = lax.all_to_all(core_rows, "hy", split_axis=0, concat_axis=0, tiled=True)
+    merged_slice = merged_slice.reshape(head_count * (local_rows // 4), -1)
     merged_count = local_rows // 4
     by_core = merged_slice.reshape(y_count, core_count, merged_count, -1)
     by_core = jnp.swapaxes(by_core, 0, 1).reshape(head_count * merged_count, -1)
@@ -190,6 +199,4 @@
         P(TOK),
         P(TOK + HEAD, None),
     )
-    return jax.shard_map(
-        body, mesh=split_mesh, in_specs=placed, out_specs=P(TOK + HEAD, None), check_vma=False
-    )
+    return jax.shard_map(body, mesh=split_mesh, in_specs=placed, out_specs=P(TOK + HEAD, None), check_vma=False)

time: 181 us -> 184 us (1.017)
  transfers between devices with their start and end apart: 7 -> 8, of which waited for: 7 -> 7; matrix products, arithmetic and copies ran while one was open for 19% -> 20% of each run, Pallas kernels for 0% -> 0%
where the time goes in v13:
time: 184 us; the launch traced here: 183 us
  waiting for transfers between devices  68.8 us (37%)
  blocking collectives  39.7 us (22%)
  matrix products  21.6 us (12%)
  other arithmetic  19 us (10%)
  between operations  13.8 us (8%)
  starting transfers between devices  13.1 us (7%)
  local copies, waits for them, and re-layouts  7.02 us (4%)
    all_to_all x1, blocking collectives, body(): lax.all_to_all(send_rows, TOK, split_axis=0, concat_axis=0, tiled=True)  28 us
    all_to_all x1, waiting for transfers between devices, body(): lax.all_to_all(chip_rows.reshape(y_count, local_rows, D), 'hy', split_axi...  22.4 us
    all_to_all x1, waiting for transfers between devices, body(): lax.all_to_all(jnp.broadcast_to(tokens[None], (y_count,) + tokens.shape),...  21.6 us
    all_to_all x1, waiting for transfers between devices, body(): lax.all_to_all(chip_terms.reshape(y_count, merged_count, -1), 'hy', split...  15.3 us
    all_to_all x1, blocking collectives, body(): lax.all_to_all(core_rows, 'hy', split_axis=0, concat_axis=0, tiled=True)  11.7 us
    sub x1, matrix products, query_block(): exponent = jnp.where(allowed[None], jnp.exp(masked - row_top), 0.0)  7.9 us
    ppermute x2, waiting for transfers between devices, pair_sum(): arrived = lax.ppermute(away, 'hc', [(0, 1), (1, 0)])  6.15 us
    dot_general x1, matrix products, body(): jnp.dot(by_core, full_merge_weight, preferred_element_type=jnp.float32)  5.35 us
  transfers between devices with their start and end apart: 8, of which 7 were waited for; matrix products, arithmetic and copies ran while one was open for 20% of the time, Pallas kernels for 0%

profile of v13, /device:TPU:32, one launch (start us, length us, event | category | flops | bytes accessed | tf_op | source)
XLA Modules:
  0.0 183.1 jit_solution(3484712337948702800)
XLA Ops:
  6.5 2.5 %broadcast_in_dim.91 = bf16[4,128,1664]{2,1,0:T(8,128)(2,1)} broadcast(bf16[128,1664]{1,0:T(8,128)(2,1)} %param.11), dimensions={1,2} | broadcast | bytes 2129920 | tf_op jit(solution)/shard_map/broadcast_in_dim | solution.py:78
  9.1 4.5 %all-to-all-start = ((bf16[4,128,1664]{2,1,0:T(8,128)(2,1)}), bf16[4,128,1664]{2,1,0:T(8,128)(2,1)}, u32[]{:S(2)}, u32[]{:S(2)}) async-start(bf16[4,128,1664]{2,1,0:T(8,128)(2,1)} %broadcast_in_dim.91), calls=%async_computation | async-start | bytes 3407872 | tf_op jit(solution)/shard_map/all_to_all | solution.py:77
  14.3 21.6 %all-to-all-done = bf16[4,128,1664]{2,1,0:T(8,128)(2,1)} async-done(((bf16[4,128,1664]{2,1,0:T(8,128)(2,1)}), bf16[4,128,1664]{2,1,0:T(8,128)(2,1)}, u32[]{:S(2)}, u32[]{:S(2)}) %all-to-all-start) | async-done | bytes 1703968 | tf_op jit(solution)/shard_map/all_to_all | solution.py:77
  37.1 1.5 fusion.13
  39.7 1.9 %select_bitcast_fusion.1 = (bf16[4,1,128,1664]{3,2,1,0:T(8,128)(2,1)S(1)}, bf16[4,1,128,1664]{3,2,1,0:T(8,128)(2,1)S(1)}) fusion(bf16[4,128,1664]{2,1,0:T(8,128)(2,1)} %all-to-all-done, bf16[4,128,1664]{2,1,0:T(8,128)(2,1)S(1)} %collective-permute-done, pred[]{:T(512)S(6)} %eq.102), kind=kLoop, calls=%fused_computation.26 | loop fusion | flops 1703936 | bytes 6815745 | tf_op jit(solution)/shard_map/stack | solution.py:82
  44.8 2.5 %fusion.50 = f32[1024,3,2,104]{0,3,2,1:T(8,128)S(1)} fusion(bf16[1024,1664,1,1]{1,0,3,2:T(8,128)(2,1)S(1)} %bitcast.71, bf16[3,2,104,1664]{3,2,1,0:T(8,128)(2,1)S(1)} %bitcast.69), kind=kOutput, calls=%fused_computation.92 | convolution fusion | flops 2126512128 | bytes 8040448 | tf_op jit(solution)/shard_map/dot_general | solution.py:86
  47.6 1.4 subtract_convert_fusion.1
  50.0 7.9 %fusion.45 = (f32[2,1024]{1,0:T(2,128)S(1)}, bf16[2,1024,1024]{1,2,0:T(8,128)(2,1)}) fusion(pred[1024,1024]{0,1:T(8,128)(4,1)S(1)} %fusion.13, bf16[1024,2,26]{0,2,1:T(8,128)(2,1)} %get-tuple-element.45, bf16[1024,2,26]{0,2,1:T(8,128)(2,1)} %get-tuple-element.46, bf16[1024,2,26]{0,2,1:T(8,128)(2,1)} %get-tuple-element.40, ...), kind=kOutput, calls=%fused_computation.91 | convolution fusion | flops 449463296 | bytes 6529024 | tf_op jit(solution)/shard_map/while/body/eval_jaxpr/sub | solution.py:115
  57.9 3.2 %fusion.21 = bf16[1024,2,104]{0,2,1:T(8,128)(2,1)S(1)} fusion(bf16[2,1024,1024]{1,2,0:T(8,128)(2,1)} %get-tuple-element.62, f32[1024,3,2,104]{0,3,2,1:T(8,128)} %copy-done.2, f32[1024,2]{0,1:T(2,128)S(1)} %bitcast.80), kind=kOutput, calls=%fused_computation.30 | convolution fusion | flops 436633600 | bytes 5054464 | tf_op jit(solution)/shard_map/while/body/eval_jaxpr/hqk,khd->qhd/dot_general | solution.py:117
  61.9 2.3 %convolution_convert_fusion.2 = bf16[1024,1664]{1,0:T(8,128)(2,1)S(1)} fusion(bf16[1024,208]{0,1:T(8,128)(2,1)S(1)} %reshape.390, bf16[208,1664]{1,0:T(8,128)(2,1)} %param.14), kind=kOutput, calls=%fused_computation.20 | convolution fusion | flops 710541312 | bytes 4526080 | tf_op jit(solution)/shard_map/dot_general | solution.py:130
  64.6 3.5 %collective-permute-done.1 = bf16[512,1664]{1,0:T(8,128)(2,1)S(1)} collective-permute-done((bf16[512,1664]{1,0:T(8,128)(2,1)S(1)}, bf16[512,1664]{1,0:T(8,128)(2,1)S(1)}, u32[]{:S(2)}, u32[]{:S(2)}) %collective-permute-start.1) | collective-permute-done | bytes 1703968 | tf_op jit(solution)/shard_map/ppermute | solution.py:43
  68.1 1.9 %add_convert_fusion = bf16[512,1664]{1,0:T(8,128)(2,1)} fusion(bf16[512,1664]{1,0:T(8,128)(2,1)S(1)} %collective-permute-done.1, pred[]{:T(512)S(6)} %eq.102, bf16[1024,1664]{1,0:T(8,128)(2,1)S(1)} %convolution_convert_fusion.2), kind=kLoop, calls=%fused_computation.23 | loop fusion | flops 4259840 | bytes 6815745 | tf_op jit(solution)/shard_map/convert_element_type | solution.py:44
  69.9 4.7 %all-to-all-start.1 = ((bf16[4,128,1664]{2,1,0:T(8,128)(2,1)}), bf16[4,128,1664]{2,1,0:T(8,128)(2,1)}, u32[]{:S(2)}, u32[]{:S(2)}) async-start(bf16[4,128,1664]{2,1,0:T(8,128)(2,1)} %bitcast.70), calls=%async_computation.1 | async-start | bytes 3407872 | tf_op jit(solution)/shard_map/all_to_all | solution.py:135
  74.8 22.4 %all-to-all-done.1 = bf16[4,128,1664]{2,1,0:T(8,128)(2,1)} async-done(((bf16[4,128,1664]{2,1,0:T(8,128)(2,1)}), bf16[4,128,1664]{2,1,0:T(8,128)(2,1)}, u32[]{:S(2)}, u32[]{:S(2)}) %all-to-all-start.1) | async-done | bytes 1703968 | tf_op jit(solution)/shard_map/all_to_all | solution.py:135
  97.2 1.9 %convert_reduce_fusion.1 = f32[128,1664]{1,0:T(8,128)S(1)} fusion(bf16[4,128,1664]{2,1,0:T(8,128)(2,1)} %all-to-all-done.1), kind=kLoop, calls=%fused_computation.22 | loop fusion | flops 1490944 | bytes 2555904 | tf_op jit(solution)/shard_map/reduce_sum | solution.py:138
  100.2 1.8 %reshape.392 = f32[32,4,2,832]{3,2,1,0:T(2,128)S(1)} reshape(f32[128,1664]{1,0:T(8,128)} %get-tuple-element.28) | data formatting | bytes 1703936 | tf_op jit(solution)/shard_map/reshape | solution.py:139
  104.1 1.5 collective-permute-done.2
  105.7 11.7 %all_to_all.25 = bf16[4,2,32,832]{3,2,1,0:T(8,128)(2,1)S(1)} all-to-all(bf16[4,2,32,832]{3,2,1,0:T(8,128)(2,1)S(1)} %copy.46), channel_id=1, replica_groups=mesh['tx'=4,'tz'=8,'hy'=4,'hc'=2] {'hy'}, dimensions={0} | all-to-all | bytes 851968 | tf_op jit(solution)/shard_map/all_to_all | solution.py:155
  117.5 5.4 %convolution_convert_fusion = bf16[256,4096]{1,0:T(8,128)(2,1)S(1)} fusion(bf16[256,832]{1,0:T(8,128)(2,1)S(1)} %bitcast.74, bf16[832,4096]{1,0:T(8,128)(2,1)} %all-gather.2.cloned.1.call-done), kind=kOutput, calls=%fused_computation.11 | convolution fusion | flops 1745879040 | bytes 9338880 | tf_op jit(solution)/shard_map/dot_general | solution.py:160
  123.1 2.6 %collective-permute-done.3 = bf16[128,4096]{1,0:T(8,128)(2,1)S(1)} collective-permute-done((bf16[128,4096]{1,0:T(8,128)(2,1)S(1)}, bf16[128,4096]{1,0:T(8,128)(2,1)S(1)}, u32[]{:S(2)}, u32[]{:S(2)}) %collective-permute-start.3) | collective-permute-done | bytes 1048608 | tf_op jit(solution)/shard_map/ppermute | solution.py:43
  125.8 1.5 add_convert_fusion.1
  127.3 3.5 %all-to-all-start.3 = ((bf16[4,32,4096]{2,1,0:T(8,128)(2,1)}), bf16[4,32,4096]{2,1,0:T(8,128)(2,1)S(1)}, u32[]{:S(2)}, u32[]{:S(2)}) async-start(bf16[4,32,4096]{2,1,0:T(8,128)(2,1)} %bitcast.26), calls=%async_computation.3 | async-start | bytes 2097152 | tf_op jit(solution)/shard_map/all_to_all | solution.py:163
  131.1 15.3 %all-to-all-done.3 = bf16[4,32,4096]{2,1,0:T(8,128)(2,1)S(1)} async-done(((bf16[4,32,4096]{2,1,0:T(8,128)(2,1)}), bf16[4,32,4096]{2,1,0:T(8,128)(2,1)S(1)}, u32[]{:S(2)}, u32[]{:S(2)}) %all-to-all-start.3) | async-done | bytes 1048608 | tf_op jit(solution)/shard_map/all_to_all | solution.py:163
  147.3 28.0 %all_to_all.26 = bf16[32,2,4096]{2,1,0:T(2,128)(2,1)S(1)} all-to-all(bf16[32,2,4096]{2,1,0:T(2,128)(2,1)S(1)} %reshape.395), channel_id=1, replica_groups=mesh['tx'=4,'tz'=8,'hy'=4,'hc'=2] {'tx','tz'}, dimensions={0} | all-to-all | bytes 1048576 | tf_op jit(solution)/shard_map/all_to_all | solution.py:180
  (71 shorter events, 14.1 us)
Async XLA Ops:
  6.5 38.3 %copy-start = (bf16[3,208,1664]{2,1,0:T(8,128)(2,1)S(1)}, bf16[3,208,1664]{2,1,0:T(8,128)(2,1)}, u32[]{:S(2)}) copy-start(bf16[3,208,1664]{2,1,0:T(8,128)(2,1)} %param.13) | copy-start | bytes 6230020
  6.5 7.7 %copy-start.9 = (s32[2,4]{1,0:T(2,128)S(1)}, s32[2,4]{1,0:T(2,128)}, u32[]{:S(2)}) copy-start(s32[2,4]{1,0:T(2,128)} %param.17) | copy-start | bytes 100
  6.5 29.4 %copy-start.3 = (s32[1024]{0:T(1024)S(1)}, s32[1024]{0:T(1024)}, u32[]{:S(2)}) copy-start(s32[1024]{0:T(1024)} %param.18) | copy-start | bytes 12292
  6.5 29.5 %copy-start.5 = (s32[2,1024]{1,0:T(2,128)S(1)}, s32[2,1024]{1,0:T(2,128)}, u32[]{:S(2)}) copy-start(s32[2,1024]{1,0:T(2,128)} %param.19) | copy-start | bytes 24580
  6.5 29.6 %copy-start.7 = (s32[1024]{0:T(1024)S(1)}, s32[1024]{0:T(1024)}, u32[]{:S(2)}) copy-start(s32[1024]{0:T(1024)} %param.20) | copy-start | bytes 12292
  9.1 26.8 %all-to-all-start = ((bf16[4,128,1664]{2,1,0:T(8,128)(2,1)}), bf16[4,128,1664]{2,1,0:T(8,128)(2,1)}, u32[]{:S(2)}, u32[]{:S(2)}) async-start(bf16[4,128,1664]{2,1,0:T(8,128)(2,1)} %broadcast_in_dim.91), calls=%async_computation | async-start | bytes 3407872 | tf_op jit(solution)/shard_map/all_to_all | solution.py:77
  13.5 104.0 %all-gather.2.cloned.1.call-start = ((), (), s32[]{:S(2)}) async-start(), calls=%async_computation.5 | async-start | bytes 7028736 | tf_op jit(solution)/shard_map/all_gather | solution.py:74
  35.9 3.8 %collective-permute-start = (bf16[4,128,1664]{2,1,0:T(8,128)(2,1)}, bf16[4,128,1664]{2,1,0:T(8,128)(2,1)S(1)}, u32[]{:S(2)}, u32[]{:S(2)}) collective-permute-start(bf16[4,128,1664]{2,1,0:T(8,128)(2,1)} %all-to-all-done), channel_id=1, source_target_pairs={{0,1},{1,0},{2,3},{3,2},{4,5},{5,4},{6,7},{7,6},{8,9},{9,8},{10,11... | collective-permute-start | bytes 5111816 | tf_op jit(solution)/shard_map/ppermute | solution.py:80
  41.6 1.7 copy-start.4
  47.3 2.6 %copy-start.2 = (f32[1024,3,2,104]{0,3,2,1:T(8,128)}, f32[1024,3,2,104]{0,3,2,1:T(8,128)S(1)}, u32[]{:S(2)}) copy-start(f32[1024,3,2,104]{0,3,2,1:T(8,128)S(1)} %fusion.50) | copy-start | bytes 7667716
  64.4 3.7 %collective-permute-start.1 = (bf16[512,1664]{1,0:T(8,128)(2,1)S(1)}, bf16[512,1664]{1,0:T(8,128)(2,1)S(1)}, u32[]{:S(2)}, u32[]{:S(2)}) collective-permute-start(bf16[512,1664]{1,0:T(8,128)(2,1)S(1)} %broadcast_select_fusion), channel_id=1, source_target_pairs={{0,1},{1,0},{2,3},{3,2},{4,5},{5,4},{6,7},{7,6},{8,9},{9,8},{10,11... | collective-permute-start | bytes 5111816 | tf_op jit(solution)/shard_map/ppermute | solution.py:43
  69.9 4.8 %copy-start.6 = (f32[1664]{0:T(1024)S(1)}, f32[1664]{0:T(1024)}, u32[]{:S(2)}) copy-start(f32[1664]{0:T(1024)} %param.15) | copy-start | bytes 19972
  69.9 29.1 %copy-start.1 = (bf16[128,1664]{1,0:T(8,128)(2,1)S(1)}, bf16[128,1664]{1,0:T(8,128)(2,1)}, u32[]{:S(2)}) copy-start(bf16[128,1664]{1,0:T(8,128)(2,1)} %param.11) | copy-start | bytes 1277956
  69.9 27.3 %all-to-all-start.1 = ((bf16[4,128,1664]{2,1,0:T(8,128)(2,1)}), bf16[4,128,1664]{2,1,0:T(8,128)(2,1)}, u32[]{:S(2)}, u32[]{:S(2)}) async-start(bf16[4,128,1664]{2,1,0:T(8,128)(2,1)} %bitcast.70), calls=%async_computation.1 | async-start | bytes 3407872 | tf_op jit(solution)/shard_map/all_to_all | solution.py:135
  104.0 1.6 collective-permute-start.2
  123.0 7.8 %copy-start.8 = (s32[32,1]{0,1:T(1,128)S(1)}, s32[32,1]{0,1:T(1,128)}, u32[]{:S(2)}) copy-start(s32[32,1]{0,1:T(1,128)} %param.21) | copy-start | bytes 388
  123.0 2.7 %collective-permute-start.3 = (bf16[128,4096]{1,0:T(8,128)(2,1)S(1)}, bf16[128,4096]{1,0:T(8,128)(2,1)S(1)}, u32[]{:S(2)}, u32[]{:S(2)}) collective-permute-start(bf16[128,4096]{1,0:T(8,128)(2,1)S(1)} %broadcast_select_fusion.1), channel_id=1, source_target_pairs={{0,1},{1,0},{2,3},{3,2},{4,5},{5,4},{6,7},{7,6},{8,9},{9,8},{10,11... | collective-permute-start | bytes 3145736 | tf_op jit(solution)/shard_map/ppermute | solution.py:43
  127.3 19.2 %all-to-all-start.3 = ((bf16[4,32,4096]{2,1,0:T(8,128)(2,1)}), bf16[4,32,4096]{2,1,0:T(8,128)(2,1)S(1)}, u32[]{:S(2)}, u32[]{:S(2)}) async-start(bf16[4,32,4096]{2,1,0:T(8,128)(2,1)} %bitcast.26), calls=%async_computation.3 | async-start | bytes 2097152 | tf_op jit(solution)/shard_map/all_to_all | solution.py:163
Sparse Core Ops, SparseCore 0:
  16.8 97.9 all-gather.1
